TPU v7x, 256 devices: a whole 4x4x8 slice. The times are simulated.
256 devices in a mesh: dom: 64 (over y, z, core), rep: 4 (over x).
Axes of the slice: x: 4, y: 4, z: 8, core: 2. Of those that a mesh axis runs over, the one named last changes fastest.
Arguments:
- x_loader: bfloat16 [131072, 512], P(('dom', 'rep')), may hold values from -6 to 6
- owner_index: int32 [131072], P(('dom', 'rep')), may hold values from 0 to 131071, as said below
- tile_vals: bfloat16 [1024, 12, 128, 128], P(('dom', 'rep')), as said below
- tile_cols: int32 [1024, 12], P(('dom', 'rep')), may hold values from 0 to 1023, as said below
- tile_live: int32 [1024, 12], P(('dom', 'rep')), may hold values from 0 to 1, as said below
- w_self: bfloat16 [512, 512], replicated, may hold values from -0.25 to 0.25
- w_neigh: bfloat16 [512, 512], replicated, may hold values from -3 to 3
- bias: float32 [512], replicated, may hold values from -3 to 3
- cotangent: bfloat16 [131072, 512], P(('dom', 'rep')), may hold values from -6 to 6
Outputs:
- layer_out: bfloat16 [131072, 512], P(('dom', 'rep'))
- grad_features: bfloat16 [131072, 512], P(('dom', 'rep'))
- grad_self: float32 [512, 512], replicated
- grad_neigh: float32 [512, 512], replicated
- grad_bias: float32 [512], replicated
Inputs may be any that keep to these rules, and one draw needn't show every extreme that they name: `owner_index`: A permutation of the 131072 rows. Loader rows are in blocks of 512 in the order of the devices (dom slowest); owner rows likewise. The 512 rows of each loader block with rep index r go to owner blocks of rep index r, 8 rows to each of the 64 partitions. `tile_cols`: partition p holds row tiles p * 16 to (p + 1) * 16 - 1. A column tile of a row tile of partition p lies in partition p or within 4 tiles beyond its edges. W is symmetric: every live slot (t, c) with tiles B is matched by a live slot (c, t) with tiles B^T, a slot with c = t holding a symmetric tile. `tile_live`: live slots are symmetric as stated for tile_cols. `tile_vals`: nonnegative edge weights.
All inputs are finite; a program needn't handle non-finite values.
Results may differ from a plain program's by a relative error of at most 0.0075.
Values may be sent and summed in bfloat16 or wider, within the bound.
No kernel may reach another device: no remote copies, remote signals or barrier semaphores. Data moves between devices by JAX's collectives and lax.ppermute only.
A program may use at most 64 MiB of HBM per device.

v0:
```python
import jax
import jax.numpy as jnp
from jax import lax
from jax.sharding import PartitionSpec as P

HALO_T = 4


def shifted(value, axis, steps):
    count = lax.axis_size(axis)
    first, last = (max(0, -steps), min(count, count - steps))
    return lax.ppermute(value, axis, [(source, source + steps) for source in range(first, last)])


def with_halo(block, sides, width):
    for axis, dim in sides:
        count = lax.axis_size(axis)
        forward = [(i, i + 1) for i in range(count - 1)]
        backward = [(target, source) for source, target in forward]
        low = lax.ppermute(
            lax.slice_in_dim(block, block.shape[dim] - width, None, axis=dim), axis, forward
        )
        high = lax.ppermute(lax.slice_in_dim(block, 0, width, axis=dim), axis, backward)
        block = jnp.concatenate([low, block, high], axis=dim)
    return block


def contract_rows(left, right):
    return lax.dot_general(
        left, right, (((0,), (0,)), ((), ())), preferred_element_type=jnp.float32
    )


def contract_cols(left, right):
    return lax.dot_general(
        left, right, (((1,), (1,)), ((), ())), preferred_element_type=jnp.float32
    )


HALVING_BITS = (2, 3, 6, 0)
DOUBLING_BITS = (4, 7, 1, 5)


def halving_sum(block, axes):
    count = 1
    for axis in axes:
        count *= lax.axis_size(axis)
    place = lax.axis_index(axes)
    bits = [bit for bit in HALVING_BITS if (1 << bit) < count]
    for bit in bits:
        pairs = [(i, i ^ (1 << bit)) for i in range(count)]
        upper = ((place >> bit) & 1) == 1
        half = block.shape[0] // 2
        kept = jnp.where(upper, block[half:], block[:half])
        sent = jnp.where(upper, block[:half], block[half:])
        block = kept + lax.ppermute(sent, axes, pairs)
    for bit in DOUBLING_BITS:
        if (1 << bit) < count:
            block = block + lax.ppermute(block, axes, [(i, i ^ (1 << bit)) for i in range(count)])
    for bit in reversed(bits):
        pairs = [(i, i ^ (1 << bit)) for i in range(count)]
        upper = ((place >> bit) & 1) == 1
        got = lax.ppermute(block, axes, pairs)
        block = jnp.where(upper, jnp.concatenate([got, block]), jnp.concatenate([block, got]))
    return block


def gather_rep(block):
    count = lax.axis_size("rep")
    place = lax.axis_index("rep")
    parts = [block] + [
        lax.ppermute(block, "rep", [(i, (i + shift) % count) for i in range(count)])
        for shift in range(1, count)
    ]
    source = (place - jnp.arange(count)) % count
    return jnp.stack(parts)[source].reshape(count * block.shape[0], *block.shape[1:])


def pass_rim(values, offset):
    return shifted(values.astype(jnp.bfloat16), "dom", offset).astype(values.dtype)


def shards(
    x_loader, owner_index, tile_vals, tile_cols, tile_live, w_self, w_neigh, bias, cotangent
):
    rows, width = x_loader.shape
    reps = lax.axis_size("rep")
    dom_place = lax.axis_index("dom")
    part_rows = rows * reps
    part_tiles = part_rows // 128
    row_tiles = rows // 128
    rim_rows = HALO_T * 128
    dest = owner_index // part_rows
    order = jnp.argsort(dest, stable=True)
    doms = lax.axis_size("dom")
    per = rows // doms
    slots = (owner_index % rows)[order].reshape(doms, per)
    code = jnp.concatenate([slots // 32, slots % 32], axis=1).astype(jnp.bfloat16)
    code = jnp.pad(code, ((0, 0), (0, 128 - 2 * per)))
    sent = jnp.concatenate([x_loader[order].reshape(doms, per * width), code], axis=1)
    got = lax.all_to_all(sent, "dom", split_axis=0, concat_axis=0, tiled=True)
    moved = got[:, : per * width].reshape(rows, width)
    codes = got[:, per * width : per * width + 2 * per].astype(jnp.int32)
    slot = (codes[:, :per] * 32 + codes[:, per:]).reshape(rows)
    features = jnp.zeros((rows, width), jnp.bfloat16).at[slot].set(moved)
    first_tile = dom_place * part_tiles - HALO_T
    local_cols = tile_cols - first_tile
    masked = tile_vals * tile_live.astype(jnp.bfloat16)[:, :, None, None]
    degree = 1.0 + jnp.sum(masked, axis=(1, 3), dtype=jnp.float32)
    whole = gather_rep(features)
    extended = with_halo(whole, (("dom", 0),), rim_rows)
    span_tiles = part_tiles + 2 * HALO_T
    onehot = (local_cols[:, :, None] == jnp.arange(span_tiles, dtype=jnp.int32)).astype(jnp.bfloat16)
    merged = jnp.einsum("tke,tkab->teab", onehot, masked, preferred_element_type=jnp.float32)
    merged_hi = merged.astype(jnp.bfloat16)
    merged_lo = (merged - merged_hi.astype(jnp.float32)).astype(jnp.bfloat16)
    span = extended.reshape(span_tiles, 128, width)
    summed = jnp.einsum(
        "teab,ebf->taf", merged_hi, span, preferred_element_type=jnp.float32
    ) + jnp.einsum("teab,ebf->taf", merged_lo, span, preferred_element_type=jnp.float32)
    agg = (summed / degree[:, :, None]).reshape(rows, width).astype(jnp.bfloat16)
    pre = (
        jnp.dot(features, w_self, preferred_element_type=jnp.float32)
        + jnp.dot(agg, w_neigh, preferred_element_type=jnp.float32)
        + bias
    )
    layer_out = jnp.where(pre > 0, pre, jnp.expm1(jnp.minimum(pre, 0.0))).astype(jnp.bfloat16)
    slope = jnp.where(pre > 0, 1.0, jnp.exp(jnp.minimum(pre, 0.0)))
    dz = (cotangent.astype(jnp.float32) * slope).astype(jnp.bfloat16)
    lanes = 2 * width * width // 256
    packed = halving_sum(
        jnp.concatenate(
            [
                jnp.concatenate([contract_rows(features, dz), contract_rows(agg, dz)]).reshape(256, lanes),
                jnp.sum(dz, axis=0, dtype=jnp.float32).reshape(256, -1),
            ],
            axis=1,
        ),
        ("dom", "rep"),
    )
    grads = packed[:, :lanes].reshape(2 * width, width)
    grad_self, grad_neigh = grads[:width], grads[width:]
    grad_bias = packed[:, lanes:].reshape(width)
    scaled = (contract_cols(dz, w_neigh) / degree.reshape(rows, 1)).astype(jnp.bfloat16)
    scaled_tiles = scaled.reshape(row_tiles, 128, width)
    buffer = jnp.einsum(
        "teab,taf->ebf", merged_hi, scaled_tiles, preferred_element_type=jnp.float32
    ) + jnp.einsum("teab,taf->ebf", merged_lo, scaled_tiles, preferred_element_type=jnp.float32)
    buffer = buffer.reshape(span_tiles * 128, width)
    lower = buffer[:rim_rows]
    upper = buffer[rim_rows + part_rows :]
    core = buffer[rim_rows : rim_rows + part_rows]
    core = core.at[:rim_rows].add(pass_rim(upper, 1))
    core = core.at[part_rows - rim_rows :].add(pass_rim(lower, -1))
    back = lax.psum_scatter(core, "rep", scatter_dimension=0, tiled=True)
    grad_features = (contract_cols(dz, w_self) + back).astype(jnp.bfloat16)
    return (layer_out, grad_features, grad_self, grad_neigh, grad_bias)


def solution(mesh):
    return jax.shard_map(
        shards,
        mesh=mesh,
        in_specs=(
            P(("dom", "rep"), None),
            P(("dom", "rep")),
            P(("dom", "rep"), None, None, None),
            P(("dom", "rep"), None),
            P(("dom", "rep"), None),
            P(),
            P(),
            P(),
            P(("dom", "rep"), None),
        ),
        out_specs=(P(("dom", "rep"), None), P(("dom", "rep"), None), P(), P(), P()),
        check_vma=False,
    )
```

profile of v0, /device:TPU:1, one launch (start us, length us, event | category | flops | bytes accessed | tf_op | source)
XLA Modules:
  0.0 256.0 jit_solution(17108561342023886246)
XLA Ops:
  8.0 3.8 %sort.17 = (s32[512]{0:T(512)}, s32[512]{0:T(512)S(1)}) sort(s32[512]{0:T(512)S(1)} %get-tuple-element.48, s32[512]{0:T(512)S(1)} %iota.12), dimensions={0}, to_apply=%region_0.1 | sort | flops 4608 | bytes 8192 | tf_op jit(solution)/shard_map/jit(argsort)/sort | solution.py:94
  11.8 3.5 %gather_fusion.1 = s32[512]{0:T(512)S(1)} fusion(s32[512]{0:T(512)S(1)} %get-tuple-element.49, s32[1024]{0:T(1024)S(1)} %pad_clamp_fusion.1), kind=kCustom, calls=%fused_computation.1 | custom fusion | bytes 6144 | tf_op jit(solution)/shard_map/gather | solution.py:97
  20.6 13.2 %all-to-all-start = ((bf16[64,2,2112]{2,1,0:T(2,128)(2,1)}), bf16[64,2,2112]{2,1,0:T(2,128)(2,1)S(1)}, u32[]{:S(2)}, u32[]{:S(2)}) async-start(bf16[64,2,2112]{2,1,0:T(2,128)(2,1)} %reshape.252), calls=%async_computation | async-start | bytes 1114112 | tf_op jit(solution)/shard_map/all_to_all | solution.py:101
  33.9 17.9 %all-to-all-done = bf16[64,2,2112]{2,1,0:T(2,128)(2,1)S(1)} async-done(((bf16[64,2,2112]{2,1,0:T(2,128)(2,1)}), bf16[64,2,2112]{2,1,0:T(2,128)(2,1)S(1)}, u32[]{:S(2)}, u32[]{:S(2)}) %all-to-all-start) | async-done | bytes 540704 | tf_op jit(solution)/shard_map/all_to_all | solution.py:101
  53.8 3.0 %scatter_custom_fusion = bf16[512,512]{1,0:T(8,128)(2,1)S(1)} fusion(s32[512]{0:T(512)S(1)} %bitcast.86, bf16[512,512]{1,0:T(8,128)(2,1)} %reshape.237, bf16[]{:T(256)} %constant.135.clone.1), kind=kCustom, calls=%fused_computation.56 | custom fusion | bytes 524800 | tf_op jit(solution)/shard_map/scatter | solution.py:105
  56.8 2.6 collective-permute-start.2
  62.2 19.2 %collective-permute-done.2 = bf16[512,512]{1,0:T(8,128)(2,1)S(1)} collective-permute-done((bf16[512,512]{1,0:T(8,128)(2,1)S(1)}, bf16[512,512]{1,0:T(8,128)(2,1)S(1)}, u32[]{:S(2)}, u32[]{:S(2)}) %collective-permute-start.2) | collective-permute-done | bytes 524320 | tf_op jit(solution)/shard_map/ppermute | solution.py:72
  81.4 4.6 %collective-permute-done = bf16[512,512]{1,0:T(8,128)(2,1)S(1)} collective-permute-done((bf16[512,512]{1,0:T(8,128)(2,1)S(1)}, bf16[512,512]{1,0:T(8,128)(2,1)S(1)}, u32[]{:S(2)}, u32[]{:S(2)}) %collective-permute-start) | collective-permute-done | bytes 524320 | tf_op jit(solution)/shard_map/ppermute | solution.py:72
  90.9 2.8 %collective-permute-start.3 = (bf16[512,512]{1,0:T(8,128)(2,1)}, bf16[512,512]{1,0:T(8,128)(2,1)}, u32[]{:S(2)}, u32[]{:S(2)}) collective-permute-start(bf16[512,512]{1,0:T(8,128)(2,1)} %get-tuple-element.41), channel_id=1, source_target_pairs={{0,4},{4,8},{8,12},{12,16},{16,20},{20,24},{24,28},{28,32},{32,36}... | collective-permute-start | bytes 1572872 | tf_op jit(solution)/shard_map/ppermute | solution.py:20
  93.7 2.4 collective-permute-start.4
  96.2 4.4 %subtract_convert_fusion = (bf16[4,24,128,128]{3,1,2,0:T(8,128)(2,1)}, bf16[4,24,128,128]{3,1,2,0:T(8,128)(2,1)}) fusion(bf16[4,12,128,128]{3,2,1,0:T(8,128)(2,1)S(1)} %copy-done.9, s32[4,12]{1,0:T(4,128)S(1)} %broadcast_subtract_fusion), kind=kOutput, calls=%fused_computation.5 | convolution fusion | flops 44041344 | bytes 7864512 | tf_op jit(solution)/shard_map/tke,tkab->teab/dot_general | solution.py:114
  102.1 2.5 collective-permute-done.4
  121.9 2.7 %copy.89 = f32[128,2050]{0,1:T(8,128)} copy(f32[128,2050]{1,0:T(8,128)} %slice_select_fusion) | data formatting | bytes 2099200 | tf_op jit(solution)/shard_map/jit(_where)/select_n | solution.py:55
  124.5 3.9 %fusion = f32[24,128,512,1]{2,1,3,0:T(8,128)S(1)} fusion(bf16[4,128,512,1]{2,1,0,3:T(8,128)(2,1)S(1)} %bitcast.79, bf16[4,24,128,128]{3,1,2,0:T(8,128)(2,1)} %get-tuple-element.35), kind=kOutput, calls=%fused_computation.7 | convolution fusion | flops 1610612736 | bytes 9961472 | tf_op jit(solution)/shard_map/teab,taf->ebf/dot_general | solution.py:148
  131.5 2.4 slice.169
  134.9 2.9 %collective-permute-start.5 = (bf16[512,512]{1,0:T(8,128)(2,1)}, bf16[512,512]{1,0:T(8,128)(2,1)S(1)}, u32[]{:S(2)}, u32[]{:S(2)}) collective-permute-start(bf16[512,512]{1,0:T(8,128)(2,1)} %bitcast.30), channel_id=1, source_target_pairs={{0,4},{4,8},{8,12},{12,16},{16,20},{20,24},{24,28},{28,32},{32,36}... | collective-permute-start | bytes 1572872 | tf_op jit(solution)/shard_map/ppermute | solution.py:12
  139.8 2.6 %copy.90 = f32[128,2050]{1,0:T(8,128)} copy(f32[128,2050]{0,1:T(8,128)} %collective-permute-done.7) | data formatting | bytes 2099200 | tf_op jit(solution)/shard_map/ppermute | solution.py:56
  148.9 2.4 fusion.33
  151.3 9.3 %collective-permute-done.8 = f32[64,2050]{1,0:T(8,128)S(1)} collective-permute-done((f32[64,2050]{1,0:T(8,128)S(1)}, f32[64,2050]{1,0:T(8,128)S(1)}, u32[]{:S(2)}, u32[]{:S(2)}) %collective-permute-start.8) | collective-permute-done | bytes 524832 | tf_op jit(solution)/shard_map/ppermute | solution.py:56
  160.7 7.4 %collective-permute-done.9 = f32[32,2050]{1,0:T(8,128)S(1)} collective-permute-done((f32[32,2050]{1,0:T(8,128)S(1)}, f32[32,2050]{1,0:T(8,128)S(1)}, u32[]{:S(2)}, u32[]{:S(2)}) %collective-permute-start.9) | collective-permute-done | bytes 262432 | tf_op jit(solution)/shard_map/ppermute | solution.py:56
  168.3 8.0 %collective-permute-done.10 = f32[16,2050]{1,0:T(8,128)S(1)} collective-permute-done((f32[16,2050]{1,0:T(8,128)S(1)}, f32[16,2050]{1,0:T(8,128)S(1)}, u32[]{:S(2)}, u32[]{:S(2)}) %collective-permute-start.10) | collective-permute-done | bytes 131232 | tf_op jit(solution)/shard_map/ppermute | solution.py:56
  178.6 4.6 %collective-permute-done.11 = f32[16,2050]{1,0:T(8,128)S(1)} collective-permute-done((f32[16,2050]{1,0:T(8,128)S(1)}, f32[16,2050]{1,0:T(8,128)S(1)}, u32[]{:S(2)}, u32[]{:S(2)}) %collective-permute-start.11) | collective-permute-done | bytes 131232 | tf_op jit(solution)/shard_map/ppermute | solution.py:59
  183.3 5.4 %collective-permute-done.12 = f32[16,2050]{1,0:T(8,128)S(1)} collective-permute-done((f32[16,2050]{1,0:T(8,128)S(1)}, f32[16,2050]{1,0:T(8,128)S(1)}, u32[]{:S(2)}, u32[]{:S(2)}) %collective-permute-start.12) | collective-permute-done | bytes 131232 | tf_op jit(solution)/shard_map/ppermute | solution.py:59
  188.8 8.5 %collective-permute-done.13 = f32[16,2050]{1,0:T(8,128)S(1)} collective-permute-done((f32[16,2050]{1,0:T(8,128)S(1)}, f32[16,2050]{1,0:T(8,128)S(1)}, u32[]{:S(2)}, u32[]{:S(2)}) %collective-permute-start.13) | collective-permute-done | bytes 131232 | tf_op jit(solution)/shard_map/ppermute | solution.py:59
  197.4 3.3 %collective-permute-start.14 = (f32[16,2050]{1,0:T(8,128)S(1)}, f32[16,2050]{1,0:T(8,128)S(1)}, u32[]{:S(2)}, u32[]{:S(2)}) collective-permute-start(f32[16,2050]{1,0:T(8,128)S(1)} %add.162), channel_id=1, source_target_pairs={{0,32},{1,33},{2,34},{3,35},{4,36},{5,37},{6,38},{7,39},{8,40},{9,... | collective-permute-start | bytes 393608 | tf_op jit(solution)/shard_map/ppermute | solution.py:59
  200.7 4.6 %collective-permute-done.14 = f32[16,2050]{1,0:T(8,128)S(1)} collective-permute-done((f32[16,2050]{1,0:T(8,128)S(1)}, f32[16,2050]{1,0:T(8,128)S(1)}, u32[]{:S(2)}, u32[]{:S(2)}) %collective-permute-start.14) | collective-permute-done | bytes 131232 | tf_op jit(solution)/shard_map/ppermute | solution.py:59
  205.5 4.2 %collective-permute-done.15 = f32[16,2050]{1,0:T(8,128)S(1)} collective-permute-done((f32[16,2050]{1,0:T(8,128)S(1)}, f32[16,2050]{1,0:T(8,128)S(1)}, u32[]{:S(2)}, u32[]{:S(2)}) %collective-permute-start.15) | collective-permute-done | bytes 131232 | tf_op jit(solution)/shard_map/ppermute | solution.py:63
  209.9 5.5 %collective-permute-done.16 = f32[32,2050]{1,0:T(8,128)S(1)} collective-permute-done((f32[32,2050]{1,0:T(8,128)S(1)}, f32[32,2050]{1,0:T(8,128)S(1)}, u32[]{:S(2)}, u32[]{:S(2)}) %collective-permute-start.16) | collective-permute-done | bytes 262432 | tf_op jit(solution)/shard_map/ppermute | solution.py:63
  216.9 7.1 %collective-permute-done.17 = f32[64,2050]{1,0:T(8,128)S(1)} collective-permute-done((f32[64,2050]{1,0:T(8,128)S(1)}, f32[64,2050]{1,0:T(8,128)S(1)}, u32[]{:S(2)}, u32[]{:S(2)}) %collective-permute-start.17) | collective-permute-done | bytes 524832 | tf_op jit(solution)/shard_map/ppermute | solution.py:63
  224.4 9.7 %collective-permute-start.18 = (f32[128,2050]{0,1:T(8,128)S(1)}, f32[128,2050]{0,1:T(8,128)}, u32[]{:S(2)}, u32[]{:S(2)}) collective-permute-start(f32[128,2050]{0,1:T(8,128)S(1)} %copy.91), channel_id=1, source_target_pairs={{0,4},{1,5},{2,6},{3,7},{4,0},{5,1},{6,2},{7,3},{8,12},{9,13},{10,... | collective-permute-start | bytes 3148808 | tf_op jit(solution)/shard_map/ppermute | solution.py:63
  240.4 2.7 %fusion.50 = (f32[128,2048]{1,0:T(8,128)}, f32[128,2048]{1,0:T(8,128)S(1)}) fusion(f32[256,2050]{1,0:T(8,128)} %copy-done.8), kind=kLoop, calls=%fused_computation.102 | loop fusion | bytes 4194304 | tf_op jit(solution)/shard_map/slice | solution.py:142
  243.1 2.6 %slice.155 = f32[512,512]{1,0:T(8,128)} reshape(f32[128,2048]{1,0:T(8,128)} %get-tuple-element.39) | data formatting | bytes 2097152 | tf_op jit(solution)/shard_map/slice | solution.py:142
  (141 shorter events, 61.8 us)
Async XLA Ops:
  7.2 103.3 %copy-start = (bf16[512,512]{1,0:T(8,128)(2,1)S(1)}, bf16[512,512]{1,0:T(8,128)(2,1)}, u32[]{:S(2)}) copy-start(bf16[512,512]{1,0:T(8,128)(2,1)} %param.19) | copy-start | bytes 1572868
  7.2 8.5 %copy-start.2 = (bf16[512,512]{1,0:T(8,128)(2,1)S(1)}, bf16[512,512]{1,0:T(8,128)(2,1)}, u32[]{:S(2)}) copy-start(bf16[512,512]{1,0:T(8,128)(2,1)} %param.13) | copy-start | bytes 1572868
  17.9 16.0 %copy-start.18 = (s32[4,12]{1,0:T(4,128)S(1)}, s32[4,12]{1,0:T(4,128)}, u32[]{:S(2)}) copy-start(s32[4,12]{1,0:T(4,128)} %param.17) | copy-start | bytes 580
  20.6 31.2 %all-to-all-start = ((bf16[64,2,2112]{2,1,0:T(2,128)(2,1)}), bf16[64,2,2112]{2,1,0:T(2,128)(2,1)S(1)}, u32[]{:S(2)}, u32[]{:S(2)}) async-start(bf16[64,2,2112]{2,1,0:T(2,128)(2,1)} %reshape.252), calls=%async_computation | async-start | bytes 1114112 | tf_op jit(solution)/shard_map/all_to_all | solution.py:101
  33.8 213.2 %reduce-scatter.2.cloned.1.call-start = ((), (), s32[]{:S(2)}) async-start(), calls=%async_computation.2 | async-start | bytes 5242880 | tf_op jit(solution)/shard_map/reduce_scatter | solution.py:155
  52.4 8.1 %copy-start.19 = (s32[4,12]{1,0:T(4,128)S(1)}, s32[4,12]{1,0:T(4,128)}, u32[]{:S(2)}) copy-start(s32[4,12]{1,0:T(4,128)} %param.16) | copy-start | bytes 580
  52.5 8.0 %copy-start.17 = (bf16[4,12,128,128]{3,2,1,0:T(8,128)(2,1)S(1)}, bf16[4,12,128,128]{3,2,1,0:T(8,128)(2,1)}, u32[]{:S(2)}) copy-start(bf16[4,12,128,128]{3,2,1,0:T(8,128)(2,1)} %param.15) | copy-start | bytes 4718596
  56.8 24.5 %collective-permute-start.2 = (bf16[512,512]{1,0:T(8,128)(2,1)S(1)}, bf16[512,512]{1,0:T(8,128)(2,1)S(1)}, u32[]{:S(2)}, u32[]{:S(2)}) collective-permute-start(bf16[512,512]{1,0:T(8,128)(2,1)S(1)} %scatter_custom_fusion), channel_id=1, source_target_pairs={{0,3},{1,0},{2,1},{3,2},{4,7},{5,4},{6,5},{7,6},{8,11},{9,8},{10,9... | collective-permute-start | bytes 1572872 | tf_op jit(solution)/shard_map/ppermute | solution.py:72
  59.4 22.0 %collective-permute-start.1 = (bf16[512,512]{1,0:T(8,128)(2,1)S(1)}, bf16[512,512]{1,0:T(8,128)(2,1)S(1)}, u32[]{:S(2)}, u32[]{:S(2)}) collective-permute-start(bf16[512,512]{1,0:T(8,128)(2,1)S(1)} %scatter_custom_fusion), channel_id=1, source_target_pairs={{0,2},{1,3},{2,0},{3,1},{4,6},{5,7},{6,4},{7,5},{8,10},{9,11},{10,... | collective-permute-start | bytes 1572872 | tf_op jit(solution)/shard_map/ppermute | solution.py:72
  59.9 26.1 %collective-permute-start = (bf16[512,512]{1,0:T(8,128)(2,1)S(1)}, bf16[512,512]{1,0:T(8,128)(2,1)S(1)}, u32[]{:S(2)}, u32[]{:S(2)}) collective-permute-start(bf16[512,512]{1,0:T(8,128)(2,1)S(1)} %scatter_custom_fusion), channel_id=1, source_target_pairs={{0,1},{1,2},{2,3},{3,0},{4,5},{5,6},{6,7},{7,4},{8,9},{9,10},{10,1... | collective-permute-start | bytes 1572872 | tf_op jit(solution)/shard_map/ppermute | solution.py:72
  89.9 6.3 %copy-start.9 = (bf16[4,12,128,128]{3,2,1,0:T(8,128)(2,1)S(1)}, bf16[4,12,128,128]{3,2,1,0:T(8,128)(2,1)}, u32[]{:S(2)}) copy-start(bf16[4,12,128,128]{3,2,1,0:T(8,128)(2,1)} %get-tuple-element.34) | copy-start | bytes 4718596
  90.9 11.2 %collective-permute-start.3 = (bf16[512,512]{1,0:T(8,128)(2,1)}, bf16[512,512]{1,0:T(8,128)(2,1)}, u32[]{:S(2)}, u32[]{:S(2)}) collective-permute-start(bf16[512,512]{1,0:T(8,128)(2,1)} %get-tuple-element.41), channel_id=1, source_target_pairs={{0,4},{4,8},{8,12},{12,16},{16,20},{20,24},{24,28},{28,32},{32,36}... | collective-permute-start | bytes 1572872 | tf_op jit(solution)/shard_map/ppermute | solution.py:20
  93.7 10.8 %collective-permute-start.4 = (bf16[512,512]{1,0:T(8,128)(2,1)}, bf16[512,512]{1,0:T(8,128)(2,1)}, u32[]{:S(2)}, u32[]{:S(2)}) collective-permute-start(bf16[512,512]{1,0:T(8,128)(2,1)} %get-tuple-element.42), channel_id=1, source_target_pairs={{4,0},{8,4},{12,8},{16,12},{20,16},{24,20},{28,24},{32,28},{36,32}... | collective-permute-start | bytes 1572872 | tf_op jit(solution)/shard_map/ppermute | solution.py:23
  124.5 15.3 %collective-permute-start.7 = (f32[128,2050]{0,1:T(8,128)}, f32[128,2050]{0,1:T(8,128)}, u32[]{:S(2)}, u32[]{:S(2)}) collective-permute-start(f32[128,2050]{0,1:T(8,128)} %copy.89), channel_id=1, source_target_pairs={{0,4},{1,5},{2,6},{3,7},{4,0},{5,1},{6,2},{7,3},{8,12},{9,13},{10,... | collective-permute-start | bytes 3148808 | tf_op jit(solution)/shard_map/ppermute | solution.py:56
  124.5 3.9 %copy-start.5 = (bf16[4,24,128,128]{3,1,2,0:T(8,128)(2,1)S(1)}, bf16[4,24,128,128]{3,1,2,0:T(8,128)(2,1)}, u32[]{:S(2)}) copy-start(bf16[4,24,128,128]{3,1,2,0:T(8,128)(2,1)} %get-tuple-element.36) | copy-start | bytes 9437188
  134.9 12.3 %collective-permute-start.5 = (bf16[512,512]{1,0:T(8,128)(2,1)}, bf16[512,512]{1,0:T(8,128)(2,1)S(1)}, u32[]{:S(2)}, u32[]{:S(2)}) collective-permute-start(bf16[512,512]{1,0:T(8,128)(2,1)} %bitcast.30), channel_id=1, source_target_pairs={{0,4},{4,8},{8,12},{12,16},{16,20},{20,24},{24,28},{28,32},{32,36}... | collective-permute-start | bytes 1572872 | tf_op jit(solution)/shard_map/ppermute | solution.py:12
  137.9 11.0 %collective-permute-start.6 = (bf16[512,512]{1,0:T(8,128)(2,1)}, bf16[512,512]{1,0:T(8,128)(2,1)S(1)}, u32[]{:S(2)}, u32[]{:S(2)}) collective-permute-start(bf16[512,512]{1,0:T(8,128)(2,1)} %bitcast.31), channel_id=1, source_target_pairs={{4,0},{8,4},{12,8},{16,12},{20,16},{24,20},{28,24},{32,28},{36,32}... | collective-permute-start | bytes 1572872 | tf_op jit(solution)/shard_map/ppermute | solution.py:12
  142.4 4.8 %copy-start.12 = (f32[4,128,512]{2,1,0:T(8,128)S(1)}, f32[4,128,512]{2,1,0:T(8,128)}, u32[]{:S(2)}) copy-start(f32[4,128,512]{2,1,0:T(8,128)} %slice.170) | copy-start | bytes 3145732
  145.0 15.5 %collective-permute-start.8 = (f32[64,2050]{1,0:T(8,128)S(1)}, f32[64,2050]{1,0:T(8,128)S(1)}, u32[]{:S(2)}, u32[]{:S(2)}) collective-permute-start(f32[64,2050]{1,0:T(8,128)S(1)} %slice_select_fusion.1), channel_id=1, source_target_pairs={{0,8},{1,9},{2,10},{3,11},{4,12},{5,13},{6,14},{7,15},{8,0},{9,1},... | collective-permute-start | bytes 1574408 | tf_op jit(solution)/shard_map/ppermute | solution.py:56
  151.2 9.3 %copy-start.7 = (f32[128,2050]{1,0:T(8,128)S(1)}, f32[128,2050]{1,0:T(8,128)}, u32[]{:S(2)}) copy-start(f32[128,2050]{1,0:T(8,128)} %copy-done.6) | copy-start | bytes 3148804
  160.6 7.5 %collective-permute-start.9 = (f32[32,2050]{1,0:T(8,128)S(1)}, f32[32,2050]{1,0:T(8,128)S(1)}, u32[]{:S(2)}, u32[]{:S(2)}) collective-permute-start(f32[32,2050]{1,0:T(8,128)S(1)} %slice_select_fusion.2), channel_id=1, source_target_pairs={{0,64},{1,65},{2,66},{3,67},{4,68},{5,69},{6,70},{7,71},{8,72},{9,... | collective-permute-start | bytes 787208 | tf_op jit(solution)/shard_map/ppermute | solution.py:56
  168.2 8.1 %collective-permute-start.10 = (f32[16,2050]{1,0:T(8,128)S(1)}, f32[16,2050]{1,0:T(8,128)S(1)}, u32[]{:S(2)}, u32[]{:S(2)}) collective-permute-start(f32[16,2050]{1,0:T(8,128)S(1)} %slice_select_fusion.3), channel_id=1, source_target_pairs={{0,1},{1,0},{2,3},{3,2},{4,5},{5,4},{6,7},{7,6},{8,9},{9,8},{10,11... | collective-permute-start | bytes 393608 | tf_op jit(solution)/shard_map/ppermute | solution.py:56
  176.4 6.8 %collective-permute-start.11 = (f32[16,2050]{1,0:T(8,128)S(1)}, f32[16,2050]{1,0:T(8,128)S(1)}, u32[]{:S(2)}, u32[]{:S(2)}) collective-permute-start(f32[16,2050]{1,0:T(8,128)S(1)} %select_add_fusion.3), channel_id=1, source_target_pairs={{0,16},{1,17},{2,18},{3,19},{4,20},{5,21},{6,22},{7,23},{8,24},{9,... | collective-permute-start | bytes 393608 | tf_op jit(solution)/shard_map/ppermute | solution.py:59
  183.2 5.5 %collective-permute-start.12 = (f32[16,2050]{1,0:T(8,128)S(1)}, f32[16,2050]{1,0:T(8,128)S(1)}, u32[]{:S(2)}, u32[]{:S(2)}) collective-permute-start(f32[16,2050]{1,0:T(8,128)S(1)} %add.160), channel_id=1, source_target_pairs={{0,128},{1,129},{2,130},{3,131},{4,132},{5,133},{6,134},{7,135},{8... | collective-permute-start | bytes 393608 | tf_op jit(solution)/shard_map/ppermute | solution.py:59
  188.7 8.6 %collective-permute-start.13 = (f32[16,2050]{1,0:T(8,128)S(1)}, f32[16,2050]{1,0:T(8,128)S(1)}, u32[]{:S(2)}, u32[]{:S(2)}) collective-permute-start(f32[16,2050]{1,0:T(8,128)S(1)} %add.161), channel_id=1, source_target_pairs={{0,2},{1,3},{2,0},{3,1},{4,6},{5,7},{6,4},{7,5},{8,10},{9,11},{10,... | collective-permute-start | bytes 393608 | tf_op jit(solution)/shard_map/ppermute | solution.py:59
  197.4 8.0 %collective-permute-start.14 = (f32[16,2050]{1,0:T(8,128)S(1)}, f32[16,2050]{1,0:T(8,128)S(1)}, u32[]{:S(2)}, u32[]{:S(2)}) collective-permute-start(f32[16,2050]{1,0:T(8,128)S(1)} %add.162), channel_id=1, source_target_pairs={{0,32},{1,33},{2,34},{3,35},{4,36},{5,37},{6,38},{7,39},{8,40},{9,... | collective-permute-start | bytes 393608 | tf_op jit(solution)/shard_map/ppermute | solution.py:59
  205.4 4.3 %collective-permute-start.15 = (f32[16,2050]{1,0:T(8,128)S(1)}, f32[16,2050]{1,0:T(8,128)S(1)}, u32[]{:S(2)}, u32[]{:S(2)}) collective-permute-start(f32[16,2050]{1,0:T(8,128)S(1)} %add.163), channel_id=1, source_target_pairs={{0,1},{1,0},{2,3},{3,2},{4,5},{5,4},{6,7},{7,6},{8,9},{9,8},{10,11... | collective-permute-start | bytes 393608 | tf_op jit(solution)/shard_map/ppermute | solution.py:63
  209.7 5.8 %collective-permute-start.16 = (f32[32,2050]{1,0:T(8,128)S(1)}, f32[32,2050]{1,0:T(8,128)S(1)}, u32[]{:S(2)}, u32[]{:S(2)}) collective-permute-start(f32[32,2050]{1,0:T(8,128)S(1)} %maximum_select_fusion.3), channel_id=1, source_target_pairs={{0,64},{1,65},{2,66},{3,67},{4,68},{5,69},{6,70},{7,71},{8,72},{9,... | collective-permute-start | bytes 787208 | tf_op jit(solution)/shard_map/ppermute | solution.py:63
  215.5 18.6 %copy-start.11 = (bf16[512,512]{1,0:T(8,128)(2,1)S(1)}, bf16[512,512]{1,0:T(8,128)(2,1)}, u32[]{:S(2)}) copy-start(bf16[512,512]{1,0:T(8,128)(2,1)} %copy-done.10) | copy-start | bytes 1572868
  215.5 18.6 %copy-start.16 = (bf16[512,512]{1,0:T(8,128)(2,1)S(1)}, bf16[512,512]{1,0:T(8,128)(2,1)}, u32[]{:S(2)}) copy-start(bf16[512,512]{1,0:T(8,128)(2,1)} %param.18) | copy-start | bytes 1572868
  215.5 8.5 %collective-permute-start.17 = (f32[64,2050]{1,0:T(8,128)S(1)}, f32[64,2050]{1,0:T(8,128)S(1)}, u32[]{:S(2)}, u32[]{:S(2)}) collective-permute-start(f32[64,2050]{1,0:T(8,128)S(1)} %maximum_select_fusion.2), channel_id=1, source_target_pairs={{0,8},{1,9},{2,10},{3,11},{4,12},{5,13},{6,14},{7,15},{8,0},{9,1},... | collective-permute-start | bytes 1574408 | tf_op jit(solution)/shard_map/ppermute | solution.py:63
  224.4 12.1 %collective-permute-start.18 = (f32[128,2050]{0,1:T(8,128)S(1)}, f32[128,2050]{0,1:T(8,128)}, u32[]{:S(2)}, u32[]{:S(2)}) collective-permute-start(f32[128,2050]{0,1:T(8,128)S(1)} %copy.91), channel_id=1, source_target_pairs={{0,4},{1,5},{2,6},{3,7},{4,0},{5,1},{6,2},{7,3},{8,12},{9,13},{10,... | collective-permute-start | bytes 3148808 | tf_op jit(solution)/shard_map/ppermute | solution.py:63
  (11 other events, 23.2 us)
Sparse Core Ops, SparseCore 0:
  151.4 53.7 reduce-scatter.1
where the time goes:
time: 257 us; the launch traced here: 256 us
  waiting for transfers between devices  110 us (43%)
  starting transfers between devices  46.6 us (18%)
  local copies, waits for them, and re-layouts  43.2 us (17%)
  matrix products  21.9 us (9%)
  other arithmetic  19.6 us (8%)
  between operations  14.6 us (6%)
    ppermute x4, waiting for transfers between devices, halving_sum(): block = kept + lax.ppermute(sent, axes, pairs)  24.7 us
    ppermute x3, waiting for transfers between devices, gather_rep(): lax.ppermute(block, 'rep', [(i, (i + shift) % count) for i in range(count)])  23.8 us
    ppermute x4, waiting for transfers between devices, halving_sum(): lax.ppermute(block, axes, [(i, i ^ 1 << bit) for i in range(count)])  23.1 us
    all_to_all x1, waiting for transfers between devices, shards(): got = lax.all_to_all(sent, 'dom', split_axis=0, concat_axis=0, tiled=True)  17.9 us
    ppermute x4, waiting for transfers between devices, halving_sum(): got = lax.ppermute(block, axes, pairs)  17.6 us
    all_to_all x1, starting transfers between devices, shards(): got = lax.all_to_all(sent, 'dom', split_axis=0, concat_axis=0, tiled=True)  13.2 us
    ppermute x4, starting transfers between devices, halving_sum(): got = lax.ppermute(block, axes, pairs)  11.5 us
    unnamed x48, local copies, waits for them, and re-layouts  7.98 us
  transfers between devices with their start and end apart: 21, of which 16 were waited for; matrix products, arithmetic and copies ran while one was open for 14% of the time, Pallas kernels for 0%

commit v1 on v0

--- a/solution.py
+++ b/solution.py
@@ -91,18 +91,27 @@
     row_tiles = rows // 128
     rim_rows = HALO_T * 128
     dest = owner_index // part_rows
-    order = jnp.argsort(dest, stable=True)
     doms = lax.axis_size("dom")
     per = rows // doms
-    slots = (owner_index % rows)[order].reshape(doms, per)
-    code = jnp.concatenate([slots // 32, slots % 32], axis=1).astype(jnp.bfloat16)
-    code = jnp.pad(code, ((0, 0), (0, 128 - 2 * per)))
-    sent = jnp.concatenate([x_loader[order].reshape(doms, per * width), code], axis=1)
+    line = jnp.arange(rows, dtype=jnp.int32)
+    dest_hot = (dest[:, None] == jnp.arange(doms, dtype=jnp.int32)).astype(jnp.bfloat16)
+    earlier = (line[:, None] > line[None, :]).astype(jnp.bfloat16)
+    before = jnp.dot(earlier, dest_hot, preferred_element_type=jnp.float32)
+    rank = jnp.sum(before * dest_hot.astype(jnp.float32), axis=1).astype(jnp.int32)
+    to_sorted = ((dest * per + rank)[None, :] == line[:, None]).astype(jnp.bfloat16)
+    slot_src = owner_index % rows
+    code_src = jnp.stack([slot_src // 32, slot_src % 32], axis=1).astype(jnp.bfloat16)
+    code = jnp.dot(to_sorted, code_src, preferred_element_type=jnp.float32)
+    code = jnp.concatenate([code[:, 0].reshape(doms, per), code[:, 1].reshape(doms, per)], axis=1)
+    code = jnp.pad(code.astype(jnp.bfloat16), ((0, 0), (0, 128 - 2 * per)))
+    x_sorted = jnp.dot(to_sorted, x_loader, preferred_element_type=jnp.float32).astype(jnp.bfloat16)
+    sent = jnp.concatenate([x_sorted.reshape(doms, per * width), code], axis=1)
     got = lax.all_to_all(sent, "dom", split_axis=0, concat_axis=0, tiled=True)
     moved = got[:, : per * width].reshape(rows, width)
     codes = got[:, per * width : per * width + 2 * per].astype(jnp.int32)
     slot = (codes[:, :per] * 32 + codes[:, per:]).reshape(rows)
-    features = jnp.zeros((rows, width), jnp.bfloat16).at[slot].set(moved)
+    to_owner = (slot[None, :] == line[:, None]).astype(jnp.bfloat16)
+    features = jnp.dot(to_owner, moved, preferred_element_type=jnp.float32).astype(jnp.bfloat16)
     first_tile = dom_place * part_tiles - HALO_T
     local_cols = tile_cols - first_tile
     masked = tile_vals * tile_live.astype(jnp.bfloat16)[:, :, None, None]

time: 257 us -> 248 us (0.965)
  local copies, waits for them, and re-layouts: 43.2 us -> 34 us
  waiting for transfers between devices: 110 us -> 102 us
  starting transfers between devices: 46.6 us -> 53.7 us
  matrix products: 21.9 us -> 26.3 us
  other arithmetic: 19.6 us -> 16.8 us
    gather x2 -> x0, local copies, waits for them, and re-layouts: 5.46 us -> none  [the longest x1 3.49 us: shards(): slots = (owner_index % rows)[order].reshape(doms, per)]
    ppermute x4, starting transfers between devices: 11.5 us -> 16.3 us  [halving_sum(): got = lax.ppermute(block, axes, pairs)]
    ppermute x4, waiting for transfers between devices: 23.1 us -> 19.3 us  [halving_sum(): lax.ppermute(block, axes, [(i, i ^ 1 << bit) for i in range(count)])]
    sort x1 -> x0, other arithmetic: 3.77 us -> none  [shards(): order = jnp.argsort(dest, stable=True)]
    dot_general x0 -> x4, matrix products: none -> 3.56 us  [the longest x1 1.49 us: shards(): jnp.dot(to_sorted, x_loader, preferred_element_type=jnp.float32)]
    ppermute x4, waiting for transfers between devices: 17.6 us -> 14.4 us  [halving_sum(): got = lax.ppermute(block, axes, pairs)]
    scatter x1 -> x0, local copies, waits for them, and re-layouts: 3.01 us -> none  [shards(): features = jnp.zeros((rows, width), jnp.bfloat16).at[slot].set(moved)]
  transfers between devices with their start and end apart: 21 -> 21, of which waited for: 16 -> 15; matrix products, arithmetic and copies ran while one was open for 14% -> 15% of each run, Pallas kernels for 0% -> 0%
where the time goes in v1:
time: 248 us; the launch traced here: 247 us
  waiting for transfers between devices  102 us (41%)
  starting transfers between devices  53.7 us (22%)
  local copies, waits for them, and re-layouts  34 us (14%)
  matrix products  26.3 us (11%)
  other arithmetic  16.8 us (7%)
  between operations  14.5 us (6%)
    ppermute x3, waiting for transfers between devices, gather_rep(): lax.ppermute(block, 'rep', [(i, (i + shift) % count) for i in range(count)])  23.8 us
    ppermute x4, waiting for transfers between devices, halving_sum(): block = kept + lax.ppermute(sent, axes, pairs)  23.8 us
    ppermute x4, waiting for transfers between devices, halving_sum(): lax.ppermute(block, axes, [(i, i ^ 1 << bit) for i in range(count)])  19.3 us
    all_to_all x1, waiting for transfers between devices, shards(): got = lax.all_to_all(sent, 'dom', split_axis=0, concat_axis=0, tiled=True)  17.9 us
    ppermute x4, starting transfers between devices, halving_sum(): got = lax.ppermute(block, axes, pairs)  16.3 us
    ppermute x4, waiting for transfers between devices, halving_sum(): got = lax.ppermute(block, axes, pairs)  14.4 us
    all_to_all x1, starting transfers between devices, shards(): got = lax.all_to_all(sent, 'dom', split_axis=0, concat_axis=0, tiled=True)  13.2 us
    ppermute x4, starting transfers between devices, halving_sum(): lax.ppermute(block, axes, [(i, i ^ 1 << bit) for i in range(count)])  8.25 us
  transfers between devices with their start and end apart: 21, of which 15 were waited for; matrix products, arithmetic and copies ran while one was open for 15% of the time, Pallas kernels for 0%

profile of v1, /device:TPU:1, one launch (start us, length us, event | category | flops | bytes accessed | tf_op | source)
XLA Modules:
  0.0 247.1 jit_solution(1148989086928737817)
XLA Ops:
  13.3 13.2 %all-to-all-start = ((bf16[64,2,2112]{2,1,0:T(2,128)(2,1)}), bf16[64,2,2112]{2,1,0:T(2,128)(2,1)S(1)}, u32[]{:S(2)}, u32[]{:S(2)}) async-start(bf16[64,2,2112]{2,1,0:T(2,128)(2,1)} %reshape.193), calls=%async_computation | async-start | bytes 1114112 | tf_op jit(solution)/shard_map/all_to_all | solution.py:109
  26.6 17.9 %all-to-all-done = bf16[64,2,2112]{2,1,0:T(2,128)(2,1)S(1)} async-done(((bf16[64,2,2112]{2,1,0:T(2,128)(2,1)}), bf16[64,2,2112]{2,1,0:T(2,128)(2,1)S(1)}, u32[]{:S(2)}, u32[]{:S(2)}) %all-to-all-start) | async-done | bytes 540704 | tf_op jit(solution)/shard_map/all_to_all | solution.py:109
  48.0 2.5 %collective-permute-start.2 = (bf16[512,512]{1,0:T(8,128)(2,1)S(1)}, bf16[512,512]{1,0:T(8,128)(2,1)S(1)}, u32[]{:S(2)}, u32[]{:S(2)}) collective-permute-start(bf16[512,512]{1,0:T(8,128)(2,1)S(1)} %convolution_convert_fusion), channel_id=1, source_target_pairs={{0,3},{1,0},{2,1},{3,2},{4,7},{5,4},{6,5},{7,6},{8,11},{9,8},{10,9... | collective-permute-start | bytes 1572872 | tf_op jit(solution)/shard_map/ppermute | solution.py:72
  53.4 19.2 %collective-permute-done.2 = bf16[512,512]{1,0:T(8,128)(2,1)S(1)} collective-permute-done((bf16[512,512]{1,0:T(8,128)(2,1)S(1)}, bf16[512,512]{1,0:T(8,128)(2,1)S(1)}, u32[]{:S(2)}, u32[]{:S(2)}) %collective-permute-start.2) | collective-permute-done | bytes 524320 | tf_op jit(solution)/shard_map/ppermute | solution.py:72
  72.6 4.6 %collective-permute-done = bf16[512,512]{1,0:T(8,128)(2,1)S(1)} collective-permute-done((bf16[512,512]{1,0:T(8,128)(2,1)S(1)}, bf16[512,512]{1,0:T(8,128)(2,1)S(1)}, u32[]{:S(2)}, u32[]{:S(2)}) %collective-permute-start) | collective-permute-done | bytes 524320 | tf_op jit(solution)/shard_map/ppermute | solution.py:72
  82.1 2.8 %collective-permute-start.3 = (bf16[512,512]{1,0:T(8,128)(2,1)}, bf16[512,512]{1,0:T(8,128)(2,1)}, u32[]{:S(2)}, u32[]{:S(2)}) collective-permute-start(bf16[512,512]{1,0:T(8,128)(2,1)} %get-tuple-element.41), channel_id=1, source_target_pairs={{0,4},{4,8},{8,12},{12,16},{16,20},{20,24},{24,28},{28,32},{32,36}... | collective-permute-start | bytes 1572872 | tf_op jit(solution)/shard_map/ppermute | solution.py:20
  84.9 2.4 collective-permute-start.4
  87.4 4.4 %subtract_convert_fusion = (bf16[4,24,128,128]{3,1,2,0:T(8,128)(2,1)}, bf16[4,24,128,128]{3,1,2,0:T(8,128)(2,1)}) fusion(bf16[4,12,128,128]{3,2,1,0:T(8,128)(2,1)S(1)} %copy-done.8, s32[4,12]{1,0:T(4,128)S(1)} %broadcast_subtract_fusion), kind=kOutput, calls=%fused_computation.2 | convolution fusion | flops 44041344 | bytes 7864512 | tf_op jit(solution)/shard_map/tke,tkab->teab/dot_general | solution.py:123
  93.3 2.5 %collective-permute-done.4 = bf16[512,512]{1,0:T(8,128)(2,1)} collective-permute-done((bf16[512,512]{1,0:T(8,128)(2,1)}, bf16[512,512]{1,0:T(8,128)(2,1)}, u32[]{:S(2)}, u32[]{:S(2)}) %collective-permute-start.4) | collective-permute-done | bytes 524320 | tf_op jit(solution)/shard_map/ppermute | solution.py:23
  113.3 2.7 %copy.114 = f32[128,2050]{0,1:T(8,128)} copy(f32[128,2050]{1,0:T(8,128)} %slice_select_fusion) | data formatting | bytes 2099200 | tf_op jit(solution)/shard_map/jit(_where)/select_n | solution.py:55
  116.0 3.9 %fusion = f32[24,128,512,1]{2,1,3,0:T(8,128)S(1)} fusion(bf16[4,128,512,1]{2,1,0,3:T(8,128)(2,1)S(1)} %bitcast.79, bf16[4,24,128,128]{3,1,2,0:T(8,128)(2,1)} %get-tuple-element.35), kind=kOutput, calls=%fused_computation.4 | convolution fusion | flops 1610612736 | bytes 9961472 | tf_op jit(solution)/shard_map/teab,taf->ebf/dot_general | solution.py:157
  122.9 2.4 slice.177
  126.4 2.7 %collective-permute-start.5 = (bf16[512,512]{1,0:T(8,128)(2,1)}, bf16[512,512]{1,0:T(8,128)(2,1)}, u32[]{:S(2)}, u32[]{:S(2)}) collective-permute-start(bf16[512,512]{1,0:T(8,128)(2,1)} %bitcast.29), channel_id=1, source_target_pairs={{0,4},{4,8},{8,12},{12,16},{16,20},{20,24},{24,28},{28,32},{32,36}... | collective-permute-start | bytes 1572872 | tf_op jit(solution)/shard_map/ppermute | solution.py:12
  129.0 2.4 collective-permute-start.6
  131.5 2.6 %copy.115 = f32[128,2050]{1,0:T(8,128)} copy(f32[128,2050]{0,1:T(8,128)} %collective-permute-done.7) | data formatting | bytes 2099200 | tf_op jit(solution)/shard_map/ppermute | solution.py:56
  140.6 2.4 fusion.33
  143.0 8.7 %collective-permute-done.8 = f32[64,2050]{1,0:T(8,128)S(1)} collective-permute-done((f32[64,2050]{1,0:T(8,128)S(1)}, f32[64,2050]{1,0:T(8,128)S(1)}, u32[]{:S(2)}, u32[]{:S(2)}) %collective-permute-start.8) | collective-permute-done | bytes 524832 | tf_op jit(solution)/shard_map/ppermute | solution.py:56
  151.9 7.1 %collective-permute-done.9 = f32[32,2050]{1,0:T(8,128)S(1)} collective-permute-done((f32[32,2050]{1,0:T(8,128)S(1)}, f32[32,2050]{1,0:T(8,128)S(1)}, u32[]{:S(2)}, u32[]{:S(2)}) %collective-permute-start.9) | collective-permute-done | bytes 262432 | tf_op jit(solution)/shard_map/ppermute | solution.py:56
  159.2 7.9 %collective-permute-done.10 = f32[16,2050]{1,0:T(8,128)S(1)} collective-permute-done((f32[16,2050]{1,0:T(8,128)S(1)}, f32[16,2050]{1,0:T(8,128)S(1)}, u32[]{:S(2)}, u32[]{:S(2)}) %collective-permute-start.10) | collective-permute-done | bytes 131232 | tf_op jit(solution)/shard_map/ppermute | solution.py:56
  167.2 2.6 %collective-permute-start.11 = (f32[16,2050]{1,0:T(8,128)S(1)}, f32[16,2050]{1,0:T(8,128)S(1)}, u32[]{:S(2)}, u32[]{:S(2)}) collective-permute-start(f32[16,2050]{1,0:T(8,128)S(1)} %select_add_fusion.3), channel_id=1, source_target_pairs={{0,16},{1,17},{2,18},{3,19},{4,20},{5,21},{6,22},{7,23},{8,24},{9,... | collective-permute-start | bytes 393608 | tf_op jit(solution)/shard_map/ppermute | solution.py:59
  169.8 2.8 %collective-permute-done.11 = f32[16,2050]{1,0:T(8,128)S(1)} collective-permute-done((f32[16,2050]{1,0:T(8,128)S(1)}, f32[16,2050]{1,0:T(8,128)S(1)}, u32[]{:S(2)}, u32[]{:S(2)}) %collective-permute-start.11) | collective-permute-done | bytes 131232 | tf_op jit(solution)/shard_map/ppermute | solution.py:59
  173.1 5.0 %collective-permute-done.12 = f32[16,2050]{1,0:T(8,128)S(1)} collective-permute-done((f32[16,2050]{1,0:T(8,128)S(1)}, f32[16,2050]{1,0:T(8,128)S(1)}, u32[]{:S(2)}, u32[]{:S(2)}) %collective-permute-start.12) | collective-permute-done | bytes 131232 | tf_op jit(solution)/shard_map/ppermute | solution.py:59
  178.4 8.4 %collective-permute-done.13 = f32[16,2050]{1,0:T(8,128)S(1)} collective-permute-done((f32[16,2050]{1,0:T(8,128)S(1)}, f32[16,2050]{1,0:T(8,128)S(1)}, u32[]{:S(2)}, u32[]{:S(2)}) %collective-permute-start.13) | collective-permute-done | bytes 131232 | tf_op jit(solution)/shard_map/ppermute | solution.py:59
  186.8 5.0 %collective-permute-start.14 = (f32[16,2050]{1,0:T(8,128)S(1)}, f32[16,2050]{1,0:T(8,128)S(1)}, u32[]{:S(2)}, u32[]{:S(2)}) collective-permute-start(f32[16,2050]{1,0:T(8,128)S(1)} %add.148), channel_id=1, source_target_pairs={{0,32},{1,33},{2,34},{3,35},{4,36},{5,37},{6,38},{7,39},{8,40},{9,... | collective-permute-start | bytes 393608 | tf_op jit(solution)/shard_map/ppermute | solution.py:59
  191.8 3.0 %collective-permute-done.14 = f32[16,2050]{1,0:T(8,128)S(1)} collective-permute-done((f32[16,2050]{1,0:T(8,128)S(1)}, f32[16,2050]{1,0:T(8,128)S(1)}, u32[]{:S(2)}, u32[]{:S(2)}) %collective-permute-start.14) | collective-permute-done | bytes 131232 | tf_op jit(solution)/shard_map/ppermute | solution.py:59
  196.2 2.6 %collective-permute-done.15 = f32[16,2050]{1,0:T(8,128)S(1)} collective-permute-done((f32[16,2050]{1,0:T(8,128)S(1)}, f32[16,2050]{1,0:T(8,128)S(1)}, u32[]{:S(2)}, u32[]{:S(2)}) %collective-permute-start.15) | collective-permute-done | bytes 131232 | tf_op jit(solution)/shard_map/ppermute | solution.py:63
  201.1 3.9 %collective-permute-done.16 = f32[32,2050]{1,0:T(8,128)S(1)} collective-permute-done((f32[32,2050]{1,0:T(8,128)S(1)}, f32[32,2050]{1,0:T(8,128)S(1)}, u32[]{:S(2)}, u32[]{:S(2)}) %collective-permute-start.16) | collective-permute-done | bytes 262432 | tf_op jit(solution)/shard_map/ppermute | solution.py:63
  205.1 3.0 %collective-permute-start.17 = (f32[64,2050]{1,0:T(8,128)S(1)}, f32[64,2050]{1,0:T(8,128)S(1)}, u32[]{:S(2)}, u32[]{:S(2)}) collective-permute-start(f32[64,2050]{1,0:T(8,128)S(1)} %maximum_select_fusion.2), channel_id=1, source_target_pairs={{0,8},{1,9},{2,10},{3,11},{4,12},{5,13},{6,14},{7,15},{8,0},{9,1},... | collective-permute-start | bytes 1574408 | tf_op jit(solution)/shard_map/ppermute | solution.py:63
  208.1 6.9 %collective-permute-done.17 = f32[64,2050]{1,0:T(8,128)S(1)} collective-permute-done((f32[64,2050]{1,0:T(8,128)S(1)}, f32[64,2050]{1,0:T(8,128)S(1)}, u32[]{:S(2)}, u32[]{:S(2)}) %collective-permute-start.17) | collective-permute-done | bytes 524832 | tf_op jit(solution)/shard_map/ppermute | solution.py:63
  215.5 9.7 %collective-permute-start.18 = (f32[128,2050]{0,1:T(8,128)S(1)}, f32[128,2050]{0,1:T(8,128)}, u32[]{:S(2)}, u32[]{:S(2)}) collective-permute-start(f32[128,2050]{0,1:T(8,128)S(1)} %copy.116), channel_id=1, source_target_pairs={{0,4},{1,5},{2,6},{3,7},{4,0},{5,1},{6,2},{7,3},{8,12},{9,13},{10,... | collective-permute-start | bytes 3148808 | tf_op jit(solution)/shard_map/ppermute | solution.py:63
  231.5 2.7 %fusion.59 = (f32[128,2048]{1,0:T(8,128)}, f32[128,2048]{1,0:T(8,128)S(1)}) fusion(f32[256,2050]{1,0:T(8,128)} %copy-done.7), kind=kLoop, calls=%fused_computation.117 | loop fusion | bytes 4194304 | tf_op jit(solution)/shard_map/slice | solution.py:151
  234.2 2.6 %slice.165 = f32[512,512]{1,0:T(8,128)} reshape(f32[128,2048]{1,0:T(8,128)} %get-tuple-element.39) | data formatting | bytes 2097152 | tf_op jit(solution)/shard_map/slice | solution.py:151
  (136 shorter events, 61.8 us)
Async XLA Ops:
  7.2 94.5 %copy-start = (bf16[512,512]{1,0:T(8,128)(2,1)S(1)}, bf16[512,512]{1,0:T(8,128)(2,1)}, u32[]{:S(2)}) copy-start(bf16[512,512]{1,0:T(8,128)(2,1)} %param.19) | copy-start | bytes 1572868
  10.5 16.0 %copy-start.18 = (s32[4,12]{1,0:T(4,128)S(1)}, s32[4,12]{1,0:T(4,128)}, u32[]{:S(2)}) copy-start(s32[4,12]{1,0:T(4,128)} %param.17) | copy-start | bytes 580
  13.3 31.2 %all-to-all-start = ((bf16[64,2,2112]{2,1,0:T(2,128)(2,1)}), bf16[64,2,2112]{2,1,0:T(2,128)(2,1)S(1)}, u32[]{:S(2)}, u32[]{:S(2)}) async-start(bf16[64,2,2112]{2,1,0:T(2,128)(2,1)} %reshape.193), calls=%async_computation | async-start | bytes 1114112 | tf_op jit(solution)/shard_map/all_to_all | solution.py:109
  26.5 211.6 %reduce-scatter.2.cloned.1.call-start = ((), (), s32[]{:S(2)}) async-start(), calls=%async_computation.2 | async-start | bytes 5242880 | tf_op jit(solution)/shard_map/reduce_scatter | solution.py:164
  45.2 6.5 %copy-start.19 = (s32[4,12]{1,0:T(4,128)S(1)}, s32[4,12]{1,0:T(4,128)}, u32[]{:S(2)}) copy-start(s32[4,12]{1,0:T(4,128)} %param.16) | copy-start | bytes 580
  45.2 6.5 %copy-start.17 = (bf16[4,12,128,128]{3,2,1,0:T(8,128)(2,1)S(1)}, bf16[4,12,128,128]{3,2,1,0:T(8,128)(2,1)}, u32[]{:S(2)}) copy-start(bf16[4,12,128,128]{3,2,1,0:T(8,128)(2,1)} %param.15) | copy-start | bytes 4718596
  48.0 43.8 %copy-start.9 = (bf16[512,512]{1,0:T(8,128)(2,1)}, bf16[512,512]{1,0:T(8,128)(2,1)S(1)}, u32[]{:S(2)}) copy-start(bf16[512,512]{1,0:T(8,128)(2,1)S(1)} %convolution_convert_fusion) | copy-start | bytes 1572868
  48.0 24.5 %collective-permute-start.2 = (bf16[512,512]{1,0:T(8,128)(2,1)S(1)}, bf16[512,512]{1,0:T(8,128)(2,1)S(1)}, u32[]{:S(2)}, u32[]{:S(2)}) collective-permute-start(bf16[512,512]{1,0:T(8,128)(2,1)S(1)} %convolution_convert_fusion), channel_id=1, source_target_pairs={{0,3},{1,0},{2,1},{3,2},{4,7},{5,4},{6,5},{7,6},{8,11},{9,8},{10,9... | collective-permute-start | bytes 1572872 | tf_op jit(solution)/shard_map/ppermute | solution.py:72
  50.6 22.0 %collective-permute-start.1 = (bf16[512,512]{1,0:T(8,128)(2,1)S(1)}, bf16[512,512]{1,0:T(8,128)(2,1)S(1)}, u32[]{:S(2)}, u32[]{:S(2)}) collective-permute-start(bf16[512,512]{1,0:T(8,128)(2,1)S(1)} %convolution_convert_fusion), channel_id=1, source_target_pairs={{0,2},{1,3},{2,0},{3,1},{4,6},{5,7},{6,4},{7,5},{8,10},{9,11},{10,... | collective-permute-start | bytes 1572872 | tf_op jit(solution)/shard_map/ppermute | solution.py:72
  51.1 26.1 %collective-permute-start = (bf16[512,512]{1,0:T(8,128)(2,1)S(1)}, bf16[512,512]{1,0:T(8,128)(2,1)S(1)}, u32[]{:S(2)}, u32[]{:S(2)}) collective-permute-start(bf16[512,512]{1,0:T(8,128)(2,1)S(1)} %convolution_convert_fusion), channel_id=1, source_target_pairs={{0,1},{1,2},{2,3},{3,0},{4,5},{5,6},{6,7},{7,4},{8,9},{9,10},{10,1... | collective-permute-start | bytes 1572872 | tf_op jit(solution)/shard_map/ppermute | solution.py:72
  81.0 6.3 %copy-start.8 = (bf16[4,12,128,128]{3,2,1,0:T(8,128)(2,1)S(1)}, bf16[4,12,128,128]{3,2,1,0:T(8,128)(2,1)}, u32[]{:S(2)}) copy-start(bf16[4,12,128,128]{3,2,1,0:T(8,128)(2,1)} %get-tuple-element.34) | copy-start | bytes 4718596
  82.1 11.2 %collective-permute-start.3 = (bf16[512,512]{1,0:T(8,128)(2,1)}, bf16[512,512]{1,0:T(8,128)(2,1)}, u32[]{:S(2)}, u32[]{:S(2)}) collective-permute-start(bf16[512,512]{1,0:T(8,128)(2,1)} %get-tuple-element.41), channel_id=1, source_target_pairs={{0,4},{4,8},{8,12},{12,16},{16,20},{20,24},{24,28},{28,32},{32,36}... | collective-permute-start | bytes 1572872 | tf_op jit(solution)/shard_map/ppermute | solution.py:20
  84.9 10.8 %collective-permute-start.4 = (bf16[512,512]{1,0:T(8,128)(2,1)}, bf16[512,512]{1,0:T(8,128)(2,1)}, u32[]{:S(2)}, u32[]{:S(2)}) collective-permute-start(bf16[512,512]{1,0:T(8,128)(2,1)} %get-tuple-element.42), channel_id=1, source_target_pairs={{4,0},{8,4},{12,8},{16,12},{20,16},{24,20},{28,24},{32,28},{36,32}... | collective-permute-start | bytes 1572872 | tf_op jit(solution)/shard_map/ppermute | solution.py:23
  115.9 15.5 %collective-permute-start.7 = (f32[128,2050]{0,1:T(8,128)}, f32[128,2050]{0,1:T(8,128)}, u32[]{:S(2)}, u32[]{:S(2)}) collective-permute-start(f32[128,2050]{0,1:T(8,128)} %copy.114), channel_id=1, source_target_pairs={{0,4},{1,5},{2,6},{3,7},{4,0},{5,1},{6,2},{7,3},{8,12},{9,13},{10,... | collective-permute-start | bytes 3148808 | tf_op jit(solution)/shard_map/ppermute | solution.py:56
  116.0 3.9 %copy-start.4 = (bf16[4,24,128,128]{3,1,2,0:T(8,128)(2,1)S(1)}, bf16[4,24,128,128]{3,1,2,0:T(8,128)(2,1)}, u32[]{:S(2)}) copy-start(bf16[4,24,128,128]{3,1,2,0:T(8,128)(2,1)} %get-tuple-element.36) | copy-start | bytes 9437188
  126.4 12.1 %collective-permute-start.5 = (bf16[512,512]{1,0:T(8,128)(2,1)}, bf16[512,512]{1,0:T(8,128)(2,1)}, u32[]{:S(2)}, u32[]{:S(2)}) collective-permute-start(bf16[512,512]{1,0:T(8,128)(2,1)} %bitcast.29), channel_id=1, source_target_pairs={{0,4},{4,8},{8,12},{12,16},{16,20},{20,24},{24,28},{28,32},{32,36}... | collective-permute-start | bytes 1572872 | tf_op jit(solution)/shard_map/ppermute | solution.py:12
  129.0 11.6 %collective-permute-start.6 = (bf16[512,512]{1,0:T(8,128)(2,1)}, bf16[512,512]{1,0:T(8,128)(2,1)S(1)}, u32[]{:S(2)}, u32[]{:S(2)}) collective-permute-start(bf16[512,512]{1,0:T(8,128)(2,1)} %bitcast.30), channel_id=1, source_target_pairs={{4,0},{8,4},{12,8},{16,12},{20,16},{24,20},{28,24},{32,28},{36,32}... | collective-permute-start | bytes 1572872 | tf_op jit(solution)/shard_map/ppermute | solution.py:12
  134.1 4.4 %copy-start.11 = (f32[4,128,512]{2,1,0:T(8,128)S(1)}, f32[4,128,512]{2,1,0:T(8,128)}, u32[]{:S(2)}) copy-start(f32[4,128,512]{2,1,0:T(8,128)} %slice.178) | copy-start | bytes 3145732
  136.7 15.0 %collective-permute-start.8 = (f32[64,2050]{1,0:T(8,128)S(1)}, f32[64,2050]{1,0:T(8,128)S(1)}, u32[]{:S(2)}, u32[]{:S(2)}) collective-permute-start(f32[64,2050]{1,0:T(8,128)S(1)} %slice_select_fusion.1), channel_id=1, source_target_pairs={{0,8},{1,9},{2,10},{3,11},{4,12},{5,13},{6,14},{7,15},{8,0},{9,1},... | collective-permute-start | bytes 1574408 | tf_op jit(solution)/shard_map/ppermute | solution.py:56
  143.0 8.7 %copy-start.6 = (f32[128,2050]{1,0:T(8,128)S(1)}, f32[128,2050]{1,0:T(8,128)}, u32[]{:S(2)}) copy-start(f32[128,2050]{1,0:T(8,128)} %copy-done.5) | copy-start | bytes 3148804
  151.8 7.2 %collective-permute-start.9 = (f32[32,2050]{1,0:T(8,128)S(1)}, f32[32,2050]{1,0:T(8,128)S(1)}, u32[]{:S(2)}, u32[]{:S(2)}) collective-permute-start(f32[32,2050]{1,0:T(8,128)S(1)} %slice_select_fusion.2), channel_id=1, source_target_pairs={{0,64},{1,65},{2,66},{3,67},{4,68},{5,69},{6,70},{7,71},{8,72},{9,... | collective-permute-start | bytes 787208 | tf_op jit(solution)/shard_map/ppermute | solution.py:56
  159.1 8.0 %collective-permute-start.10 = (f32[16,2050]{1,0:T(8,128)S(1)}, f32[16,2050]{1,0:T(8,128)S(1)}, u32[]{:S(2)}, u32[]{:S(2)}) collective-permute-start(f32[16,2050]{1,0:T(8,128)S(1)} %slice_select_fusion.3), channel_id=1, source_target_pairs={{0,1},{1,0},{2,3},{3,2},{4,5},{5,4},{6,7},{7,6},{8,9},{9,8},{10,11... | collective-permute-start | bytes 393608 | tf_op jit(solution)/shard_map/ppermute | solution.py:56
  167.2 5.4 %collective-permute-start.11 = (f32[16,2050]{1,0:T(8,128)S(1)}, f32[16,2050]{1,0:T(8,128)S(1)}, u32[]{:S(2)}, u32[]{:S(2)}) collective-permute-start(f32[16,2050]{1,0:T(8,128)S(1)} %select_add_fusion.3), channel_id=1, source_target_pairs={{0,16},{1,17},{2,18},{3,19},{4,20},{5,21},{6,22},{7,23},{8,24},{9,... | collective-permute-start | bytes 393608 | tf_op jit(solution)/shard_map/ppermute | solution.py:59
  172.6 5.5 %collective-permute-start.12 = (f32[16,2050]{1,0:T(8,128)S(1)}, f32[16,2050]{1,0:T(8,128)S(1)}, u32[]{:S(2)}, u32[]{:S(2)}) collective-permute-start(f32[16,2050]{1,0:T(8,128)S(1)} %add.146), channel_id=1, source_target_pairs={{0,128},{1,129},{2,130},{3,131},{4,132},{5,133},{6,134},{7,135},{8... | collective-permute-start | bytes 393608 | tf_op jit(solution)/shard_map/ppermute | solution.py:59
  178.2 8.6 %collective-permute-start.13 = (f32[16,2050]{1,0:T(8,128)S(1)}, f32[16,2050]{1,0:T(8,128)S(1)}, u32[]{:S(2)}, u32[]{:S(2)}) collective-permute-start(f32[16,2050]{1,0:T(8,128)S(1)} %add.147), channel_id=1, source_target_pairs={{0,2},{1,3},{2,0},{3,1},{4,6},{5,7},{6,4},{7,5},{8,10},{9,11},{10,... | collective-permute-start | bytes 393608 | tf_op jit(solution)/shard_map/ppermute | solution.py:59
  186.8 8.0 %collective-permute-start.14 = (f32[16,2050]{1,0:T(8,128)S(1)}, f32[16,2050]{1,0:T(8,128)S(1)}, u32[]{:S(2)}, u32[]{:S(2)}) collective-permute-start(f32[16,2050]{1,0:T(8,128)S(1)} %add.148), channel_id=1, source_target_pairs={{0,32},{1,33},{2,34},{3,35},{4,36},{5,37},{6,38},{7,39},{8,40},{9,... | collective-permute-start | bytes 393608 | tf_op jit(solution)/shard_map/ppermute | solution.py:59
  194.9 4.0 %collective-permute-start.15 = (f32[16,2050]{1,0:T(8,128)S(1)}, f32[16,2050]{1,0:T(8,128)S(1)}, u32[]{:S(2)}, u32[]{:S(2)}) collective-permute-start(f32[16,2050]{1,0:T(8,128)S(1)} %add.149), channel_id=1, source_target_pairs={{0,1},{1,0},{2,3},{3,2},{4,5},{5,4},{6,7},{7,6},{8,9},{9,8},{10,11... | collective-permute-start | bytes 393608 | tf_op jit(solution)/shard_map/ppermute | solution.py:63
  198.9 6.2 %collective-permute-start.16 = (f32[32,2050]{1,0:T(8,128)S(1)}, f32[32,2050]{1,0:T(8,128)S(1)}, u32[]{:S(2)}, u32[]{:S(2)}) collective-permute-start(f32[32,2050]{1,0:T(8,128)S(1)} %maximum_select_fusion.3), channel_id=1, source_target_pairs={{0,64},{1,65},{2,66},{3,67},{4,68},{5,69},{6,70},{7,71},{8,72},{9,... | collective-permute-start | bytes 787208 | tf_op jit(solution)/shard_map/ppermute | solution.py:63
  205.1 20.1 %copy-start.15 = (bf16[512,512]{1,0:T(8,128)(2,1)S(1)}, bf16[512,512]{1,0:T(8,128)(2,1)}, u32[]{:S(2)}) copy-start(bf16[512,512]{1,0:T(8,128)(2,1)} %param.18) | copy-start | bytes 1572868
  205.1 10.0 %collective-permute-start.17 = (f32[64,2050]{1,0:T(8,128)S(1)}, f32[64,2050]{1,0:T(8,128)S(1)}, u32[]{:S(2)}, u32[]{:S(2)}) collective-permute-start(f32[64,2050]{1,0:T(8,128)S(1)} %maximum_select_fusion.2), channel_id=1, source_target_pairs={{0,8},{1,9},{2,10},{3,11},{4,12},{5,13},{6,14},{7,15},{8,0},{9,1},... | collective-permute-start | bytes 1574408 | tf_op jit(solution)/shard_map/ppermute | solution.py:63
  215.5 12.2 %collective-permute-start.18 = (f32[128,2050]{0,1:T(8,128)S(1)}, f32[128,2050]{0,1:T(8,128)}, u32[]{:S(2)}, u32[]{:S(2)}) collective-permute-start(f32[128,2050]{0,1:T(8,128)S(1)} %copy.116), channel_id=1, source_target_pairs={{0,4},{1,5},{2,6},{3,7},{4,0},{5,1},{6,2},{7,3},{8,12},{9,13},{10,... | collective-permute-start | bytes 3148808 | tf_op jit(solution)/shard_map/ppermute | solution.py:63
  234.2 3.8 %copy-start.12 = (f32[512,512]{1,0:T(8,128)S(1)}, f32[512,512]{1,0:T(8,128)}, u32[]{:S(2)}) copy-start(f32[512,512]{1,0:T(8,128)} %fusion.62) | copy-start | bytes 3145732
  (11 other events, 21.9 us)
Sparse Core Ops, SparseCore 0:
  143.1 53.1 reduce-scatter.1

commit v2 on v1

--- a/solution.py
+++ b/solution.py
@@ -37,8 +37,22 @@
     )
 
 
-HALVING_BITS = (2, 3, 6, 0)
+HALVING_ORDERS = ((2, 3, 6, 0), (2, 6, 3, 0))
 DOUBLING_BITS = (4, 7, 1, 5)
+
+
+def by_bit(bits, pieces, axes, count):
+    got = [None] * len(pieces)
+    for bit in dict.fromkeys(bits):
+        group = [i for i, b in enumerate(bits) if b == bit]
+        sizes = [pieces[i].shape[1] for i in group]
+        joined = jnp.concatenate([pieces[i] for i in group], axis=1)
+        moved = lax.ppermute(joined, axes, [(i, i ^ (1 << bit)) for i in range(count)])
+        offset = 0
+        for i, size in zip(group, sizes):
+            got[i] = moved[:, offset : offset + size]
+            offset += size
+    return got
 
 
 def halving_sum(block, axes):
@@ -46,23 +60,28 @@
     for axis in axes:
         count *= lax.axis_size(axis)
     place = lax.axis_index(axes)
-    bits = [bit for bit in HALVING_BITS if (1 << bit) < count]
-    for bit in bits:
-        pairs = [(i, i ^ (1 << bit)) for i in range(count)]
-        upper = ((place >> bit) & 1) == 1
-        half = block.shape[0] // 2
-        kept = jnp.where(upper, block[half:], block[:half])
-        sent = jnp.where(upper, block[:half], block[half:])
-        block = kept + lax.ppermute(sent, axes, pairs)
+    split = block.shape[1] // 256 * 128
+    parts = [block[:, :split], block[:, split:]]
+    stages = list(zip(*HALVING_ORDERS))
+    for bits in stages:
+        uppers = [((place >> bit) & 1) == 1 for bit in bits]
+        half = parts[0].shape[0] // 2
+        kept = [jnp.where(u, p[half:], p[:half]) for p, u in zip(parts, uppers)]
+        sent = [jnp.where(u, p[:half], p[half:]) for p, u in zip(parts, uppers)]
+        got = by_bit(bits, sent, axes, count)
+        parts = [k + g for k, g in zip(kept, got)]
+    block = jnp.concatenate(parts, axis=1)
     for bit in DOUBLING_BITS:
-        if (1 << bit) < count:
-            block = block + lax.ppermute(block, axes, [(i, i ^ (1 << bit)) for i in range(count)])
-    for bit in reversed(bits):
-        pairs = [(i, i ^ (1 << bit)) for i in range(count)]
-        upper = ((place >> bit) & 1) == 1
-        got = lax.ppermute(block, axes, pairs)
-        block = jnp.where(upper, jnp.concatenate([got, block]), jnp.concatenate([block, got]))
-    return block
+        block = block + lax.ppermute(block, axes, [(i, i ^ (1 << bit)) for i in range(count)])
+    parts = [block[:, :split], block[:, split:]]
+    for bits in reversed(stages):
+        uppers = [((place >> bit) & 1) == 1 for bit in bits]
+        got = by_bit(bits, parts, axes, count)
+        parts = [
+            jnp.where(u, jnp.concatenate([g, p]), jnp.concatenate([p, g]))
+            for p, g, u in zip(parts, got, uppers)
+        ]
+    return jnp.concatenate(parts, axis=1)
 
 
 def gather_rep(block):

time: 248 us -> 250 us (level)
  waiting for transfers between devices: 102 us -> 92.5 us
  starting transfers between devices: 53.7 us -> 59.1 us
  other arithmetic: 16.8 us -> 20.6 us
    ppermute x8 -> x12, waiting for transfers between devices: 38.2 us -> 26.4 us  [by_bit(): lax.ppermute(joined, axes, [(i, i ^ 1 << bit) for i in range(count)])]
    ppermute x4, starting transfers between devices: 8.25 us -> 14.2 us  [halving_sum(): lax.ppermute(block, axes, [(i, i ^ 1 << bit) for i in range(count)])]
    ppermute x2 -> x0, local copies, waits for them, and re-layouts: 4.22 us -> none  [the longest x1 2.63 us: halving_sum(): block = kept + lax.ppermute(sent, axes, pairs)]
    concatenate x0 -> x2, local copies, waits for them, and re-layouts: none -> 3.88 us  [by_bit(): joined = jnp.concatenate([pieces[i] for i in group], axis=1)]
    slice x0 -> x8, local copies, waits for them, and re-layouts: none -> 3.29 us  [the longest x6 3.28 us: by_bit(): got[i] = moved[:, offset:offset + size]]
    select_n x2 -> x0, local copies, waits for them, and re-layouts: 2.99 us -> none  [the longest x1 2.66 us: halving_sum(): sent = jnp.where(upper, block[:half], block[half:])]
    dot_general x1, matrix products: 1.98 us -> 4.7 us  [shards(): jnp.einsum('teab,taf->ebf', merged_hi, scaled_tiles, preferred_element_ty...]
    slice x3 -> x2, local copies, waits for them, and re-layouts: 6.53 us -> 3.84 us  [shards(): grad_self, grad_neigh = (grads[:width], grads[width:])]
  transfers between devices with their start and end apart: 21 -> 25, of which waited for: 15 -> 17; matrix products, arithmetic and copies ran while one was open for 15% -> 16% of each run, Pallas kernels for 0% -> 0%
where the time goes in v2:
time: 250 us; the launch traced here: 248 us
  waiting for transfers between devices  92.5 us (37%)
  starting transfers between devices  59.1 us (24%)
  local copies, waits for them, and re-layouts  35.5 us (14%)
  matrix products  25.9 us (10%)
  other arithmetic  20.6 us (8%)
  between operations  14.7 us (6%)
    ppermute x12, waiting for transfers between devices, by_bit(): lax.ppermute(joined, axes, [(i, i ^ 1 << bit) for i in range(count)])  26.4 us
    ppermute x3, waiting for transfers between devices, gather_rep(): lax.ppermute(block, 'rep', [(i, (i + shift) % count) for i in range(count)])  23.8 us
    ppermute x4, waiting for transfers between devices, halving_sum(): lax.ppermute(block, axes, [(i, i ^ 1 << bit) for i in range(count)])  21.6 us
    ppermute x12, starting transfers between devices, by_bit(): lax.ppermute(joined, axes, [(i, i ^ 1 << bit) for i in range(count)])  18.8 us
    all_to_all x1, waiting for transfers between devices, shards(): got = lax.all_to_all(sent, 'dom', split_axis=0, concat_axis=0, tiled=True)  17.9 us
    ppermute x4, starting transfers between devices, halving_sum(): lax.ppermute(block, axes, [(i, i ^ 1 << bit) for i in range(count)])  14.2 us
    all_to_all x1, starting transfers between devices, shards(): got = lax.all_to_all(sent, 'dom', split_axis=0, concat_axis=0, tiled=True)  13.2 us
    unnamed x44, local copies, waits for them, and re-layouts  8.71 us
  transfers between devices with their start and end apart: 25, of which 17 were waited for; matrix products, arithmetic and copies ran while one was open for 16% of the time, Pallas kernels for 0%

profile of v2, /device:TPU:1, one launch (start us, length us, event | category | flops | bytes accessed | tf_op | source)
XLA Modules:
  0.0 248.4 jit_solution(9808141940529945579)
XLA Ops:
  13.3 13.2 %all-to-all-start = ((bf16[64,2,2112]{2,1,0:T(2,128)(2,1)}), bf16[64,2,2112]{2,1,0:T(2,128)(2,1)S(1)}, u32[]{:S(2)}, u32[]{:S(2)}) async-start(bf16[64,2,2112]{2,1,0:T(2,128)(2,1)} %reshape.193), calls=%async_computation | async-start | bytes 1114112 | tf_op jit(solution)/shard_map/all_to_all | solution.py:128
  26.6 17.9 %all-to-all-done = bf16[64,2,2112]{2,1,0:T(2,128)(2,1)S(1)} async-done(((bf16[64,2,2112]{2,1,0:T(2,128)(2,1)}), bf16[64,2,2112]{2,1,0:T(2,128)(2,1)S(1)}, u32[]{:S(2)}, u32[]{:S(2)}) %all-to-all-start) | async-done | bytes 540704 | tf_op jit(solution)/shard_map/all_to_all | solution.py:128
  48.0 2.5 %collective-permute-start.2 = (bf16[512,512]{1,0:T(8,128)(2,1)S(1)}, bf16[512,512]{1,0:T(8,128)(2,1)S(1)}, u32[]{:S(2)}, u32[]{:S(2)}) collective-permute-start(bf16[512,512]{1,0:T(8,128)(2,1)S(1)} %convolution_convert_fusion), channel_id=1, source_target_pairs={{0,3},{1,0},{2,1},{3,2},{4,7},{5,4},{6,5},{7,6},{8,11},{9,8},{10,9... | collective-permute-start | bytes 1572872 | tf_op jit(solution)/shard_map/ppermute | solution.py:91
  53.4 19.2 %collective-permute-done.2 = bf16[512,512]{1,0:T(8,128)(2,1)S(1)} collective-permute-done((bf16[512,512]{1,0:T(8,128)(2,1)S(1)}, bf16[512,512]{1,0:T(8,128)(2,1)S(1)}, u32[]{:S(2)}, u32[]{:S(2)}) %collective-permute-start.2) | collective-permute-done | bytes 524320 | tf_op jit(solution)/shard_map/ppermute | solution.py:91
  72.6 4.6 %collective-permute-done = bf16[512,512]{1,0:T(8,128)(2,1)S(1)} collective-permute-done((bf16[512,512]{1,0:T(8,128)(2,1)S(1)}, bf16[512,512]{1,0:T(8,128)(2,1)S(1)}, u32[]{:S(2)}, u32[]{:S(2)}) %collective-permute-start) | collective-permute-done | bytes 524320 | tf_op jit(solution)/shard_map/ppermute | solution.py:91
  78.8 2.3 gather_fusion
  82.1 2.8 %collective-permute-start.3 = (bf16[512,512]{1,0:T(8,128)(2,1)}, bf16[512,512]{1,0:T(8,128)(2,1)}, u32[]{:S(2)}, u32[]{:S(2)}) collective-permute-start(bf16[512,512]{1,0:T(8,128)(2,1)} %get-tuple-element.41), channel_id=1, source_target_pairs={{0,4},{4,8},{8,12},{12,16},{16,20},{20,24},{24,28},{28,32},{32,36}... | collective-permute-start | bytes 1572872 | tf_op jit(solution)/shard_map/ppermute | solution.py:20
  84.9 2.4 collective-permute-start.4
  87.4 4.4 %subtract_convert_fusion = (bf16[4,24,128,128]{3,1,2,0:T(8,128)(2,1)}, bf16[4,24,128,128]{3,1,2,0:T(8,128)(2,1)}) fusion(bf16[4,12,128,128]{3,2,1,0:T(8,128)(2,1)S(1)} %copy-done.7, s32[4,12]{1,0:T(4,128)S(1)} %broadcast_subtract_fusion), kind=kOutput, calls=%fused_computation.2 | convolution fusion | flops 44041344 | bytes 7864512 | tf_op jit(solution)/shard_map/tke,tkab->teab/dot_general | solution.py:142
  93.3 2.5 %collective-permute-done.4 = bf16[512,512]{1,0:T(8,128)(2,1)} collective-permute-done((bf16[512,512]{1,0:T(8,128)(2,1)}, bf16[512,512]{1,0:T(8,128)(2,1)}, u32[]{:S(2)}, u32[]{:S(2)}) %collective-permute-start.4) | collective-permute-done | bytes 524320 | tf_op jit(solution)/shard_map/ppermute | solution.py:23
  107.9 2.2 reshape.173
  114.9 4.7 %fusion.60 = (bf16[24,128,512]{2,1,0:T(8,128)(2,1)S(1)}, f32[24,128,512]{2,1,0:T(8,128)}) fusion(f32[24,128,512,1]{2,1,3,0:T(8,128)S(1)} %fusion, bf16[4,128,512,1]{2,1,0,3:T(8,128)(2,1)S(1)} %bitcast.80, bf16[4,24,128,128]{3,1,2,0:T(8,128)(2,1)S(1)} %copy-done.5), kind=kOutput, calls=%fused_computation.136 | convolution fusion | flops 1613758464 | bytes 19398656 | tf_op jit(solution)/shard_map/teab,taf->ebf/dot_general | solution.py:174
  123.7 2.6 %copy.108 = f32[128,2050]{0,1:T(8,128)} copy(f32[128,2050]{1,0:T(8,128)} %pad_maximum_fusion.3) | data formatting | bytes 2099200 | tf_op jit(solution)/shard_map/concatenate | solution.py:49
  131.0 4.9 %slice.264 = f32[16,128,512]{2,1,0:T(8,128)} slice(f32[24,128,512]{2,1,0:T(8,128)} %get-tuple-element.50), slice={[4:20], [0:128], [0:512]} | slice | bytes 8388608 | tf_op jit(solution)/shard_map/slice | solution.py:180
  138.2 2.4 fusion.33
  148.2 6.5 %collective-permute-done.8 = f32[64,1024]{1,0:T(8,128)S(1)} collective-permute-done((f32[64,1024]{1,0:T(8,128)S(1)}, f32[64,1024]{1,0:T(8,128)S(1)}, u32[]{:S(2)}, u32[]{:S(2)}) %collective-permute-start.8) | collective-permute-done | bytes 262176 | tf_op jit(solution)/shard_map/ppermute | solution.py:50
  155.1 4.0 %collective-permute-done.9 = f32[32,1024]{1,0:T(8,128)S(1)} collective-permute-done((f32[32,1024]{1,0:T(8,128)S(1)}, f32[32,1024]{1,0:T(8,128)S(1)}, u32[]{:S(2)}, u32[]{:S(2)}) %collective-permute-start.9) | collective-permute-done | bytes 131104 | tf_op jit(solution)/shard_map/ppermute | solution.py:50
  159.7 7.2 %collective-permute-done.12 = f32[16,2050]{1,0:T(8,128)S(1)} collective-permute-done((f32[16,2050]{1,0:T(8,128)S(1)}, f32[16,2050]{1,0:T(8,128)S(1)}, u32[]{:S(2)}, u32[]{:S(2)}) %collective-permute-start.12) | collective-permute-done | bytes 131232 | tf_op jit(solution)/shard_map/ppermute | solution.py:50
  167.0 7.9 %collective-permute-start.13 = (f32[16,2050]{1,0:T(8,128)S(1)}, f32[16,2050]{1,0:T(8,128)S(1)}, u32[]{:S(2)}, u32[]{:S(2)}) collective-permute-start(f32[16,2050]{1,0:T(8,128)S(1)} %pad_maximum_fusion.8), channel_id=1, source_target_pairs={{0,16},{1,17},{2,18},{3,19},{4,20},{5,21},{6,22},{7,23},{8,24},{9,... | collective-permute-start | bytes 393608 | tf_op jit(solution)/shard_map/ppermute | solution.py:75
  174.8 7.1 %collective-permute-done.13 = f32[16,2050]{1,0:T(8,128)S(1)} collective-permute-done((f32[16,2050]{1,0:T(8,128)S(1)}, f32[16,2050]{1,0:T(8,128)S(1)}, u32[]{:S(2)}, u32[]{:S(2)}) %collective-permute-start.13) | collective-permute-done | bytes 131232 | tf_op jit(solution)/shard_map/ppermute | solution.py:75
  182.0 6.4 %collective-permute-done.14 = f32[16,2050]{1,0:T(8,128)S(1)} collective-permute-done((f32[16,2050]{1,0:T(8,128)S(1)}, f32[16,2050]{1,0:T(8,128)S(1)}, u32[]{:S(2)}, u32[]{:S(2)}) %collective-permute-start.14) | collective-permute-done | bytes 131232 | tf_op jit(solution)/shard_map/ppermute | solution.py:75
  188.5 5.4 %collective-permute-done.15 = f32[16,2050]{1,0:T(8,128)S(1)} collective-permute-done((f32[16,2050]{1,0:T(8,128)S(1)}, f32[16,2050]{1,0:T(8,128)S(1)}, u32[]{:S(2)}, u32[]{:S(2)}) %collective-permute-start.15) | collective-permute-done | bytes 131232 | tf_op jit(solution)/shard_map/ppermute | solution.py:75
  193.9 6.1 %collective-permute-start.16 = (f32[16,2050]{1,0:T(8,128)S(1)}, f32[16,2050]{1,0:T(8,128)S(1)}, u32[]{:S(2)}, u32[]{:S(2)}) collective-permute-start(f32[16,2050]{1,0:T(8,128)S(1)} %add.164), channel_id=1, source_target_pairs={{0,32},{1,33},{2,34},{3,35},{4,36},{5,37},{6,38},{7,39},{8,40},{9,... | collective-permute-start | bytes 393608 | tf_op jit(solution)/shard_map/ppermute | solution.py:75
  200.0 2.9 %collective-permute-done.16 = f32[16,2050]{1,0:T(8,128)S(1)} collective-permute-done((f32[16,2050]{1,0:T(8,128)S(1)}, f32[16,2050]{1,0:T(8,128)S(1)}, u32[]{:S(2)}, u32[]{:S(2)}) %collective-permute-start.16) | collective-permute-done | bytes 131232 | tf_op jit(solution)/shard_map/ppermute | solution.py:75
  203.0 3.9 %collective-permute-done.17 = f32[16,2050]{1,0:T(8,128)S(1)} collective-permute-done((f32[16,2050]{1,0:T(8,128)S(1)}, f32[16,2050]{1,0:T(8,128)S(1)}, u32[]{:S(2)}, u32[]{:S(2)}) %collective-permute-start.17) | collective-permute-done | bytes 131232 | tf_op jit(solution)/shard_map/ppermute | solution.py:50
  208.2 3.5 %collective-permute-start.20 = (f32[32,1026]{1,0:T(8,128)S(1)}, f32[32,1026]{1,0:T(8,128)S(1)}, u32[]{:S(2)}, u32[]{:S(2)}) collective-permute-start(f32[32,1026]{1,0:T(8,128)S(1)} %maximum_select_fusion.6), channel_id=1, source_target_pairs={{0,8},{1,9},{2,10},{3,11},{4,12},{5,13},{6,14},{7,15},{8,0},{9,1},... | collective-permute-start | bytes 393992 | tf_op jit(solution)/shard_map/ppermute | solution.py:50
  211.7 2.3 collective-permute-start.19
  215.6 3.7 %collective-permute-done.19 = f32[64,1024]{1,0:T(8,128)S(1)} collective-permute-done((f32[64,1024]{1,0:T(8,128)S(1)}, f32[64,1024]{1,0:T(8,128)S(1)}, u32[]{:S(2)}, u32[]{:S(2)}) %collective-permute-start.19) | collective-permute-done | bytes 262176 | tf_op jit(solution)/shard_map/ppermute | solution.py:50
  221.4 7.0 %collective-permute-start.22 = (f32[128,2050]{0,1:T(8,128)}, f32[128,2050]{0,1:T(8,128)S(1)}, u32[]{:S(2)}, u32[]{:S(2)}) collective-permute-start(f32[128,2050]{0,1:T(8,128)} %copy.111), channel_id=1, source_target_pairs={{0,4},{1,5},{2,6},{3,7},{4,0},{5,1},{6,2},{7,3},{8,12},{9,13},{10,... | collective-permute-start | bytes 3148808 | tf_op jit(solution)/shard_map/ppermute | solution.py:50
  228.4 2.5 %fusion.62 = f32[512,512]{1,0:T(8,128)} fusion(bf16[512,512]{1,0:T(8,128)(2,1)S(1)} %get-tuple-element.32, bf16[512,512]{1,0:T(8,128)(2,1)} %param.18), kind=kOutput, calls=%fused_computation.138 | convolution fusion | flops 268435456 | bytes 2097152 | tf_op jit(solution)/shard_map/dot_general | solution.py:35
  235.5 2.6 %slice.252 = f32[512,512]{1,0:T(8,128)} reshape(f32[128,2048]{1,0:T(8,128)} %get-tuple-element.39) | data formatting | bytes 2097152 | tf_op jit(solution)/shard_map/slice | solution.py:170
  239.4 2.2 add_convert_fusion
  (162 shorter events, 64.1 us)
Async XLA Ops:
  7.2 94.5 %copy-start = (bf16[512,512]{1,0:T(8,128)(2,1)S(1)}, bf16[512,512]{1,0:T(8,128)(2,1)}, u32[]{:S(2)}) copy-start(bf16[512,512]{1,0:T(8,128)(2,1)} %param.19) | copy-start | bytes 1572868
  10.5 16.0 %copy-start.14 = (s32[4,12]{1,0:T(4,128)S(1)}, s32[4,12]{1,0:T(4,128)}, u32[]{:S(2)}) copy-start(s32[4,12]{1,0:T(4,128)} %param.17) | copy-start | bytes 580
  13.3 31.2 %all-to-all-start = ((bf16[64,2,2112]{2,1,0:T(2,128)(2,1)}), bf16[64,2,2112]{2,1,0:T(2,128)(2,1)S(1)}, u32[]{:S(2)}, u32[]{:S(2)}) async-start(bf16[64,2,2112]{2,1,0:T(2,128)(2,1)} %reshape.193), calls=%async_computation | async-start | bytes 1114112 | tf_op jit(solution)/shard_map/all_to_all | solution.py:128
  26.5 212.8 %reduce-scatter.2.cloned.1.call-start = ((), (), s32[]{:S(2)}) async-start(), calls=%async_computation.2 | async-start | bytes 5242880 | tf_op jit(solution)/shard_map/reduce_scatter | solution.py:183
  45.2 6.5 %copy-start.15 = (s32[4,12]{1,0:T(4,128)S(1)}, s32[4,12]{1,0:T(4,128)}, u32[]{:S(2)}) copy-start(s32[4,12]{1,0:T(4,128)} %param.16) | copy-start | bytes 580
  45.2 6.5 %copy-start.12 = (bf16[4,12,128,128]{3,2,1,0:T(8,128)(2,1)S(1)}, bf16[4,12,128,128]{3,2,1,0:T(8,128)(2,1)}, u32[]{:S(2)}) copy-start(bf16[4,12,128,128]{3,2,1,0:T(8,128)(2,1)} %param.15) | copy-start | bytes 4718596
  48.0 43.8 %copy-start.8 = (bf16[512,512]{1,0:T(8,128)(2,1)}, bf16[512,512]{1,0:T(8,128)(2,1)S(1)}, u32[]{:S(2)}) copy-start(bf16[512,512]{1,0:T(8,128)(2,1)S(1)} %convolution_convert_fusion) | copy-start | bytes 1572868
  48.0 24.5 %collective-permute-start.2 = (bf16[512,512]{1,0:T(8,128)(2,1)S(1)}, bf16[512,512]{1,0:T(8,128)(2,1)S(1)}, u32[]{:S(2)}, u32[]{:S(2)}) collective-permute-start(bf16[512,512]{1,0:T(8,128)(2,1)S(1)} %convolution_convert_fusion), channel_id=1, source_target_pairs={{0,3},{1,0},{2,1},{3,2},{4,7},{5,4},{6,5},{7,6},{8,11},{9,8},{10,9... | collective-permute-start | bytes 1572872 | tf_op jit(solution)/shard_map/ppermute | solution.py:91
  50.6 22.0 %collective-permute-start.1 = (bf16[512,512]{1,0:T(8,128)(2,1)S(1)}, bf16[512,512]{1,0:T(8,128)(2,1)S(1)}, u32[]{:S(2)}, u32[]{:S(2)}) collective-permute-start(bf16[512,512]{1,0:T(8,128)(2,1)S(1)} %convolution_convert_fusion), channel_id=1, source_target_pairs={{0,2},{1,3},{2,0},{3,1},{4,6},{5,7},{6,4},{7,5},{8,10},{9,11},{10,... | collective-permute-start | bytes 1572872 | tf_op jit(solution)/shard_map/ppermute | solution.py:91
  51.1 26.1 %collective-permute-start = (bf16[512,512]{1,0:T(8,128)(2,1)S(1)}, bf16[512,512]{1,0:T(8,128)(2,1)S(1)}, u32[]{:S(2)}, u32[]{:S(2)}) collective-permute-start(bf16[512,512]{1,0:T(8,128)(2,1)S(1)} %convolution_convert_fusion), channel_id=1, source_target_pairs={{0,1},{1,2},{2,3},{3,0},{4,5},{5,6},{6,7},{7,4},{8,9},{9,10},{10,1... | collective-permute-start | bytes 1572872 | tf_op jit(solution)/shard_map/ppermute | solution.py:91
  81.0 6.3 %copy-start.7 = (bf16[4,12,128,128]{3,2,1,0:T(8,128)(2,1)S(1)}, bf16[4,12,128,128]{3,2,1,0:T(8,128)(2,1)}, u32[]{:S(2)}) copy-start(bf16[4,12,128,128]{3,2,1,0:T(8,128)(2,1)} %get-tuple-element.34) | copy-start | bytes 4718596
  82.1 11.2 %collective-permute-start.3 = (bf16[512,512]{1,0:T(8,128)(2,1)}, bf16[512,512]{1,0:T(8,128)(2,1)}, u32[]{:S(2)}, u32[]{:S(2)}) collective-permute-start(bf16[512,512]{1,0:T(8,128)(2,1)} %get-tuple-element.41), channel_id=1, source_target_pairs={{0,4},{4,8},{8,12},{12,16},{16,20},{20,24},{24,28},{28,32},{32,36}... | collective-permute-start | bytes 1572872 | tf_op jit(solution)/shard_map/ppermute | solution.py:20
  84.9 10.8 %collective-permute-start.4 = (bf16[512,512]{1,0:T(8,128)(2,1)}, bf16[512,512]{1,0:T(8,128)(2,1)}, u32[]{:S(2)}, u32[]{:S(2)}) collective-permute-start(bf16[512,512]{1,0:T(8,128)(2,1)} %get-tuple-element.42), channel_id=1, source_target_pairs={{4,0},{8,4},{12,8},{16,12},{20,16},{24,20},{28,24},{32,28},{36,32}... | collective-permute-start | bytes 1572872 | tf_op jit(solution)/shard_map/ppermute | solution.py:23
  120.7 15.1 %collective-permute-start.5 = (bf16[512,512]{1,0:T(8,128)(2,1)}, bf16[512,512]{1,0:T(8,128)(2,1)}, u32[]{:S(2)}, u32[]{:S(2)}) collective-permute-start(bf16[512,512]{1,0:T(8,128)(2,1)} %bitcast.29), channel_id=1, source_target_pairs={{0,4},{4,8},{8,12},{12,16},{16,20},{20,24},{24,28},{28,32},{32,36}... | collective-permute-start | bytes 1572872 | tf_op jit(solution)/shard_map/ppermute | solution.py:12
  126.2 14.4 %collective-permute-start.7 = (f32[128,2050]{0,1:T(8,128)}, f32[128,2050]{0,1:T(8,128)}, u32[]{:S(2)}, u32[]{:S(2)}) collective-permute-start(f32[128,2050]{0,1:T(8,128)} %copy.108), channel_id=1, source_target_pairs={{0,4},{1,5},{2,6},{3,7},{4,0},{5,1},{6,2},{7,3},{8,12},{9,13},{10,... | collective-permute-start | bytes 3148808 | tf_op jit(solution)/shard_map/ppermute | solution.py:50
  127.5 10.7 %collective-permute-start.6 = (bf16[512,512]{1,0:T(8,128)(2,1)}, bf16[512,512]{1,0:T(8,128)(2,1)S(1)}, u32[]{:S(2)}, u32[]{:S(2)}) collective-permute-start(bf16[512,512]{1,0:T(8,128)(2,1)} %bitcast.81), channel_id=1, source_target_pairs={{4,0},{8,4},{12,8},{16,12},{20,16},{24,20},{28,24},{32,28},{36,32}... | collective-permute-start | bytes 1572872 | tf_op jit(solution)/shard_map/ppermute | solution.py:12
  146.5 8.2 %collective-permute-start.8 = (f32[64,1024]{1,0:T(8,128)S(1)}, f32[64,1024]{1,0:T(8,128)S(1)}, u32[]{:S(2)}, u32[]{:S(2)}) collective-permute-start(f32[64,1024]{1,0:T(8,128)S(1)} %slice_select_fusion.3), channel_id=1, source_target_pairs={{0,8},{1,9},{2,10},{3,11},{4,12},{5,13},{6,14},{7,15},{8,0},{9,1},... | collective-permute-start | bytes 786440 | tf_op jit(solution)/shard_map/ppermute | solution.py:50
  146.7 8.2 %collective-permute-start.10 = (f32[64,1026]{1,0:T(8,128)S(1)}, f32[64,1026]{1,0:T(8,128)S(1)}, u32[]{:S(2)}, u32[]{:S(2)}) collective-permute-start(f32[64,1026]{1,0:T(8,128)S(1)} %slice_select_fusion.2), channel_id=1, source_target_pairs={{0,64},{1,65},{2,66},{3,67},{4,68},{5,69},{6,70},{7,71},{8,72},{9,... | collective-permute-start | bytes 787976 | tf_op jit(solution)/shard_map/ppermute | solution.py:50
  154.8 4.3 %collective-permute-start.9 = (f32[32,1024]{1,0:T(8,128)S(1)}, f32[32,1024]{1,0:T(8,128)S(1)}, u32[]{:S(2)}, u32[]{:S(2)}) collective-permute-start(f32[32,1024]{1,0:T(8,128)S(1)} %slice_select_fusion.5), channel_id=1, source_target_pairs={{0,64},{1,65},{2,66},{3,67},{4,68},{5,69},{6,70},{7,71},{8,72},{9,... | collective-permute-start | bytes 393224 | tf_op jit(solution)/shard_map/ppermute | solution.py:50
  155.0 4.5 %collective-permute-start.11 = (f32[32,1026]{1,0:T(8,128)S(1)}, f32[32,1026]{1,0:T(8,128)S(1)}, u32[]{:S(2)}, u32[]{:S(2)}) collective-permute-start(f32[32,1026]{1,0:T(8,128)S(1)} %slice_select_fusion.4), channel_id=1, source_target_pairs={{0,8},{1,9},{2,10},{3,11},{4,12},{5,13},{6,14},{7,15},{8,0},{9,1},... | collective-permute-start | bytes 393992 | tf_op jit(solution)/shard_map/ppermute | solution.py:50
  159.6 7.3 %collective-permute-start.12 = (f32[16,2050]{1,0:T(8,128)S(1)}, f32[16,2050]{1,0:T(8,128)S(1)}, u32[]{:S(2)}, u32[]{:S(2)}) collective-permute-start(f32[16,2050]{1,0:T(8,128)S(1)} %pad_maximum_fusion.7), channel_id=1, source_target_pairs={{0,1},{1,0},{2,3},{3,2},{4,5},{5,4},{6,7},{7,6},{8,9},{9,8},{10,11... | collective-permute-start | bytes 393608 | tf_op jit(solution)/shard_map/ppermute | solution.py:50
  167.0 14.9 %collective-permute-start.13 = (f32[16,2050]{1,0:T(8,128)S(1)}, f32[16,2050]{1,0:T(8,128)S(1)}, u32[]{:S(2)}, u32[]{:S(2)}) collective-permute-start(f32[16,2050]{1,0:T(8,128)S(1)} %pad_maximum_fusion.8), channel_id=1, source_target_pairs={{0,16},{1,17},{2,18},{3,19},{4,20},{5,21},{6,22},{7,23},{8,24},{9,... | collective-permute-start | bytes 393608 | tf_op jit(solution)/shard_map/ppermute | solution.py:75
  181.9 6.5 %collective-permute-start.14 = (f32[16,2050]{1,0:T(8,128)S(1)}, f32[16,2050]{1,0:T(8,128)S(1)}, u32[]{:S(2)}, u32[]{:S(2)}) collective-permute-start(f32[16,2050]{1,0:T(8,128)S(1)} %fusion.57), channel_id=1, source_target_pairs={{0,128},{1,129},{2,130},{3,131},{4,132},{5,133},{6,134},{7,135},{8... | collective-permute-start | bytes 393608 | tf_op jit(solution)/shard_map/ppermute | solution.py:75
  188.4 5.5 %collective-permute-start.15 = (f32[16,2050]{1,0:T(8,128)S(1)}, f32[16,2050]{1,0:T(8,128)S(1)}, u32[]{:S(2)}, u32[]{:S(2)}) collective-permute-start(f32[16,2050]{1,0:T(8,128)S(1)} %add.163), channel_id=1, source_target_pairs={{0,2},{1,3},{2,0},{3,1},{4,6},{5,7},{6,4},{7,5},{8,10},{9,11},{10,... | collective-permute-start | bytes 393608 | tf_op jit(solution)/shard_map/ppermute | solution.py:75
  193.9 9.0 %collective-permute-start.16 = (f32[16,2050]{1,0:T(8,128)S(1)}, f32[16,2050]{1,0:T(8,128)S(1)}, u32[]{:S(2)}, u32[]{:S(2)}) collective-permute-start(f32[16,2050]{1,0:T(8,128)S(1)} %add.164), channel_id=1, source_target_pairs={{0,32},{1,33},{2,34},{3,35},{4,36},{5,37},{6,38},{7,39},{8,40},{9,... | collective-permute-start | bytes 393608 | tf_op jit(solution)/shard_map/ppermute | solution.py:75
  202.9 4.0 %collective-permute-start.17 = (f32[16,2050]{1,0:T(8,128)S(1)}, f32[16,2050]{1,0:T(8,128)S(1)}, u32[]{:S(2)}, u32[]{:S(2)}) collective-permute-start(f32[16,2050]{1,0:T(8,128)S(1)} %add.165), channel_id=1, source_target_pairs={{0,1},{1,0},{2,3},{3,2},{4,5},{5,4},{6,7},{7,6},{8,9},{9,8},{10,11... | collective-permute-start | bytes 393608 | tf_op jit(solution)/shard_map/ppermute | solution.py:50
  206.9 4.8 %collective-permute-start.18 = (f32[32,1024]{1,0:T(8,128)S(1)}, f32[32,1024]{1,0:T(8,128)S(1)}, u32[]{:S(2)}, u32[]{:S(2)}) collective-permute-start(f32[32,1024]{1,0:T(8,128)S(1)} %maximum_select_fusion.7), channel_id=1, source_target_pairs={{0,64},{1,65},{2,66},{3,67},{4,68},{5,69},{6,70},{7,71},{8,72},{9,... | collective-permute-start | bytes 393224 | tf_op jit(solution)/shard_map/ppermute | solution.py:50
  208.2 6.0 %collective-permute-start.20 = (f32[32,1026]{1,0:T(8,128)S(1)}, f32[32,1026]{1,0:T(8,128)S(1)}, u32[]{:S(2)}, u32[]{:S(2)}) collective-permute-start(f32[32,1026]{1,0:T(8,128)S(1)} %maximum_select_fusion.6), channel_id=1, source_target_pairs={{0,8},{1,9},{2,10},{3,11},{4,12},{5,13},{6,14},{7,15},{8,0},{9,1},... | collective-permute-start | bytes 393992 | tf_op jit(solution)/shard_map/ppermute | solution.py:50
  211.7 7.7 %collective-permute-start.19 = (f32[64,1024]{1,0:T(8,128)S(1)}, f32[64,1024]{1,0:T(8,128)S(1)}, u32[]{:S(2)}, u32[]{:S(2)}) collective-permute-start(f32[64,1024]{1,0:T(8,128)S(1)} %maximum_select_fusion.5), channel_id=1, source_target_pairs={{0,8},{1,9},{2,10},{3,11},{4,12},{5,13},{6,14},{7,15},{8,0},{9,1},... | collective-permute-start | bytes 786440 | tf_op jit(solution)/shard_map/ppermute | solution.py:50
  214.3 5.7 %collective-permute-start.21 = (f32[64,1026]{1,0:T(8,128)S(1)}, f32[64,1026]{1,0:T(8,128)S(1)}, u32[]{:S(2)}, u32[]{:S(2)}) collective-permute-start(f32[64,1026]{1,0:T(8,128)S(1)} %maximum_select_fusion.4), channel_id=1, source_target_pairs={{0,64},{1,65},{2,66},{3,67},{4,68},{5,69},{6,70},{7,71},{8,72},{9,... | collective-permute-start | bytes 787976 | tf_op jit(solution)/shard_map/ppermute | solution.py:50
  221.4 9.5 %collective-permute-start.22 = (f32[128,2050]{0,1:T(8,128)}, f32[128,2050]{0,1:T(8,128)S(1)}, u32[]{:S(2)}, u32[]{:S(2)}) collective-permute-start(f32[128,2050]{0,1:T(8,128)} %copy.111), channel_id=1, source_target_pairs={{0,4},{1,5},{2,6},{3,7},{4,0},{5,1},{6,2},{7,3},{8,12},{9,13},{10,... | collective-permute-start | bytes 3148808 | tf_op jit(solution)/shard_map/ppermute | solution.py:50
  235.5 3.8 %copy-start.10 = (f32[512,512]{1,0:T(8,128)S(1)}, f32[512,512]{1,0:T(8,128)}, u32[]{:S(2)}) copy-start(f32[512,512]{1,0:T(8,128)} %fusion.62) | copy-start | bytes 3145732
  (11 other events, 20.9 us)
Sparse Core Ops, SparseCore 0:
  140.8 50.6 reduce-scatter.1

commit v3 on v1

--- a/solution.py
+++ b/solution.py
@@ -41,7 +41,7 @@
 DOUBLING_BITS = (4, 7, 1, 5)
 
 
-def halving_sum(block, axes):
+def halving_sum(block, axes, held, side):
     count = 1
     for axis in axes:
         count *= lax.axis_size(axis)
@@ -54,15 +54,31 @@
         kept = jnp.where(upper, block[half:], block[:half])
         sent = jnp.where(upper, block[:half], block[half:])
         block = kept + lax.ppermute(sent, axes, pairs)
+        if bit == bits[0]:
+            block, held = lax.optimization_barrier((block, held))
+            held = side(held)
     for bit in DOUBLING_BITS:
         if (1 << bit) < count:
             block = block + lax.ppermute(block, axes, [(i, i ^ (1 << bit)) for i in range(count)])
+    block, held = lax.optimization_barrier((block, held))
     for bit in reversed(bits):
         pairs = [(i, i ^ (1 << bit)) for i in range(count)]
         upper = ((place >> bit) & 1) == 1
         got = lax.ppermute(block, axes, pairs)
         block = jnp.where(upper, jnp.concatenate([got, block]), jnp.concatenate([block, got]))
-    return block
+    return block, held
+
+
+def scatter_rep(block):
+    count = lax.axis_size("rep")
+    place = lax.axis_index("rep")
+    tiles = block.reshape(count, block.shape[0] // count, *block.shape[1:])
+    total = tiles[place]
+    for shift in range(1, count):
+        total = total + lax.ppermute(
+            tiles[(place + shift) % count], "rep", [(i, (i + shift) % count) for i in range(count)]
+        )
+    return total
 
 
 def gather_rep(block):
@@ -136,20 +152,6 @@
     layer_out = jnp.where(pre > 0, pre, jnp.expm1(jnp.minimum(pre, 0.0))).astype(jnp.bfloat16)
     slope = jnp.where(pre > 0, 1.0, jnp.exp(jnp.minimum(pre, 0.0)))
     dz = (cotangent.astype(jnp.float32) * slope).astype(jnp.bfloat16)
-    lanes = 2 * width * width // 256
-    packed = halving_sum(
-        jnp.concatenate(
-            [
-                jnp.concatenate([contract_rows(features, dz), contract_rows(agg, dz)]).reshape(256, lanes),
-                jnp.sum(dz, axis=0, dtype=jnp.float32).reshape(256, -1),
-            ],
-            axis=1,
-        ),
-        ("dom", "rep"),
-    )
-    grads = packed[:, :lanes].reshape(2 * width, width)
-    grad_self, grad_neigh = grads[:width], grads[width:]
-    grad_bias = packed[:, lanes:].reshape(width)
     scaled = (contract_cols(dz, w_neigh) / degree.reshape(rows, 1)).astype(jnp.bfloat16)
     scaled_tiles = scaled.reshape(row_tiles, 128, width)
     buffer = jnp.einsum(
@@ -161,7 +163,22 @@
     core = buffer[rim_rows : rim_rows + part_rows]
     core = core.at[:rim_rows].add(pass_rim(upper, 1))
     core = core.at[part_rows - rim_rows :].add(pass_rim(lower, -1))
-    back = lax.psum_scatter(core, "rep", scatter_dimension=0, tiled=True)
+    lanes = 2 * width * width // 256
+    packed, back = halving_sum(
+        jnp.concatenate(
+            [
+                jnp.concatenate([contract_rows(features, dz), contract_rows(agg, dz)]).reshape(256, lanes),
+                jnp.sum(dz, axis=0, dtype=jnp.float32).reshape(256, -1),
+            ],
+            axis=1,
+        ),
+        ("dom", "rep"),
+        core,
+        scatter_rep,
+    )
+    grads = packed[:, :lanes].reshape(2 * width, width)
+    grad_self, grad_neigh = grads[:width], grads[width:]
+    grad_bias = packed[:, lanes:].reshape(width)
     grad_features = (contract_cols(dz, w_self) + back).astype(jnp.bfloat16)
     return (layer_out, grad_features, grad_self, grad_neigh, grad_bias)
 

time: 248 us -> 263 us (1.060); the launches traced: 247 us -> 259 us
  waiting for transfers between devices: 102 us -> 121 us
  between operations: 14.5 us -> 1.2 us
  local copies, waits for them, and re-layouts: 34 us -> 36.8 us
    ppermute x4, waiting for transfers between devices: 19.3 us -> 39 us  [halving_sum(): lax.ppermute(block, axes, [(i, i ^ 1 << bit) for i in range(count)])]
    ppermute x4, waiting for transfers between devices: 23.8 us -> 19 us  [halving_sum(): block = kept + lax.ppermute(sent, axes, pairs)]
    slice x3, local copies, waits for them, and re-layouts: 6.53 us -> 2.77 us  [shards(): grad_self, grad_neigh = (grads[:width], grads[width:])]
    ppermute x4, starting transfers between devices: 16.3 us -> 12.7 us  [halving_sum(): got = lax.ppermute(block, axes, pairs)]
    squeeze x0 -> x1, local copies, waits for them, and re-layouts: none -> 3.49 us  [scatter_rep(): tiles[(place + shift) % count]]
    add x0 -> x1, other arithmetic: none -> 3.32 us  [scatter_rep(): total + lax.ppermute(tiles[(place + shift) % count], 'rep', [(i, (i + shi...]
    ppermute x0 -> x3, starting transfers between devices: none -> 3.23 us  [scatter_rep(): lax.ppermute(tiles[(place + shift) % count], 'rep', [(i, (i + shift) % co...]
    ppermute x4, starting transfers between devices: 8.25 us -> 11.4 us  [halving_sum(): lax.ppermute(block, axes, [(i, i ^ 1 << bit) for i in range(count)])]
  transfers between devices with their start and end apart: 21 -> 23, of which waited for: 15 -> 16; matrix products, arithmetic and copies ran while one was open for 15% -> 11% of each run, Pallas kernels for 0% -> 0%
where the time goes in v3:
time: 263 us; the launch traced here: 259 us
  waiting for transfers between devices  121 us (46%)
  starting transfers between devices  54.9 us (21%)
  local copies, waits for them, and re-layouts  36.8 us (14%)
  matrix products  25.9 us (10%)
  other arithmetic  19.1 us (7%)
    ppermute x4, waiting for transfers between devices, halving_sum(): lax.ppermute(block, axes, [(i, i ^ 1 << bit) for i in range(count)])  39 us
    ppermute x3, waiting for transfers between devices, gather_rep(): lax.ppermute(block, 'rep', [(i, (i + shift) % count) for i in range(count)])  23.8 us
    ppermute x4, waiting for transfers between devices, halving_sum(): block = kept + lax.ppermute(sent, axes, pairs)  19 us
    all_to_all x1, waiting for transfers between devices, shards(): got = lax.all_to_all(sent, 'dom', split_axis=0, concat_axis=0, tiled=True)  18 us
    ppermute x4, waiting for transfers between devices, halving_sum(): got = lax.ppermute(block, axes, pairs)  17.4 us
    all_to_all x1, starting transfers between devices, shards(): got = lax.all_to_all(sent, 'dom', split_axis=0, concat_axis=0, tiled=True)  13.2 us
    ppermute x4, starting transfers between devices, halving_sum(): got = lax.ppermute(block, axes, pairs)  12.7 us
    ppermute x4, starting transfers between devices, halving_sum(): lax.ppermute(block, axes, [(i, i ^ 1 << bit) for i in range(count)])  11.4 us
  transfers between devices with their start and end apart: 23, of which 16 were waited for; matrix products, arithmetic and copies ran while one was open for 11% of the time, Pallas kernels for 0%

profile of v3, /device:TPU:1, one launch (start us, length us, event | category | flops | bytes accessed | tf_op | source)
XLA Modules:
  0.0 258.9 jit_solution(17568869914292664546)
XLA Ops:
  6.8 13.2 %all-to-all-start = ((bf16[64,2,2112]{2,1,0:T(2,128)(2,1)}), bf16[64,2,2112]{2,1,0:T(2,128)(2,1)S(1)}, u32[]{:S(2)}, u32[]{:S(2)}) async-start(bf16[64,2,2112]{2,1,0:T(2,128)(2,1)} %reshape.197), calls=%async_computation | async-start | bytes 1114112 | tf_op jit(solution)/shard_map/all_to_all | solution.py:125
  20.0 18.0 %all-to-all-done = bf16[64,2,2112]{2,1,0:T(2,128)(2,1)S(1)} async-done(((bf16[64,2,2112]{2,1,0:T(2,128)(2,1)}), bf16[64,2,2112]{2,1,0:T(2,128)(2,1)S(1)}, u32[]{:S(2)}, u32[]{:S(2)}) %all-to-all-start) | async-done | bytes 540704 | tf_op jit(solution)/shard_map/all_to_all | solution.py:125
  41.5 2.5 collective-permute-start.2
  46.9 8.8 %collective-permute-done.2 = bf16[512,512]{1,0:T(8,128)(2,1)S(1)} collective-permute-done((bf16[512,512]{1,0:T(8,128)(2,1)S(1)}, bf16[512,512]{1,0:T(8,128)(2,1)S(1)}, u32[]{:S(2)}, u32[]{:S(2)}) %collective-permute-start.2) | collective-permute-done | bytes 524320 | tf_op jit(solution)/shard_map/ppermute | solution.py:88
  55.6 2.7 %collective-permute-done.1 = bf16[512,512]{1,0:T(8,128)(2,1)S(1)} collective-permute-done((bf16[512,512]{1,0:T(8,128)(2,1)S(1)}, bf16[512,512]{1,0:T(8,128)(2,1)S(1)}, u32[]{:S(2)}, u32[]{:S(2)}) %collective-permute-start.1) | collective-permute-done | bytes 524320 | tf_op jit(solution)/shard_map/ppermute | solution.py:88
  58.4 12.3 %collective-permute-done = bf16[512,512]{1,0:T(8,128)(2,1)S(1)} collective-permute-done((bf16[512,512]{1,0:T(8,128)(2,1)S(1)}, bf16[512,512]{1,0:T(8,128)(2,1)S(1)}, u32[]{:S(2)}, u32[]{:S(2)}) %collective-permute-start) | collective-permute-done | bytes 524320 | tf_op jit(solution)/shard_map/ppermute | solution.py:88
  72.2 2.3 gather_fusion
  75.6 2.8 %collective-permute-start.3 = (bf16[512,512]{1,0:T(8,128)(2,1)}, bf16[512,512]{1,0:T(8,128)(2,1)}, u32[]{:S(2)}, u32[]{:S(2)}) collective-permute-start(bf16[512,512]{1,0:T(8,128)(2,1)} %get-tuple-element.52), channel_id=1, source_target_pairs={{0,4},{4,8},{8,12},{12,16},{16,20},{20,24},{24,28},{28,32},{32,36}... | collective-permute-start | bytes 1572872 | tf_op jit(solution)/shard_map/ppermute | solution.py:20
  78.4 2.4 collective-permute-start.4
  80.8 4.4 %subtract_convert_fusion = (bf16[4,24,128,128]{3,1,2,0:T(8,128)(2,1)}, bf16[4,24,128,128]{3,1,2,0:T(8,128)(2,1)}) fusion(bf16[4,12,128,128]{3,2,1,0:T(8,128)(2,1)S(1)} %copy-done.7, s32[4,12]{1,0:T(4,128)S(1)} %broadcast_subtract_fusion), kind=kOutput, calls=%fused_computation.2 | convolution fusion | flops 44041344 | bytes 7864512 | tf_op jit(solution)/shard_map/tke,tkab->teab/dot_general | solution.py:139
  86.7 2.5 collective-permute-done.4
  108.4 4.7 %fusion.62 = (bf16[24,128,512]{2,1,0:T(8,128)(2,1)S(1)}, f32[24,128,512]{2,1,0:T(8,128)}) fusion(f32[24,128,512,1]{2,1,3,0:T(8,128)S(1)} %fusion, bf16[4,128,512,1]{2,1,0,3:T(8,128)(2,1)S(1)} %bitcast.93, bf16[4,24,128,128]{3,1,2,0:T(8,128)(2,1)S(1)} %copy-done.5), kind=kOutput, calls=%fused_computation.124 | convolution fusion | flops 1613758464 | bytes 19398656 | tf_op jit(solution)/shard_map/teab,taf->ebf/dot_general | solution.py:157
  117.2 2.6 copy.112
  123.8 4.9 %slice.179 = f32[16,128,512]{2,1,0:T(8,128)} slice(f32[24,128,512]{2,1,0:T(8,128)} %get-tuple-element.61), slice={[4:20], [0:128], [0:512]} | slice | bytes 8388608 | tf_op jit(solution)/shard_map/slice | solution.py:163
  131.1 2.5 fusion.33
  133.6 2.6 %copy.113 = f32[128,2050]{1,0:T(8,128)} copy(f32[128,2050]{0,1:T(8,128)} %collective-permute-done.5) | data formatting | bytes 2099200 | tf_op jit(solution)/shard_map/ppermute | solution.py:56
  139.5 12.9 %collective-permute-done.8 = f32[64,2050]{1,0:T(8,128)S(1)} collective-permute-done((f32[64,2050]{1,0:T(8,128)S(1)}, f32[64,2050]{1,0:T(8,128)S(1)}, u32[]{:S(2)}, u32[]{:S(2)}) %collective-permute-start.8) | collective-permute-done | bytes 524832 | tf_op jit(solution)/shard_map/ppermute | solution.py:56
  153.8 6.2 %collective-permute-done.9 = f32[32,2050]{1,0:T(8,128)S(1)} collective-permute-done((f32[32,2050]{1,0:T(8,128)S(1)}, f32[32,2050]{1,0:T(8,128)S(1)}, u32[]{:S(2)}, u32[]{:S(2)}) %collective-permute-start.9) | collective-permute-done | bytes 262432 | tf_op jit(solution)/shard_map/ppermute | solution.py:56
  160.2 3.5 %dynamic-slice_bitcast_fusion.2 = (f32[512,512]{1,0:T(8,128)}, f32[512,512]{1,0:T(8,128)}, f32[512,512]{1,0:T(8,128)S(1)}) fusion(f32[4,512,512]{2,1,0:T(8,128)} %bitcast.31, s32[]{:T(128)S(6)} %select_n.172, s32[]{:T(128)S(6)} %select_n.176, s32[]{:T(128)S(6)} %select_n.174), kind=kLoop, calls=%fused_computation.48 | loop fusion | bytes 6291468 | tf_op jit(solution)/shard_map/squeeze | solution.py:79
  166.9 3.4 %collective-permute-start.11 = (f32[16,2050]{1,0:T(8,128)S(1)}, f32[16,2050]{1,0:T(8,128)S(1)}, u32[]{:S(2)}, u32[]{:S(2)}) collective-permute-start(f32[16,2050]{1,0:T(8,128)S(1)} %select_add_fusion.3), channel_id=1, source_target_pairs={{0,16},{1,17},{2,18},{3,19},{4,20},{5,21},{6,22},{7,23},{8,24},{9,... | collective-permute-start | bytes 393608 | tf_op jit(solution)/shard_map/ppermute | solution.py:62
  170.3 2.7 %collective-permute-done.11 = f32[16,2050]{1,0:T(8,128)S(1)} collective-permute-done((f32[16,2050]{1,0:T(8,128)S(1)}, f32[16,2050]{1,0:T(8,128)S(1)}, u32[]{:S(2)}, u32[]{:S(2)}) %collective-permute-start.11) | collective-permute-done | bytes 131232 | tf_op jit(solution)/shard_map/ppermute | solution.py:62
  173.1 4.3 %collective-permute-start.12 = (f32[16,2050]{1,0:T(8,128)S(1)}, f32[16,2050]{1,0:T(8,128)S(1)}, u32[]{:S(2)}, u32[]{:S(2)}) collective-permute-start(f32[16,2050]{1,0:T(8,128)S(1)} %add.183), channel_id=1, source_target_pairs={{0,128},{1,129},{2,130},{3,131},{4,132},{5,133},{6,134},{7,135},{8... | collective-permute-start | bytes 393608 | tf_op jit(solution)/shard_map/ppermute | solution.py:62
  177.4 2.4 collective-permute-done.12
  179.9 2.2 collective-permute-start.13
  182.1 30.7 %collective-permute-done.13 = f32[16,2050]{1,0:T(8,128)S(1)} collective-permute-done((f32[16,2050]{1,0:T(8,128)S(1)}, f32[16,2050]{1,0:T(8,128)S(1)}, u32[]{:S(2)}, u32[]{:S(2)}) %collective-permute-start.13) | collective-permute-done | bytes 131232 | tf_op jit(solution)/shard_map/ppermute | solution.py:62
  214.2 3.3 %fusion.35 = f32[512,512]{1,0:T(8,128)} fusion(f32[512,512]{1,0:T(8,128)} %collective-permute-done.17, f32[512,512]{1,0:T(8,128)} %collective-permute-done.16, f32[512,512]{1,0:T(8,128)S(1)} %collective-permute-done.15, f32[4,512,512]{2,1,0:T(8,128)} %bitcast.31, s32[]{:T(128)S(6)} %select_n.170), kind=kLoop, calls=%fused_computation.43 | loop fusion | flops 786432 | bytes 5242884 | tf_op jit(solution)/shard_map/add | solution.py:78
  217.5 3.1 %collective-permute-done.14 = f32[16,2050]{1,0:T(8,128)S(1)} collective-permute-done((f32[16,2050]{1,0:T(8,128)S(1)}, f32[16,2050]{1,0:T(8,128)S(1)}, u32[]{:S(2)}, u32[]{:S(2)}) %collective-permute-start.14) | collective-permute-done | bytes 131232 | tf_op jit(solution)/shard_map/ppermute | solution.py:62
  220.9 3.9 %collective-permute-done.18 = f32[16,2050]{1,0:T(8,128)S(1)} collective-permute-done((f32[16,2050]{1,0:T(8,128)S(1)}, f32[16,2050]{1,0:T(8,128)S(1)}, u32[]{:S(2)}, u32[]{:S(2)}) %collective-permute-start.18) | collective-permute-done | bytes 131232 | tf_op jit(solution)/shard_map/ppermute | solution.py:67
  224.9 5.4 %collective-permute-done.19 = f32[32,2050]{1,0:T(8,128)S(1)} collective-permute-done((f32[32,2050]{1,0:T(8,128)S(1)}, f32[32,2050]{1,0:T(8,128)S(1)}, u32[]{:S(2)}, u32[]{:S(2)}) %collective-permute-start.19) | collective-permute-done | bytes 262432 | tf_op jit(solution)/shard_map/ppermute | solution.py:67
  230.3 3.2 %collective-permute-start.20 = (f32[64,2050]{1,0:T(8,128)S(1)}, f32[64,2050]{1,0:T(8,128)S(1)}, u32[]{:S(2)}, u32[]{:S(2)}) collective-permute-start(f32[64,2050]{1,0:T(8,128)S(1)} %maximum_select_fusion.2), channel_id=1, source_target_pairs={{0,8},{1,9},{2,10},{3,11},{4,12},{5,13},{6,14},{7,15},{8,0},{9,1},... | collective-permute-start | bytes 1574408 | tf_op jit(solution)/shard_map/ppermute | solution.py:67
  233.6 6.9 %collective-permute-done.20 = f32[64,2050]{1,0:T(8,128)S(1)} collective-permute-done((f32[64,2050]{1,0:T(8,128)S(1)}, f32[64,2050]{1,0:T(8,128)S(1)}, u32[]{:S(2)}, u32[]{:S(2)}) %collective-permute-start.20) | collective-permute-done | bytes 524832 | tf_op jit(solution)/shard_map/ppermute | solution.py:67
  241.9 9.2 %collective-permute-start.21 = (f32[128,2050]{0,1:T(8,128)}, f32[128,2050]{0,1:T(8,128)}, u32[]{:S(2)}, u32[]{:S(2)}) collective-permute-start(f32[128,2050]{0,1:T(8,128)} %copy.116), channel_id=1, source_target_pairs={{0,4},{1,5},{2,6},{3,7},{4,0},{5,1},{6,2},{7,3},{8,12},{9,13},{10,... | collective-permute-start | bytes 3148808 | tf_op jit(solution)/shard_map/ppermute | solution.py:67
  (137 shorter events, 65.4 us)
Async XLA Ops:
  0.6 94.5 %copy-start = (bf16[512,512]{1,0:T(8,128)(2,1)S(1)}, bf16[512,512]{1,0:T(8,128)(2,1)}, u32[]{:S(2)}) copy-start(bf16[512,512]{1,0:T(8,128)(2,1)} %param.19) | copy-start | bytes 1572868
  4.0 16.0 %copy-start.16 = (s32[4,12]{1,0:T(4,128)S(1)}, s32[4,12]{1,0:T(4,128)}, u32[]{:S(2)}) copy-start(s32[4,12]{1,0:T(4,128)} %param.17) | copy-start | bytes 580
  6.8 31.2 %all-to-all-start = ((bf16[64,2,2112]{2,1,0:T(2,128)(2,1)}), bf16[64,2,2112]{2,1,0:T(2,128)(2,1)S(1)}, u32[]{:S(2)}, u32[]{:S(2)}) async-start(bf16[64,2,2112]{2,1,0:T(2,128)(2,1)} %reshape.197), calls=%async_computation | async-start | bytes 1114112 | tf_op jit(solution)/shard_map/all_to_all | solution.py:125
  38.7 6.5 %copy-start.17 = (s32[4,12]{1,0:T(4,128)S(1)}, s32[4,12]{1,0:T(4,128)}, u32[]{:S(2)}) copy-start(s32[4,12]{1,0:T(4,128)} %param.16) | copy-start | bytes 580
  38.7 6.5 %copy-start.15 = (bf16[4,12,128,128]{3,2,1,0:T(8,128)(2,1)S(1)}, bf16[4,12,128,128]{3,2,1,0:T(8,128)(2,1)}, u32[]{:S(2)}) copy-start(bf16[4,12,128,128]{3,2,1,0:T(8,128)(2,1)} %param.15) | copy-start | bytes 4718596
  41.5 43.8 %copy-start.8 = (bf16[512,512]{1,0:T(8,128)(2,1)}, bf16[512,512]{1,0:T(8,128)(2,1)S(1)}, u32[]{:S(2)}) copy-start(bf16[512,512]{1,0:T(8,128)(2,1)S(1)} %convolution_convert_fusion) | copy-start | bytes 1572868
  41.5 14.1 %collective-permute-start.2 = (bf16[512,512]{1,0:T(8,128)(2,1)S(1)}, bf16[512,512]{1,0:T(8,128)(2,1)S(1)}, u32[]{:S(2)}, u32[]{:S(2)}) collective-permute-start(bf16[512,512]{1,0:T(8,128)(2,1)S(1)} %convolution_convert_fusion), channel_id=1, source_target_pairs={{0,3},{1,0},{2,1},{3,2},{4,7},{5,4},{6,5},{7,6},{8,11},{9,8},{10,9... | collective-permute-start | bytes 1572872 | tf_op jit(solution)/shard_map/ppermute | solution.py:88
  44.0 14.3 %collective-permute-start.1 = (bf16[512,512]{1,0:T(8,128)(2,1)S(1)}, bf16[512,512]{1,0:T(8,128)(2,1)S(1)}, u32[]{:S(2)}, u32[]{:S(2)}) collective-permute-start(bf16[512,512]{1,0:T(8,128)(2,1)S(1)} %convolution_convert_fusion), channel_id=1, source_target_pairs={{0,2},{1,3},{2,0},{3,1},{4,6},{5,7},{6,4},{7,5},{8,10},{9,11},{10,... | collective-permute-start | bytes 1572872 | tf_op jit(solution)/shard_map/ppermute | solution.py:88
  44.6 26.1 %collective-permute-start = (bf16[512,512]{1,0:T(8,128)(2,1)S(1)}, bf16[512,512]{1,0:T(8,128)(2,1)S(1)}, u32[]{:S(2)}, u32[]{:S(2)}) collective-permute-start(bf16[512,512]{1,0:T(8,128)(2,1)S(1)} %convolution_convert_fusion), channel_id=1, source_target_pairs={{0,1},{1,2},{2,3},{3,0},{4,5},{5,6},{6,7},{7,4},{8,9},{9,10},{10,1... | collective-permute-start | bytes 1572872 | tf_op jit(solution)/shard_map/ppermute | solution.py:88
  74.5 6.3 %copy-start.7 = (bf16[4,12,128,128]{3,2,1,0:T(8,128)(2,1)S(1)}, bf16[4,12,128,128]{3,2,1,0:T(8,128)(2,1)}, u32[]{:S(2)}) copy-start(bf16[4,12,128,128]{3,2,1,0:T(8,128)(2,1)} %get-tuple-element.42) | copy-start | bytes 4718596
  75.6 11.2 %collective-permute-start.3 = (bf16[512,512]{1,0:T(8,128)(2,1)}, bf16[512,512]{1,0:T(8,128)(2,1)}, u32[]{:S(2)}, u32[]{:S(2)}) collective-permute-start(bf16[512,512]{1,0:T(8,128)(2,1)} %get-tuple-element.52), channel_id=1, source_target_pairs={{0,4},{4,8},{8,12},{12,16},{16,20},{20,24},{24,28},{28,32},{32,36}... | collective-permute-start | bytes 1572872 | tf_op jit(solution)/shard_map/ppermute | solution.py:20
  78.4 10.8 %collective-permute-start.4 = (bf16[512,512]{1,0:T(8,128)(2,1)}, bf16[512,512]{1,0:T(8,128)(2,1)}, u32[]{:S(2)}, u32[]{:S(2)}) collective-permute-start(bf16[512,512]{1,0:T(8,128)(2,1)} %get-tuple-element.53), channel_id=1, source_target_pairs={{4,0},{8,4},{12,8},{16,12},{20,16},{24,20},{28,24},{32,28},{36,32}... | collective-permute-start | bytes 1572872 | tf_op jit(solution)/shard_map/ppermute | solution.py:23
  114.2 14.4 %collective-permute-start.6 = (bf16[512,512]{1,0:T(8,128)(2,1)}, bf16[512,512]{1,0:T(8,128)(2,1)S(1)}, u32[]{:S(2)}, u32[]{:S(2)}) collective-permute-start(bf16[512,512]{1,0:T(8,128)(2,1)} %bitcast.29), channel_id=1, source_target_pairs={{0,4},{4,8},{8,12},{12,16},{16,20},{20,24},{24,28},{28,32},{32,36}... | collective-permute-start | bytes 1572872 | tf_op jit(solution)/shard_map/ppermute | solution.py:12
  119.8 13.8 %collective-permute-start.5 = (f32[128,2050]{0,1:T(8,128)}, f32[128,2050]{0,1:T(8,128)}, u32[]{:S(2)}, u32[]{:S(2)}) collective-permute-start(f32[128,2050]{0,1:T(8,128)} %copy.112), channel_id=1, source_target_pairs={{0,4},{1,5},{2,6},{3,7},{4,0},{5,1},{6,2},{7,3},{8,12},{9,13},{10,... | collective-permute-start | bytes 3148808 | tf_op jit(solution)/shard_map/ppermute | solution.py:56
  120.3 10.8 %collective-permute-start.7 = (bf16[512,512]{1,0:T(8,128)(2,1)}, bf16[512,512]{1,0:T(8,128)(2,1)}, u32[]{:S(2)}, u32[]{:S(2)}) collective-permute-start(bf16[512,512]{1,0:T(8,128)(2,1)} %bitcast.94), channel_id=1, source_target_pairs={{4,0},{8,4},{12,8},{16,12},{20,16},{24,20},{28,24},{32,28},{36,32}... | collective-permute-start | bytes 1572872 | tf_op jit(solution)/shard_map/ppermute | solution.py:12
  138.7 13.6 %collective-permute-start.8 = (f32[64,2050]{1,0:T(8,128)S(1)}, f32[64,2050]{1,0:T(8,128)S(1)}, u32[]{:S(2)}, u32[]{:S(2)}) collective-permute-start(f32[64,2050]{1,0:T(8,128)S(1)} %slice_select_fusion.1), channel_id=1, source_target_pairs={{0,8},{1,9},{2,10},{3,11},{4,12},{5,13},{6,14},{7,15},{8,0},{9,1},... | collective-permute-start | bytes 1574408 | tf_op jit(solution)/shard_map/ppermute | solution.py:56
  153.7 6.3 %collective-permute-start.9 = (f32[32,2050]{1,0:T(8,128)S(1)}, f32[32,2050]{1,0:T(8,128)S(1)}, u32[]{:S(2)}, u32[]{:S(2)}) collective-permute-start(f32[32,2050]{1,0:T(8,128)S(1)} %slice_select_fusion.2), channel_id=1, source_target_pairs={{0,64},{1,65},{2,66},{3,67},{4,68},{5,69},{6,70},{7,71},{8,72},{9,... | collective-permute-start | bytes 787208 | tf_op jit(solution)/shard_map/ppermute | solution.py:56
  160.1 6.8 %collective-permute-start.10 = (f32[16,2050]{1,0:T(8,128)S(1)}, f32[16,2050]{1,0:T(8,128)S(1)}, u32[]{:S(2)}, u32[]{:S(2)}) collective-permute-start(f32[16,2050]{1,0:T(8,128)S(1)} %slice_select_fusion.3), channel_id=1, source_target_pairs={{0,1},{1,0},{2,3},{3,2},{4,5},{5,4},{6,7},{7,6},{8,9},{9,8},{10,11... | collective-permute-start | bytes 393608 | tf_op jit(solution)/shard_map/ppermute | solution.py:56
  163.6 50.5 %collective-permute-start.15 = (f32[512,512]{1,0:T(8,128)}, f32[512,512]{1,0:T(8,128)S(1)}, u32[]{:S(2)}, u32[]{:S(2)}) collective-permute-start(f32[512,512]{1,0:T(8,128)} %get-tuple-element.45), channel_id=1, source_target_pairs={{0,1},{1,2},{2,3},{3,0},{4,5},{5,6},{6,7},{7,4},{8,9},{9,10},{10,1... | collective-permute-start | bytes 3145736 | tf_op jit(solution)/shard_map/ppermute | solution.py:78
  165.1 49.1 %collective-permute-start.17 = (f32[512,512]{1,0:T(8,128)}, f32[512,512]{1,0:T(8,128)}, u32[]{:S(2)}, u32[]{:S(2)}) collective-permute-start(f32[512,512]{1,0:T(8,128)} %get-tuple-element.46), channel_id=1, source_target_pairs={{0,3},{1,0},{2,1},{3,2},{4,7},{5,4},{6,5},{7,6},{8,11},{9,8},{10,9... | collective-permute-start | bytes 3145736 | tf_op jit(solution)/shard_map/ppermute | solution.py:78
  166.3 47.9 %collective-permute-start.16 = (f32[512,512]{1,0:T(8,128)S(1)}, f32[512,512]{1,0:T(8,128)}, u32[]{:S(2)}, u32[]{:S(2)}) collective-permute-start(f32[512,512]{1,0:T(8,128)S(1)} %get-tuple-element.47), channel_id=1, source_target_pairs={{0,2},{1,3},{2,0},{3,1},{4,6},{5,7},{6,4},{7,5},{8,10},{9,11},{10,... | collective-permute-start | bytes 3145736 | tf_op jit(solution)/shard_map/ppermute | solution.py:78
  166.9 6.1 %collective-permute-start.11 = (f32[16,2050]{1,0:T(8,128)S(1)}, f32[16,2050]{1,0:T(8,128)S(1)}, u32[]{:S(2)}, u32[]{:S(2)}) collective-permute-start(f32[16,2050]{1,0:T(8,128)S(1)} %select_add_fusion.3), channel_id=1, source_target_pairs={{0,16},{1,17},{2,18},{3,19},{4,20},{5,21},{6,22},{7,23},{8,24},{9,... | collective-permute-start | bytes 393608 | tf_op jit(solution)/shard_map/ppermute | solution.py:62
  173.1 6.8 %collective-permute-start.12 = (f32[16,2050]{1,0:T(8,128)S(1)}, f32[16,2050]{1,0:T(8,128)S(1)}, u32[]{:S(2)}, u32[]{:S(2)}) collective-permute-start(f32[16,2050]{1,0:T(8,128)S(1)} %add.183), channel_id=1, source_target_pairs={{0,128},{1,129},{2,130},{3,131},{4,132},{5,133},{6,134},{7,135},{8... | collective-permute-start | bytes 393608 | tf_op jit(solution)/shard_map/ppermute | solution.py:62
  179.9 32.9 %collective-permute-start.13 = (f32[16,2050]{1,0:T(8,128)S(1)}, f32[16,2050]{1,0:T(8,128)S(1)}, u32[]{:S(2)}, u32[]{:S(2)}) collective-permute-start(f32[16,2050]{1,0:T(8,128)S(1)} %add.184), channel_id=1, source_target_pairs={{0,2},{1,3},{2,0},{3,1},{4,6},{5,7},{6,4},{7,5},{8,10},{9,11},{10,... | collective-permute-start | bytes 393608 | tf_op jit(solution)/shard_map/ppermute | solution.py:62
  212.7 7.9 %collective-permute-start.14 = (f32[16,2050]{1,0:T(8,128)S(1)}, f32[16,2050]{1,0:T(8,128)S(1)}, u32[]{:S(2)}, u32[]{:S(2)}) collective-permute-start(f32[16,2050]{1,0:T(8,128)S(1)} %add.185), channel_id=1, source_target_pairs={{0,32},{1,33},{2,34},{3,35},{4,36},{5,37},{6,38},{7,39},{8,40},{9,... | collective-permute-start | bytes 393608 | tf_op jit(solution)/shard_map/ppermute | solution.py:62
  220.7 4.1 %collective-permute-start.18 = (f32[16,2050]{1,0:T(8,128)S(1)}, f32[16,2050]{1,0:T(8,128)S(1)}, u32[]{:S(2)}, u32[]{:S(2)}) collective-permute-start(f32[16,2050]{1,0:T(8,128)S(1)} %add.186), channel_id=1, source_target_pairs={{0,1},{1,0},{2,3},{3,2},{4,5},{5,4},{6,7},{7,6},{8,9},{9,8},{10,11... | collective-permute-start | bytes 393608 | tf_op jit(solution)/shard_map/ppermute | solution.py:67
  224.8 5.5 %collective-permute-start.19 = (f32[32,2050]{1,0:T(8,128)S(1)}, f32[32,2050]{1,0:T(8,128)S(1)}, u32[]{:S(2)}, u32[]{:S(2)}) collective-permute-start(f32[32,2050]{1,0:T(8,128)S(1)} %maximum_select_fusion.3), channel_id=1, source_target_pairs={{0,64},{1,65},{2,66},{3,67},{4,68},{5,69},{6,70},{7,71},{8,72},{9,... | collective-permute-start | bytes 787208 | tf_op jit(solution)/shard_map/ppermute | solution.py:67
  230.3 20.7 %copy-start.13 = (bf16[512,512]{1,0:T(8,128)(2,1)S(1)}, bf16[512,512]{1,0:T(8,128)(2,1)}, u32[]{:S(2)}) copy-start(bf16[512,512]{1,0:T(8,128)(2,1)} %param.18) | copy-start | bytes 1572868
  230.3 10.1 %collective-permute-start.20 = (f32[64,2050]{1,0:T(8,128)S(1)}, f32[64,2050]{1,0:T(8,128)S(1)}, u32[]{:S(2)}, u32[]{:S(2)}) collective-permute-start(f32[64,2050]{1,0:T(8,128)S(1)} %maximum_select_fusion.2), channel_id=1, source_target_pairs={{0,8},{1,9},{2,10},{3,11},{4,12},{5,13},{6,14},{7,15},{8,0},{9,1},... | collective-permute-start | bytes 1574408 | tf_op jit(solution)/shard_map/ppermute | solution.py:67
  241.9 9.6 %copy-start.10 = (f32[512,512]{1,0:T(8,128)S(1)}, f32[512,512]{1,0:T(8,128)}, u32[]{:S(2)}) copy-start(f32[512,512]{1,0:T(8,128)} %fusion.35) | copy-start | bytes 3145732
  241.9 11.8 %collective-permute-start.21 = (f32[128,2050]{0,1:T(8,128)}, f32[128,2050]{0,1:T(8,128)}, u32[]{:S(2)}, u32[]{:S(2)}) collective-permute-start(f32[128,2050]{0,1:T(8,128)} %copy.116), channel_id=1, source_target_pairs={{0,4},{1,5},{2,6},{3,7},{4,0},{5,1},{6,2},{7,3},{8,12},{9,13},{10,... | collective-permute-start | bytes 3148808 | tf_op jit(solution)/shard_map/ppermute | solution.py:67
  255.4 3.5 %copy-start.1 = (bf16[512,512]{1,0:T(8,128)(2,1)S(1)}, bf16[512,512]{1,0:T(8,128)(2,1)}, u32[]{:S(2)}) copy-start(bf16[512,512]{1,0:T(8,128)(2,1)} %param.19) | copy-start | bytes 1572868
  (11 other events, 20.2 us)

commit v4 on v1

--- a/solution.py
+++ b/solution.py
@@ -141,7 +141,7 @@
         jnp.concatenate(
             [
                 jnp.concatenate([contract_rows(features, dz), contract_rows(agg, dz)]).reshape(256, lanes),
-                jnp.sum(dz, axis=0, dtype=jnp.float32).reshape(256, -1),
+                jnp.pad(jnp.sum(dz, axis=0, dtype=jnp.float32).reshape(256, -1), ((0, 0), (0, 126))),
             ],
             axis=1,
         ),
@@ -149,7 +149,7 @@
     )
     grads = packed[:, :lanes].reshape(2 * width, width)
     grad_self, grad_neigh = grads[:width], grads[width:]
-    grad_bias = packed[:, lanes:].reshape(width)
+    grad_bias = packed[:, lanes : lanes + 2].reshape(width)
     scaled = (contract_cols(dz, w_neigh) / degree.reshape(rows, 1)).astype(jnp.bfloat16)
     scaled_tiles = scaled.reshape(row_tiles, 128, width)
     buffer = jnp.einsum(

time: 248 us -> 232 us (0.935)
  local copies, waits for them, and re-layouts: 34 us -> 20.5 us
  matrix products: 26.3 us -> 23.1 us
  starting transfers between devices: 53.7 us -> 56.9 us
    ppermute x4, waiting for transfers between devices: 23.8 us -> 8.14 us  [halving_sum(): block = kept + lax.ppermute(sent, axes, pairs)]
    ppermute x2, waiting for transfers between devices: 0.01 us -> 10.8 us  [shifted(): lax.ppermute(value, axis, [(source, source + steps) for source in range(f...]
    ppermute x4, waiting for transfers between devices: 14.4 us -> 19.5 us  [halving_sum(): got = lax.ppermute(block, axes, pairs)]
    ppermute x2 -> x0, local copies, waits for them, and re-layouts: 4.22 us -> none  [the longest x1 2.63 us: halving_sum(): block = kept + lax.ppermute(sent, axes, pairs)]
    select_n x2 -> x0, local copies, waits for them, and re-layouts: 2.99 us -> none  [the longest x1 2.66 us: halving_sum(): sent = jnp.where(upper, block[:half], block[half:])]
    unnamed x48 -> x43, local copies, waits for them, and re-layouts: 7.39 us -> 4.9 us
  transfers between devices with their start and end apart: 21 -> 21, of which waited for: 15 -> 16; matrix products, arithmetic and copies ran while one was open for 15% -> 11% of each run, Pallas kernels for 0% -> 0%
where the time goes in v4:
time: 232 us; the launch traced here: 231 us
  waiting for transfers between devices  101 us (44%)
  starting transfers between devices  56.9 us (25%)
  matrix products  23.1 us (10%)
  local copies, waits for them, and re-layouts  20.5 us (9%)
  other arithmetic  15.3 us (7%)
  between operations  14.6 us (6%)
    ppermute x3, waiting for transfers between devices, gather_rep(): lax.ppermute(block, 'rep', [(i, (i + shift) % count) for i in range(count)])  23.8 us
    ppermute x4, waiting for transfers between devices, halving_sum(): got = lax.ppermute(block, axes, pairs)  19.5 us
    all_to_all x1, waiting for transfers between devices, shards(): got = lax.all_to_all(sent, 'dom', split_axis=0, concat_axis=0, tiled=True)  17.9 us
    ppermute x4, waiting for transfers between devices, halving_sum(): lax.ppermute(block, axes, [(i, i ^ 1 << bit) for i in range(count)])  17.9 us
    ppermute x4, starting transfers between devices, halving_sum(): got = lax.ppermute(block, axes, pairs)  17.1 us
    all_to_all x1, starting transfers between devices, shards(): got = lax.all_to_all(sent, 'dom', split_axis=0, concat_axis=0, tiled=True)  13.2 us
    ppermute x2, waiting for transfers between devices, shifted(): lax.ppermute(value, axis, [(source, source + steps) for source in range(f...  10.8 us
    ppermute x4, starting transfers between devices, halving_sum(): lax.ppermute(block, axes, [(i, i ^ 1 << bit) for i in range(count)])  10.1 us
  transfers between devices with their start and end apart: 21, of which 16 were waited for; matrix products, arithmetic and copies ran while one was open for 11% of the time, Pallas kernels for 0%

profile of v4, /device:TPU:1, one launch (start us, length us, event | category | flops | bytes accessed | tf_op | source)
XLA Modules:
  0.0 230.9 jit_solution(18273033618853649990)
XLA Ops:
  13.3 13.2 %all-to-all-start = ((bf16[64,2,2112]{2,1,0:T(2,128)(2,1)}), bf16[64,2,2112]{2,1,0:T(2,128)(2,1)S(1)}, u32[]{:S(2)}, u32[]{:S(2)}) async-start(bf16[64,2,2112]{2,1,0:T(2,128)(2,1)} %reshape.193), calls=%async_computation | async-start | bytes 1114112 | tf_op jit(solution)/shard_map/all_to_all | solution.py:109
  26.6 17.9 %all-to-all-done = bf16[64,2,2112]{2,1,0:T(2,128)(2,1)S(1)} async-done(((bf16[64,2,2112]{2,1,0:T(2,128)(2,1)}), bf16[64,2,2112]{2,1,0:T(2,128)(2,1)S(1)}, u32[]{:S(2)}, u32[]{:S(2)}) %all-to-all-start) | async-done | bytes 540704 | tf_op jit(solution)/shard_map/all_to_all | solution.py:109
  46.2 2.6 %collective-permute-start.2 = (bf16[512,512]{1,0:T(8,128)(2,1)S(1)}, bf16[512,512]{1,0:T(8,128)(2,1)S(1)}, u32[]{:S(2)}, u32[]{:S(2)}) collective-permute-start(bf16[512,512]{1,0:T(8,128)(2,1)S(1)} %convolution_convert_fusion), channel_id=1, source_target_pairs={{0,3},{1,0},{2,1},{3,2},{4,7},{5,4},{6,5},{7,6},{8,11},{9,8},{10,9... | collective-permute-start | bytes 1572872 | tf_op jit(solution)/shard_map/ppermute | solution.py:72
  51.6 19.2 %collective-permute-done.2 = bf16[512,512]{1,0:T(8,128)(2,1)S(1)} collective-permute-done((bf16[512,512]{1,0:T(8,128)(2,1)S(1)}, bf16[512,512]{1,0:T(8,128)(2,1)S(1)}, u32[]{:S(2)}, u32[]{:S(2)}) %collective-permute-start.2) | collective-permute-done | bytes 524320 | tf_op jit(solution)/shard_map/ppermute | solution.py:72
  70.8 4.6 %collective-permute-done = bf16[512,512]{1,0:T(8,128)(2,1)S(1)} collective-permute-done((bf16[512,512]{1,0:T(8,128)(2,1)S(1)}, bf16[512,512]{1,0:T(8,128)(2,1)S(1)}, u32[]{:S(2)}, u32[]{:S(2)}) %collective-permute-start) | collective-permute-done | bytes 524320 | tf_op jit(solution)/shard_map/ppermute | solution.py:72
  77.0 2.3 gather_fusion
  80.3 2.8 %collective-permute-start.3 = (bf16[512,512]{1,0:T(8,128)(2,1)}, bf16[512,512]{1,0:T(8,128)(2,1)}, u32[]{:S(2)}, u32[]{:S(2)}) collective-permute-start(bf16[512,512]{1,0:T(8,128)(2,1)} %get-tuple-element.41), channel_id=1, source_target_pairs={{0,4},{4,8},{8,12},{12,16},{16,20},{20,24},{24,28},{28,32},{32,36}... | collective-permute-start | bytes 1572872 | tf_op jit(solution)/shard_map/ppermute | solution.py:20
  83.1 2.4 %collective-permute-start.4 = (bf16[512,512]{1,0:T(8,128)(2,1)}, bf16[512,512]{1,0:T(8,128)(2,1)}, u32[]{:S(2)}, u32[]{:S(2)}) collective-permute-start(bf16[512,512]{1,0:T(8,128)(2,1)} %get-tuple-element.42), channel_id=1, source_target_pairs={{4,0},{8,4},{12,8},{16,12},{20,16},{24,20},{28,24},{32,28},{36,32}... | collective-permute-start | bytes 1572872 | tf_op jit(solution)/shard_map/ppermute | solution.py:23
  85.6 4.4 %subtract_convert_fusion = (bf16[4,24,128,128]{3,1,2,0:T(8,128)(2,1)}, bf16[4,24,128,128]{3,1,2,0:T(8,128)(2,1)}) fusion(bf16[4,12,128,128]{3,2,1,0:T(8,128)(2,1)S(1)} %copy-done.6, s32[4,12]{1,0:T(4,128)S(1)} %broadcast_subtract_fusion), kind=kOutput, calls=%fused_computation.2 | convolution fusion | flops 44041344 | bytes 7864512 | tf_op jit(solution)/shard_map/tke,tkab->teab/dot_general | solution.py:123
  91.4 2.5 %collective-permute-done.4 = bf16[512,512]{1,0:T(8,128)(2,1)} collective-permute-done((bf16[512,512]{1,0:T(8,128)(2,1)}, bf16[512,512]{1,0:T(8,128)(2,1)}, u32[]{:S(2)}, u32[]{:S(2)}) %collective-permute-start.4) | collective-permute-done | bytes 524320 | tf_op jit(solution)/shard_map/ppermute | solution.py:23
  116.3 2.4 %slice.177 = f32[16,128,512]{2,1,0:T(8,128)} slice(f32[24,128,512]{2,1,0:T(8,128)S(1)} %get-tuple-element.50), slice={[4:20], [0:128], [0:512]} | slice | bytes 8388608 | tf_op jit(solution)/shard_map/slice | solution.py:161
  120.7 2.7 %collective-permute-start.6 = (bf16[512,512]{1,0:T(8,128)(2,1)S(1)}, bf16[512,512]{1,0:T(8,128)(2,1)S(1)}, u32[]{:S(2)}, u32[]{:S(2)}) collective-permute-start(bf16[512,512]{1,0:T(8,128)(2,1)S(1)} %bitcast.81), channel_id=1, source_target_pairs={{4,0},{8,4},{12,8},{16,12},{20,16},{24,20},{28,24},{32,28},{36,32}... | collective-permute-start | bytes 1572872 | tf_op jit(solution)/shard_map/ppermute | solution.py:12
  124.4 3.1 %collective-permute-done.5 = bf16[512,512]{1,0:T(8,128)(2,1)S(1)} collective-permute-done((bf16[512,512]{1,0:T(8,128)(2,1)S(1)}, bf16[512,512]{1,0:T(8,128)(2,1)S(1)}, u32[]{:S(2)}, u32[]{:S(2)}) %collective-permute-start.5) | collective-permute-done | bytes 524320 | tf_op jit(solution)/shard_map/ppermute | solution.py:12
  128.7 7.7 %collective-permute-done.6 = bf16[512,512]{1,0:T(8,128)(2,1)S(1)} collective-permute-done((bf16[512,512]{1,0:T(8,128)(2,1)S(1)}, bf16[512,512]{1,0:T(8,128)(2,1)S(1)}, u32[]{:S(2)}, u32[]{:S(2)}) %collective-permute-start.6) | collective-permute-done | bytes 524320 | tf_op jit(solution)/shard_map/ppermute | solution.py:12
  136.3 2.4 %fusion.33 = f32[2048,512]{1,0:T(8,128)} fusion(f32[2048,512]{1,0:T(8,128)} %constant_dynamic-update-slice_fusion, bf16[512,512]{1,0:T(8,128)(2,1)S(1)} %collective-permute-done.6), kind=kLoop, calls=%fused_computation.42 | loop fusion | flops 524288 | bytes 2621440 | tf_op jit(solution)/shard_map/scatter-add | solution.py:163
  140.8 3.9 %collective-permute-done.9 = f32[32,2176]{1,0:T(8,128)S(1)} collective-permute-done((f32[32,2176]{1,0:T(8,128)S(1)}, f32[32,2176]{1,0:T(8,128)S(1)}, u32[]{:S(2)}, u32[]{:S(2)}) %collective-permute-start.9) | collective-permute-done | bytes 278560 | tf_op jit(solution)/shard_map/ppermute | solution.py:56
  144.9 4.2 %collective-permute-done.10 = f32[16,2176]{1,0:T(8,128)S(1)} collective-permute-done((f32[16,2176]{1,0:T(8,128)S(1)}, f32[16,2176]{1,0:T(8,128)S(1)}, u32[]{:S(2)}, u32[]{:S(2)}) %collective-permute-start.10) | collective-permute-done | bytes 139296 | tf_op jit(solution)/shard_map/ppermute | solution.py:56
  149.1 2.5 %collective-permute-start.11 = (f32[16,2176]{1,0:T(8,128)S(1)}, f32[16,2176]{1,0:T(8,128)S(1)}, u32[]{:S(2)}, u32[]{:S(2)}) collective-permute-start(f32[16,2176]{1,0:T(8,128)S(1)} %select_add_fusion.3), channel_id=1, source_target_pairs={{0,16},{1,17},{2,18},{3,19},{4,20},{5,21},{6,22},{7,23},{8,24},{9,... | collective-permute-start | bytes 417800 | tf_op jit(solution)/shard_map/ppermute | solution.py:59
  151.6 2.9 %collective-permute-done.11 = f32[16,2176]{1,0:T(8,128)S(1)} collective-permute-done((f32[16,2176]{1,0:T(8,128)S(1)}, f32[16,2176]{1,0:T(8,128)S(1)}, u32[]{:S(2)}, u32[]{:S(2)}) %collective-permute-start.11) | collective-permute-done | bytes 139296 | tf_op jit(solution)/shard_map/ppermute | solution.py:59
  154.5 3.6 %collective-permute-start.12 = (f32[16,2176]{1,0:T(8,128)S(1)}, f32[16,2176]{1,0:T(8,128)S(1)}, u32[]{:S(2)}, u32[]{:S(2)}) collective-permute-start(f32[16,2176]{1,0:T(8,128)S(1)} %add.148), channel_id=1, source_target_pairs={{0,128},{1,129},{2,130},{3,131},{4,132},{5,133},{6,134},{7,135},{8... | collective-permute-start | bytes 417800 | tf_op jit(solution)/shard_map/ppermute | solution.py:59
  158.1 2.5 %collective-permute-done.12 = f32[16,2176]{1,0:T(8,128)S(1)} collective-permute-done((f32[16,2176]{1,0:T(8,128)S(1)}, f32[16,2176]{1,0:T(8,128)S(1)}, u32[]{:S(2)}, u32[]{:S(2)}) %collective-permute-start.12) | collective-permute-done | bytes 139296 | tf_op jit(solution)/shard_map/ppermute | solution.py:59
  160.8 8.4 %collective-permute-done.13 = f32[16,2176]{1,0:T(8,128)S(1)} collective-permute-done((f32[16,2176]{1,0:T(8,128)S(1)}, f32[16,2176]{1,0:T(8,128)S(1)}, u32[]{:S(2)}, u32[]{:S(2)}) %collective-permute-start.13) | collective-permute-done | bytes 139296 | tf_op jit(solution)/shard_map/ppermute | solution.py:59
  169.3 3.8 %collective-permute-start.14 = (f32[16,2176]{1,0:T(8,128)S(1)}, f32[16,2176]{1,0:T(8,128)S(1)}, u32[]{:S(2)}, u32[]{:S(2)}) collective-permute-start(f32[16,2176]{1,0:T(8,128)S(1)} %add.150), channel_id=1, source_target_pairs={{0,32},{1,33},{2,34},{3,35},{4,36},{5,37},{6,38},{7,39},{8,40},{9,... | collective-permute-start | bytes 417800 | tf_op jit(solution)/shard_map/ppermute | solution.py:59
  173.1 4.2 %collective-permute-done.14 = f32[16,2176]{1,0:T(8,128)S(1)} collective-permute-done((f32[16,2176]{1,0:T(8,128)S(1)}, f32[16,2176]{1,0:T(8,128)S(1)}, u32[]{:S(2)}, u32[]{:S(2)}) %collective-permute-start.14) | collective-permute-done | bytes 139296 | tf_op jit(solution)/shard_map/ppermute | solution.py:59
  177.4 7.4 %collective-permute-done.15 = f32[16,2176]{1,0:T(8,128)S(1)} collective-permute-done((f32[16,2176]{1,0:T(8,128)S(1)}, f32[16,2176]{1,0:T(8,128)S(1)}, u32[]{:S(2)}, u32[]{:S(2)}) %collective-permute-start.15) | collective-permute-done | bytes 139296 | tf_op jit(solution)/shard_map/ppermute | solution.py:63
  184.8 2.7 %collective-permute-start.16 = (f32[32,2176]{1,0:T(8,128)S(1)}, f32[32,2176]{1,0:T(8,128)S(1)}, u32[]{:S(2)}, u32[]{:S(2)}) collective-permute-start(f32[32,2176]{1,0:T(8,128)S(1)} %maximum_select_fusion.3), channel_id=1, source_target_pairs={{0,64},{1,65},{2,66},{3,67},{4,68},{5,69},{6,70},{7,71},{8,72},{9,... | collective-permute-start | bytes 835592 | tf_op jit(solution)/shard_map/ppermute | solution.py:63
  187.6 3.9 %collective-permute-done.16 = f32[32,2176]{1,0:T(8,128)S(1)} collective-permute-done((f32[32,2176]{1,0:T(8,128)S(1)}, f32[32,2176]{1,0:T(8,128)S(1)}, u32[]{:S(2)}, u32[]{:S(2)}) %collective-permute-start.16) | collective-permute-done | bytes 278560 | tf_op jit(solution)/shard_map/ppermute | solution.py:63
  191.5 3.0 %collective-permute-start.17 = (f32[64,2176]{1,0:T(8,128)S(1)}, f32[64,2176]{1,0:T(8,128)S(1)}, u32[]{:S(2)}, u32[]{:S(2)}) collective-permute-start(f32[64,2176]{1,0:T(8,128)S(1)} %maximum_select_fusion.2), channel_id=1, source_target_pairs={{0,8},{1,9},{2,10},{3,11},{4,12},{5,13},{6,14},{7,15},{8,0},{9,1},... | collective-permute-start | bytes 1671176 | tf_op jit(solution)/shard_map/ppermute | solution.py:63
  194.6 7.2 %collective-permute-done.17 = f32[64,2176]{1,0:T(8,128)S(1)} collective-permute-done((f32[64,2176]{1,0:T(8,128)S(1)}, f32[64,2176]{1,0:T(8,128)S(1)}, u32[]{:S(2)}, u32[]{:S(2)}) %collective-permute-start.17) | collective-permute-done | bytes 557088 | tf_op jit(solution)/shard_map/ppermute | solution.py:63
  201.9 11.2 %collective-permute-start.18 = (f32[128,2176]{1,0:T(8,128)S(1)}, f32[128,2176]{1,0:T(8,128)S(1)}, u32[]{:S(2)}, u32[]{:S(2)}) collective-permute-start(f32[128,2176]{1,0:T(8,128)S(1)} %maximum_select_fusion.1), channel_id=1, source_target_pairs={{0,4},{1,5},{2,6},{3,7},{4,0},{5,1},{6,2},{7,3},{8,12},{9,13},{10,... | collective-permute-start | bytes 3342344 | tf_op jit(solution)/shard_map/ppermute | solution.py:63
  217.9 2.6 %slice.165 = f32[512,512]{1,0:T(8,128)} reshape(f32[128,2048]{1,0:T(8,128)} %get-tuple-element.39) | data formatting | bytes 2097152 | tf_op jit(solution)/shard_map/slice | solution.py:151
  221.8 2.2 add_convert_fusion
  (127 shorter events, 50.0 us)
Async XLA Ops:
  7.2 92.7 %copy-start = (bf16[512,512]{1,0:T(8,128)(2,1)S(1)}, bf16[512,512]{1,0:T(8,128)(2,1)}, u32[]{:S(2)}) copy-start(bf16[512,512]{1,0:T(8,128)(2,1)} %param.19) | copy-start | bytes 1572868
  10.5 16.0 %copy-start.16 = (s32[4,12]{1,0:T(4,128)S(1)}, s32[4,12]{1,0:T(4,128)}, u32[]{:S(2)}) copy-start(s32[4,12]{1,0:T(4,128)} %param.17) | copy-start | bytes 580
  13.3 31.2 %all-to-all-start = ((bf16[64,2,2112]{2,1,0:T(2,128)(2,1)}), bf16[64,2,2112]{2,1,0:T(2,128)(2,1)S(1)}, u32[]{:S(2)}, u32[]{:S(2)}) async-start(bf16[64,2,2112]{2,1,0:T(2,128)(2,1)} %reshape.193), calls=%async_computation | async-start | bytes 1114112 | tf_op jit(solution)/shard_map/all_to_all | solution.py:109
  26.5 195.3 %reduce-scatter.2.cloned.1.call-start = ((), (), s32[]{:S(2)}) async-start(), calls=%async_computation.2 | async-start | bytes 5242880 | tf_op jit(solution)/shard_map/reduce_scatter | solution.py:164
  45.2 4.7 %copy-start.17 = (s32[4,12]{1,0:T(4,128)S(1)}, s32[4,12]{1,0:T(4,128)}, u32[]{:S(2)}) copy-start(s32[4,12]{1,0:T(4,128)} %param.16) | copy-start | bytes 580
  45.2 4.6 %copy-start.15 = (bf16[4,12,128,128]{3,2,1,0:T(8,128)(2,1)S(1)}, bf16[4,12,128,128]{3,2,1,0:T(8,128)(2,1)}, u32[]{:S(2)}) copy-start(bf16[4,12,128,128]{3,2,1,0:T(8,128)(2,1)} %param.15) | copy-start | bytes 4718596
  46.2 43.8 %copy-start.7 = (bf16[512,512]{1,0:T(8,128)(2,1)}, bf16[512,512]{1,0:T(8,128)(2,1)S(1)}, u32[]{:S(2)}) copy-start(bf16[512,512]{1,0:T(8,128)(2,1)S(1)} %convolution_convert_fusion) | copy-start | bytes 1572868
  46.2 24.5 %collective-permute-start.2 = (bf16[512,512]{1,0:T(8,128)(2,1)S(1)}, bf16[512,512]{1,0:T(8,128)(2,1)S(1)}, u32[]{:S(2)}, u32[]{:S(2)}) collective-permute-start(bf16[512,512]{1,0:T(8,128)(2,1)S(1)} %convolution_convert_fusion), channel_id=1, source_target_pairs={{0,3},{1,0},{2,1},{3,2},{4,7},{5,4},{6,5},{7,6},{8,11},{9,8},{10,9... | collective-permute-start | bytes 1572872 | tf_op jit(solution)/shard_map/ppermute | solution.py:72
  48.8 22.0 %collective-permute-start.1 = (bf16[512,512]{1,0:T(8,128)(2,1)S(1)}, bf16[512,512]{1,0:T(8,128)(2,1)S(1)}, u32[]{:S(2)}, u32[]{:S(2)}) collective-permute-start(bf16[512,512]{1,0:T(8,128)(2,1)S(1)} %convolution_convert_fusion), channel_id=1, source_target_pairs={{0,2},{1,3},{2,0},{3,1},{4,6},{5,7},{6,4},{7,5},{8,10},{9,11},{10,... | collective-permute-start | bytes 1572872 | tf_op jit(solution)/shard_map/ppermute | solution.py:72
  49.3 26.1 %collective-permute-start = (bf16[512,512]{1,0:T(8,128)(2,1)S(1)}, bf16[512,512]{1,0:T(8,128)(2,1)S(1)}, u32[]{:S(2)}, u32[]{:S(2)}) collective-permute-start(bf16[512,512]{1,0:T(8,128)(2,1)S(1)} %convolution_convert_fusion), channel_id=1, source_target_pairs={{0,1},{1,2},{2,3},{3,0},{4,5},{5,6},{6,7},{7,4},{8,9},{9,10},{10,1... | collective-permute-start | bytes 1572872 | tf_op jit(solution)/shard_map/ppermute | solution.py:72
  79.2 6.3 %copy-start.6 = (bf16[4,12,128,128]{3,2,1,0:T(8,128)(2,1)S(1)}, bf16[4,12,128,128]{3,2,1,0:T(8,128)(2,1)}, u32[]{:S(2)}) copy-start(bf16[4,12,128,128]{3,2,1,0:T(8,128)(2,1)} %get-tuple-element.34) | copy-start | bytes 4718596
  80.3 11.2 %collective-permute-start.3 = (bf16[512,512]{1,0:T(8,128)(2,1)}, bf16[512,512]{1,0:T(8,128)(2,1)}, u32[]{:S(2)}, u32[]{:S(2)}) collective-permute-start(bf16[512,512]{1,0:T(8,128)(2,1)} %get-tuple-element.41), channel_id=1, source_target_pairs={{0,4},{4,8},{8,12},{12,16},{16,20},{20,24},{24,28},{28,32},{32,36}... | collective-permute-start | bytes 1572872 | tf_op jit(solution)/shard_map/ppermute | solution.py:20
  83.1 10.8 %collective-permute-start.4 = (bf16[512,512]{1,0:T(8,128)(2,1)}, bf16[512,512]{1,0:T(8,128)(2,1)}, u32[]{:S(2)}, u32[]{:S(2)}) collective-permute-start(bf16[512,512]{1,0:T(8,128)(2,1)} %get-tuple-element.42), channel_id=1, source_target_pairs={{4,0},{8,4},{12,8},{16,12},{20,16},{24,20},{28,24},{32,28},{36,32}... | collective-permute-start | bytes 1572872 | tf_op jit(solution)/shard_map/ppermute | solution.py:23
  93.9 2.2 copy-start.2
  110.5 12.8 %collective-permute-start.7 = (f32[128,2176]{1,0:T(8,128)S(1)}, f32[128,2176]{1,0:T(8,128)S(1)}, u32[]{:S(2)}, u32[]{:S(2)}) collective-permute-start(f32[128,2176]{1,0:T(8,128)S(1)} %slice_select_fusion), channel_id=1, source_target_pairs={{0,4},{1,5},{2,6},{3,7},{4,0},{5,1},{6,2},{7,3},{8,12},{9,13},{10,... | collective-permute-start | bytes 3342344 | tf_op jit(solution)/shard_map/ppermute | solution.py:56
  118.8 8.8 %collective-permute-start.5 = (bf16[512,512]{1,0:T(8,128)(2,1)S(1)}, bf16[512,512]{1,0:T(8,128)(2,1)S(1)}, u32[]{:S(2)}, u32[]{:S(2)}) collective-permute-start(bf16[512,512]{1,0:T(8,128)(2,1)S(1)} %bitcast.82), channel_id=1, source_target_pairs={{0,4},{4,8},{8,12},{12,16},{16,20},{20,24},{24,28},{28,32},{32,36}... | collective-permute-start | bytes 1572872 | tf_op jit(solution)/shard_map/ppermute | solution.py:12
  120.7 15.7 %collective-permute-start.6 = (bf16[512,512]{1,0:T(8,128)(2,1)S(1)}, bf16[512,512]{1,0:T(8,128)(2,1)S(1)}, u32[]{:S(2)}, u32[]{:S(2)}) collective-permute-start(bf16[512,512]{1,0:T(8,128)(2,1)S(1)} %bitcast.81), channel_id=1, source_target_pairs={{4,0},{8,4},{12,8},{16,12},{20,16},{24,20},{28,24},{32,28},{36,32}... | collective-permute-start | bytes 1572872 | tf_op jit(solution)/shard_map/ppermute | solution.py:12
  123.6 15.1 %collective-permute-start.8 = (f32[64,2176]{1,0:T(8,128)S(1)}, f32[64,2176]{1,0:T(8,128)S(1)}, u32[]{:S(2)}, u32[]{:S(2)}) collective-permute-start(f32[64,2176]{1,0:T(8,128)S(1)} %slice_select_fusion.1), channel_id=1, source_target_pairs={{0,8},{1,9},{2,10},{3,11},{4,12},{5,13},{6,14},{7,15},{8,0},{9,1},... | collective-permute-start | bytes 1671176 | tf_op jit(solution)/shard_map/ppermute | solution.py:56
  138.9 5.9 %collective-permute-start.9 = (f32[32,2176]{1,0:T(8,128)S(1)}, f32[32,2176]{1,0:T(8,128)S(1)}, u32[]{:S(2)}, u32[]{:S(2)}) collective-permute-start(f32[32,2176]{1,0:T(8,128)S(1)} %slice_select_fusion.2), channel_id=1, source_target_pairs={{0,64},{1,65},{2,66},{3,67},{4,68},{5,69},{6,70},{7,71},{8,72},{9,... | collective-permute-start | bytes 835592 | tf_op jit(solution)/shard_map/ppermute | solution.py:56
  144.8 4.3 %collective-permute-start.10 = (f32[16,2176]{1,0:T(8,128)S(1)}, f32[16,2176]{1,0:T(8,128)S(1)}, u32[]{:S(2)}, u32[]{:S(2)}) collective-permute-start(f32[16,2176]{1,0:T(8,128)S(1)} %slice_select_fusion.3), channel_id=1, source_target_pairs={{0,1},{1,0},{2,3},{3,2},{4,5},{5,4},{6,7},{7,6},{8,9},{9,8},{10,11... | collective-permute-start | bytes 417800 | tf_op jit(solution)/shard_map/ppermute | solution.py:56
  149.1 5.3 %collective-permute-start.11 = (f32[16,2176]{1,0:T(8,128)S(1)}, f32[16,2176]{1,0:T(8,128)S(1)}, u32[]{:S(2)}, u32[]{:S(2)}) collective-permute-start(f32[16,2176]{1,0:T(8,128)S(1)} %select_add_fusion.3), channel_id=1, source_target_pairs={{0,16},{1,17},{2,18},{3,19},{4,20},{5,21},{6,22},{7,23},{8,24},{9,... | collective-permute-start | bytes 417800 | tf_op jit(solution)/shard_map/ppermute | solution.py:59
  154.5 6.1 %collective-permute-start.12 = (f32[16,2176]{1,0:T(8,128)S(1)}, f32[16,2176]{1,0:T(8,128)S(1)}, u32[]{:S(2)}, u32[]{:S(2)}) collective-permute-start(f32[16,2176]{1,0:T(8,128)S(1)} %add.148), channel_id=1, source_target_pairs={{0,128},{1,129},{2,130},{3,131},{4,132},{5,133},{6,134},{7,135},{8... | collective-permute-start | bytes 417800 | tf_op jit(solution)/shard_map/ppermute | solution.py:59
  160.6 8.6 %collective-permute-start.13 = (f32[16,2176]{1,0:T(8,128)S(1)}, f32[16,2176]{1,0:T(8,128)S(1)}, u32[]{:S(2)}, u32[]{:S(2)}) collective-permute-start(f32[16,2176]{1,0:T(8,128)S(1)} %add.149), channel_id=1, source_target_pairs={{0,2},{1,3},{2,0},{3,1},{4,6},{5,7},{6,4},{7,5},{8,10},{9,11},{10,... | collective-permute-start | bytes 417800 | tf_op jit(solution)/shard_map/ppermute | solution.py:59
  169.2 43.9 %copy-start.13 = (bf16[512,512]{1,0:T(8,128)(2,1)S(1)}, bf16[512,512]{1,0:T(8,128)(2,1)}, u32[]{:S(2)}) copy-start(bf16[512,512]{1,0:T(8,128)(2,1)} %param.18) | copy-start | bytes 1572868
  169.3 8.0 %collective-permute-start.14 = (f32[16,2176]{1,0:T(8,128)S(1)}, f32[16,2176]{1,0:T(8,128)S(1)}, u32[]{:S(2)}, u32[]{:S(2)}) collective-permute-start(f32[16,2176]{1,0:T(8,128)S(1)} %add.150), channel_id=1, source_target_pairs={{0,32},{1,33},{2,34},{3,35},{4,36},{5,37},{6,38},{7,39},{8,40},{9,... | collective-permute-start | bytes 417800 | tf_op jit(solution)/shard_map/ppermute | solution.py:59
  177.3 7.5 %collective-permute-start.15 = (f32[16,2176]{1,0:T(8,128)S(1)}, f32[16,2176]{1,0:T(8,128)S(1)}, u32[]{:S(2)}, u32[]{:S(2)}) collective-permute-start(f32[16,2176]{1,0:T(8,128)S(1)} %add.151), channel_id=1, source_target_pairs={{0,1},{1,0},{2,3},{3,2},{4,5},{5,4},{6,7},{7,6},{8,9},{9,8},{10,11... | collective-permute-start | bytes 417800 | tf_op jit(solution)/shard_map/ppermute | solution.py:63
  184.8 6.6 %collective-permute-start.16 = (f32[32,2176]{1,0:T(8,128)S(1)}, f32[32,2176]{1,0:T(8,128)S(1)}, u32[]{:S(2)}, u32[]{:S(2)}) collective-permute-start(f32[32,2176]{1,0:T(8,128)S(1)} %maximum_select_fusion.3), channel_id=1, source_target_pairs={{0,64},{1,65},{2,66},{3,67},{4,68},{5,69},{6,70},{7,71},{8,72},{9,... | collective-permute-start | bytes 835592 | tf_op jit(solution)/shard_map/ppermute | solution.py:63
  191.5 10.3 %collective-permute-start.17 = (f32[64,2176]{1,0:T(8,128)S(1)}, f32[64,2176]{1,0:T(8,128)S(1)}, u32[]{:S(2)}, u32[]{:S(2)}) collective-permute-start(f32[64,2176]{1,0:T(8,128)S(1)} %maximum_select_fusion.2), channel_id=1, source_target_pairs={{0,8},{1,9},{2,10},{3,11},{4,12},{5,13},{6,14},{7,15},{8,0},{9,1},... | collective-permute-start | bytes 1671176 | tf_op jit(solution)/shard_map/ppermute | solution.py:63
  201.9 13.6 %collective-permute-start.18 = (f32[128,2176]{1,0:T(8,128)S(1)}, f32[128,2176]{1,0:T(8,128)S(1)}, u32[]{:S(2)}, u32[]{:S(2)}) collective-permute-start(f32[128,2176]{1,0:T(8,128)S(1)} %maximum_select_fusion.1), channel_id=1, source_target_pairs={{0,4},{1,5},{2,6},{3,7},{4,0},{5,1},{6,2},{7,3},{8,12},{9,13},{10,... | collective-permute-start | bytes 3342344 | tf_op jit(solution)/shard_map/ppermute | solution.py:63
  217.9 2.6 %copy-start.12 = (f32[128,2048]{1,0:T(8,128)S(1)}, f32[128,2048]{1,0:T(8,128)}, u32[]{:S(2)}) copy-start(f32[128,2048]{1,0:T(8,128)} %get-tuple-element.40) | copy-start | bytes 3145732
  217.9 3.9 %copy-start.9 = (f32[512,512]{1,0:T(8,128)S(1)}, f32[512,512]{1,0:T(8,128)}, u32[]{:S(2)}) copy-start(f32[512,512]{1,0:T(8,128)} %fusion.62) | copy-start | bytes 3145732
  220.6 3.4 %copy-start.1 = (bf16[512,512]{1,0:T(8,128)(2,1)S(1)}, bf16[512,512]{1,0:T(8,128)(2,1)}, u32[]{:S(2)}) copy-start(bf16[512,512]{1,0:T(8,128)(2,1)} %param.19) | copy-start | bytes 1572868
  (9 other events, 15.8 us)
Sparse Core Ops, SparseCore 0:
  138.8 52.3 reduce-scatter.1

commit v5 on v4

--- a/solution.py
+++ b/solution.py
@@ -41,7 +41,7 @@
 DOUBLING_BITS = (4, 7, 1, 5)
 
 
-def halving_sum(block, axes):
+def halving_sum(block, axes, held, side, at=1):
     count = 1
     for axis in axes:
         count *= lax.axis_size(axis)
@@ -53,7 +53,14 @@
         half = block.shape[0] // 2
         kept = jnp.where(upper, block[half:], block[:half])
         sent = jnp.where(upper, block[:half], block[half:])
-        block = kept + lax.ppermute(sent, axes, pairs)
+        if bit == bits[at]:
+            sent, held = lax.optimization_barrier((sent, held))
+            got = lax.ppermute(sent, axes, pairs)
+            held = side(held)
+            got, held = lax.optimization_barrier((got, held))
+            block = kept + got
+        else:
+            block = kept + lax.ppermute(sent, axes, pairs)
     for bit in DOUBLING_BITS:
         if (1 << bit) < count:
             block = block + lax.ppermute(block, axes, [(i, i ^ (1 << bit)) for i in range(count)])
@@ -62,7 +69,7 @@
         upper = ((place >> bit) & 1) == 1
         got = lax.ppermute(block, axes, pairs)
         block = jnp.where(upper, jnp.concatenate([got, block]), jnp.concatenate([block, got]))
-    return block
+    return block, held
 
 
 def gather_rep(block):
@@ -136,8 +143,22 @@
     layer_out = jnp.where(pre > 0, pre, jnp.expm1(jnp.minimum(pre, 0.0))).astype(jnp.bfloat16)
     slope = jnp.where(pre > 0, 1.0, jnp.exp(jnp.minimum(pre, 0.0)))
     dz = (cotangent.astype(jnp.float32) * slope).astype(jnp.bfloat16)
+    def backward(dz):
+        scaled = (contract_cols(dz, w_neigh) / degree.reshape(rows, 1)).astype(jnp.bfloat16)
+        scaled_tiles = scaled.reshape(row_tiles, 128, width)
+        buffer = jnp.einsum(
+            "teab,taf->ebf", merged_hi, scaled_tiles, preferred_element_type=jnp.float32
+        ) + jnp.einsum("teab,taf->ebf", merged_lo, scaled_tiles, preferred_element_type=jnp.float32)
+        buffer = buffer.reshape(span_tiles * 128, width)
+        lower = buffer[:rim_rows]
+        upper = buffer[rim_rows + part_rows :]
+        core = buffer[rim_rows : rim_rows + part_rows]
+        core = core.at[:rim_rows].add(pass_rim(upper, 1))
+        core = core.at[part_rows - rim_rows :].add(pass_rim(lower, -1))
+        return core
+
     lanes = 2 * width * width // 256
-    packed = halving_sum(
+    packed, core = halving_sum(
         jnp.concatenate(
             [
                 jnp.concatenate([contract_rows(features, dz), contract_rows(agg, dz)]).reshape(256, lanes),
@@ -146,21 +167,12 @@
             axis=1,
         ),
         ("dom", "rep"),
+        dz,
+        backward,
     )
     grads = packed[:, :lanes].reshape(2 * width, width)
     grad_self, grad_neigh = grads[:width], grads[width:]
     grad_bias = packed[:, lanes : lanes + 2].reshape(width)
-    scaled = (contract_cols(dz, w_neigh) / degree.reshape(rows, 1)).astype(jnp.bfloat16)
-    scaled_tiles = scaled.reshape(row_tiles, 128, width)
-    buffer = jnp.einsum(
-        "teab,taf->ebf", merged_hi, scaled_tiles, preferred_element_type=jnp.float32
-    ) + jnp.einsum("teab,taf->ebf", merged_lo, scaled_tiles, preferred_element_type=jnp.float32)
-    buffer = buffer.reshape(span_tiles * 128, width)
-    lower = buffer[:rim_rows]
-    upper = buffer[rim_rows + part_rows :]
-    core = buffer[rim_rows : rim_rows + part_rows]
-    core = core.at[:rim_rows].add(pass_rim(upper, 1))
-    core = core.at[part_rows - rim_rows :].add(pass_rim(lower, -1))
     back = lax.psum_scatter(core, "rep", scatter_dimension=0, tiled=True)
     grad_features = (contract_cols(dz, w_self) + back).astype(jnp.bfloat16)
     return (layer_out, grad_features, grad_self, grad_neigh, grad_bias)

time: 232 us -> 242 us (1.043)
  waiting for transfers between devices: 101 us -> 106 us
  starting transfers between devices: 56.9 us -> 52.2 us
  local copies, waits for them, and re-layouts: 20.5 us -> 24.6 us
  other arithmetic: 15.3 us -> 19 us
    ppermute x2, waiting for transfers between devices: 10.8 us -> 0.01 us  [shifted(): lax.ppermute(value, axis, [(source, source + steps) for source in range(f...]
    ppermute x0 -> x1, waiting for transfers between devices: none -> 9.44 us  [halving_sum(): got = lax.ppermute(sent, axes, pairs)]
    ppermute x4 -> x3, waiting for transfers between devices: 8.14 us -> 14.6 us  [halving_sum(): block = kept + lax.ppermute(sent, axes, pairs)]
    ppermute x4, starting transfers between devices: 17.1 us -> 12.6 us  [halving_sum(): got = lax.ppermute(block, axes, pairs)]
    slice x2, local copies, waits for them, and re-layouts: 2.5 us -> 5.74 us  [the longest x1 4.85 us: backward(): core = buffer[rim_rows:rim_rows + part_rows]]
    ppermute x4 -> x3, starting transfers between devices: 2.95 us -> 0.19 us  [halving_sum(): block = kept + lax.ppermute(sent, axes, pairs)]
    dot_general x2, matrix products: 3.81 us -> 6.53 us  [the longest x1 4.7 us: backward(): jnp.einsum('teab,taf->ebf', merged_hi, scaled_tiles, preferred_element_ty...]
    unnamed x43 -> x41, local copies, waits for them, and re-layouts: 4.9 us -> 4.54 us
where the time goes in v5:
time: 242 us; the launch traced here: 241 us
  waiting for transfers between devices  106 us (44%)
  starting transfers between devices  52.2 us (22%)
  matrix products  25 us (10%)
  local copies, waits for them, and re-layouts  24.6 us (10%)
  other arithmetic  19 us (8%)
  between operations  14.5 us (6%)
    ppermute x3, waiting for transfers between devices, gather_rep(): lax.ppermute(block, 'rep', [(i, (i + shift) % count) for i in range(count)])  23.8 us
    ppermute x4, waiting for transfers between devices, halving_sum(): got = lax.ppermute(block, axes, pairs)  19.5 us
    ppermute x4, waiting for transfers between devices, halving_sum(): lax.ppermute(block, axes, [(i, i ^ 1 << bit) for i in range(count)])  18.1 us
    all_to_all x1, waiting for transfers between devices, shards(): got = lax.all_to_all(sent, 'dom', split_axis=0, concat_axis=0, tiled=True)  17.9 us
    ppermute x3, waiting for transfers between devices, halving_sum(): block = kept + lax.ppermute(sent, axes, pairs)  14.6 us
    all_to_all x1, starting transfers between devices, shards(): got = lax.all_to_all(sent, 'dom', split_axis=0, concat_axis=0, tiled=True)  13.2 us
    ppermute x4, starting transfers between devices, halving_sum(): got = lax.ppermute(block, axes, pairs)  12.6 us
    ppermute x4, starting transfers between devices, halving_sum(): lax.ppermute(block, axes, [(i, i ^ 1 << bit) for i in range(count)])  10.6 us
  transfers between devices with their start and end apart: 21, of which 16 were waited for; matrix products, arithmetic and copies ran while one was open for 11% of the time, Pallas kernels for 0%

profile of v5, /device:TPU:1, one launch (start us, length us, event | category | flops | bytes accessed | tf_op | source)
XLA Modules:
  0.0 241.3 jit_solution(7061289201463573324)
XLA Ops:
  13.3 13.2 %all-to-all-start = ((bf16[64,2,2112]{2,1,0:T(2,128)(2,1)}), bf16[64,2,2112]{2,1,0:T(2,128)(2,1)S(1)}, u32[]{:S(2)}, u32[]{:S(2)}) async-start(bf16[64,2,2112]{2,1,0:T(2,128)(2,1)} %reshape.193), calls=%async_computation | async-start | bytes 1114112 | tf_op jit(solution)/shard_map/all_to_all | solution.py:116
  26.6 17.9 %all-to-all-done = bf16[64,2,2112]{2,1,0:T(2,128)(2,1)S(1)} async-done(((bf16[64,2,2112]{2,1,0:T(2,128)(2,1)}), bf16[64,2,2112]{2,1,0:T(2,128)(2,1)S(1)}, u32[]{:S(2)}, u32[]{:S(2)}) %all-to-all-start) | async-done | bytes 540704 | tf_op jit(solution)/shard_map/all_to_all | solution.py:116
  46.2 2.6 %collective-permute-start.2 = (bf16[512,512]{1,0:T(8,128)(2,1)S(1)}, bf16[512,512]{1,0:T(8,128)(2,1)S(1)}, u32[]{:S(2)}, u32[]{:S(2)}) collective-permute-start(bf16[512,512]{1,0:T(8,128)(2,1)S(1)} %convolution_convert_fusion), channel_id=1, source_target_pairs={{0,3},{1,0},{2,1},{3,2},{4,7},{5,4},{6,5},{7,6},{8,11},{9,8},{10,9... | collective-permute-start | bytes 1572872 | tf_op jit(solution)/shard_map/ppermute | solution.py:79
  51.6 19.2 %collective-permute-done.2 = bf16[512,512]{1,0:T(8,128)(2,1)S(1)} collective-permute-done((bf16[512,512]{1,0:T(8,128)(2,1)S(1)}, bf16[512,512]{1,0:T(8,128)(2,1)S(1)}, u32[]{:S(2)}, u32[]{:S(2)}) %collective-permute-start.2) | collective-permute-done | bytes 524320 | tf_op jit(solution)/shard_map/ppermute | solution.py:79
  70.8 4.6 %collective-permute-done = bf16[512,512]{1,0:T(8,128)(2,1)S(1)} collective-permute-done((bf16[512,512]{1,0:T(8,128)(2,1)S(1)}, bf16[512,512]{1,0:T(8,128)(2,1)S(1)}, u32[]{:S(2)}, u32[]{:S(2)}) %collective-permute-start) | collective-permute-done | bytes 524320 | tf_op jit(solution)/shard_map/ppermute | solution.py:79
  77.0 2.3 gather_fusion
  80.3 2.8 %collective-permute-start.3 = (bf16[512,512]{1,0:T(8,128)(2,1)}, bf16[512,512]{1,0:T(8,128)(2,1)}, u32[]{:S(2)}, u32[]{:S(2)}) collective-permute-start(bf16[512,512]{1,0:T(8,128)(2,1)} %get-tuple-element.49), channel_id=1, source_target_pairs={{0,4},{4,8},{8,12},{12,16},{16,20},{20,24},{24,28},{28,32},{32,36}... | collective-permute-start | bytes 1572872 | tf_op jit(solution)/shard_map/ppermute | solution.py:20
  83.1 2.4 %collective-permute-start.4 = (bf16[512,512]{1,0:T(8,128)(2,1)}, bf16[512,512]{1,0:T(8,128)(2,1)}, u32[]{:S(2)}, u32[]{:S(2)}) collective-permute-start(bf16[512,512]{1,0:T(8,128)(2,1)} %get-tuple-element.50), channel_id=1, source_target_pairs={{4,0},{8,4},{12,8},{16,12},{20,16},{24,20},{28,24},{32,28},{36,32}... | collective-permute-start | bytes 1572872 | tf_op jit(solution)/shard_map/ppermute | solution.py:23
  85.6 4.4 %subtract_convert_fusion = (bf16[4,24,128,128]{3,1,2,0:T(8,128)(2,1)}, bf16[4,24,128,128]{3,1,2,0:T(8,128)(2,1)}) fusion(bf16[4,12,128,128]{3,2,1,0:T(8,128)(2,1)S(1)} %copy-done.8, s32[4,12]{1,0:T(4,128)S(1)} %broadcast_subtract_fusion), kind=kOutput, calls=%fused_computation.2 | convolution fusion | flops 44041344 | bytes 7864512 | tf_op jit(solution)/shard_map/tke,tkab->teab/dot_general | solution.py:130
  91.5 2.5 %collective-permute-done.4 = bf16[512,512]{1,0:T(8,128)(2,1)} collective-permute-done((bf16[512,512]{1,0:T(8,128)(2,1)}, bf16[512,512]{1,0:T(8,128)(2,1)}, u32[]{:S(2)}, u32[]{:S(2)}) %collective-permute-start.4) | collective-permute-done | bytes 524320 | tf_op jit(solution)/shard_map/ppermute | solution.py:23
  111.3 3.1 %collective-permute-done.5 = f32[128,2176]{1,0:T(8,128)} collective-permute-done((f32[128,2176]{1,0:T(8,128)}, f32[128,2176]{1,0:T(8,128)}, u32[]{:S(2)}, u32[]{:S(2)}) %collective-permute-start.5) | collective-permute-done | bytes 1114144 | tf_op jit(solution)/shard_map/ppermute | solution.py:63
  120.0 4.7 %fusion.60 = (bf16[24,128,512]{2,1,0:T(8,128)(2,1)S(1)}, f32[24,128,512]{2,1,0:T(8,128)}) fusion(f32[24,128,512,1]{2,1,3,0:T(8,128)S(1)} %fusion, bf16[4,128,512,1]{2,1,0,3:T(8,128)(2,1)S(1)} %bitcast.80, bf16[4,24,128,128]{3,1,2,0:T(8,128)(2,1)S(1)} %copy-done.5), kind=kOutput, calls=%fused_computation.118 | convolution fusion | flops 1613758464 | bytes 19398656 | tf_op jit(solution)/shard_map/teab,taf->ebf/dot_general | solution.py:149
  125.5 2.3 collective-permute-start.7
  127.9 2.2 collective-permute-start.8
  131.4 4.8 %slice.181 = f32[16,128,512]{2,1,0:T(8,128)} slice(f32[24,128,512]{2,1,0:T(8,128)} %get-tuple-element.58), slice={[4:20], [0:128], [0:512]} | slice | bytes 8388608 | tf_op jit(solution)/shard_map/slice | solution.py:155
  139.5 2.4 fusion.33
  141.9 9.4 %collective-permute-done.6 = f32[64,2176]{1,0:T(8,128)S(1)} collective-permute-done((f32[64,2176]{1,0:T(8,128)S(1)}, f32[64,2176]{1,0:T(8,128)S(1)}, u32[]{:S(2)}, u32[]{:S(2)}) %collective-permute-start.6) | collective-permute-done | bytes 557088 | tf_op jit(solution)/shard_map/ppermute | solution.py:58
  151.6 7.6 %collective-permute-done.9 = f32[32,2176]{1,0:T(8,128)S(1)} collective-permute-done((f32[32,2176]{1,0:T(8,128)S(1)}, f32[32,2176]{1,0:T(8,128)S(1)}, u32[]{:S(2)}, u32[]{:S(2)}) %collective-permute-start.9) | collective-permute-done | bytes 278560 | tf_op jit(solution)/shard_map/ppermute | solution.py:63
  159.3 3.9 %collective-permute-done.10 = f32[16,2176]{1,0:T(8,128)S(1)} collective-permute-done((f32[16,2176]{1,0:T(8,128)S(1)}, f32[16,2176]{1,0:T(8,128)S(1)}, u32[]{:S(2)}, u32[]{:S(2)}) %collective-permute-start.10) | collective-permute-done | bytes 139296 | tf_op jit(solution)/shard_map/ppermute | solution.py:63
  163.2 2.1 collective-permute-start.11
  165.3 3.2 %collective-permute-done.11 = f32[16,2176]{1,0:T(8,128)S(1)} collective-permute-done((f32[16,2176]{1,0:T(8,128)S(1)}, f32[16,2176]{1,0:T(8,128)S(1)}, u32[]{:S(2)}, u32[]{:S(2)}) %collective-permute-start.11) | collective-permute-done | bytes 139296 | tf_op jit(solution)/shard_map/ppermute | solution.py:66
  168.7 5.4 %collective-permute-done.12 = f32[16,2176]{1,0:T(8,128)S(1)} collective-permute-done((f32[16,2176]{1,0:T(8,128)S(1)}, f32[16,2176]{1,0:T(8,128)S(1)}, u32[]{:S(2)}, u32[]{:S(2)}) %collective-permute-start.12) | collective-permute-done | bytes 139296 | tf_op jit(solution)/shard_map/ppermute | solution.py:66
  175.8 7.0 %collective-permute-done.13 = f32[16,2176]{1,0:T(8,128)S(1)} collective-permute-done((f32[16,2176]{1,0:T(8,128)S(1)}, f32[16,2176]{1,0:T(8,128)S(1)}, u32[]{:S(2)}, u32[]{:S(2)}) %collective-permute-start.13) | collective-permute-done | bytes 139296 | tf_op jit(solution)/shard_map/ppermute | solution.py:66
  182.8 6.7 %collective-permute-start.14 = (f32[16,2176]{1,0:T(8,128)S(1)}, f32[16,2176]{1,0:T(8,128)S(1)}, u32[]{:S(2)}, u32[]{:S(2)}) collective-permute-start(f32[16,2176]{1,0:T(8,128)S(1)} %add.150), channel_id=1, source_target_pairs={{0,32},{1,33},{2,34},{3,35},{4,36},{5,37},{6,38},{7,39},{8,40},{9,... | collective-permute-start | bytes 417800 | tf_op jit(solution)/shard_map/ppermute | solution.py:66
  189.5 2.5 %collective-permute-done.14 = f32[16,2176]{1,0:T(8,128)S(1)} collective-permute-done((f32[16,2176]{1,0:T(8,128)S(1)}, f32[16,2176]{1,0:T(8,128)S(1)}, u32[]{:S(2)}, u32[]{:S(2)}) %collective-permute-start.14) | collective-permute-done | bytes 139296 | tf_op jit(solution)/shard_map/ppermute | solution.py:66
  192.2 7.4 %collective-permute-done.15 = f32[16,2176]{1,0:T(8,128)S(1)} collective-permute-done((f32[16,2176]{1,0:T(8,128)S(1)}, f32[16,2176]{1,0:T(8,128)S(1)}, u32[]{:S(2)}, u32[]{:S(2)}) %collective-permute-start.15) | collective-permute-done | bytes 139296 | tf_op jit(solution)/shard_map/ppermute | solution.py:70
  201.6 4.2 %collective-permute-done.16 = f32[32,2176]{1,0:T(8,128)S(1)} collective-permute-done((f32[32,2176]{1,0:T(8,128)S(1)}, f32[32,2176]{1,0:T(8,128)S(1)}, u32[]{:S(2)}, u32[]{:S(2)}) %collective-permute-start.16) | collective-permute-done | bytes 278560 | tf_op jit(solution)/shard_map/ppermute | solution.py:70
  205.9 2.1 collective-permute-start.17
  208.0 6.9 %collective-permute-done.17 = f32[64,2176]{1,0:T(8,128)S(1)} collective-permute-done((f32[64,2176]{1,0:T(8,128)S(1)}, f32[64,2176]{1,0:T(8,128)S(1)}, u32[]{:S(2)}, u32[]{:S(2)}) %collective-permute-start.17) | collective-permute-done | bytes 557088 | tf_op jit(solution)/shard_map/ppermute | solution.py:70
  215.0 8.5 %collective-permute-start.18 = (f32[128,2176]{1,0:T(8,128)S(1)}, f32[128,2176]{1,0:T(8,128)S(1)}, u32[]{:S(2)}, u32[]{:S(2)}) collective-permute-start(f32[128,2176]{1,0:T(8,128)S(1)} %maximum_select_fusion.1), channel_id=1, source_target_pairs={{0,4},{1,5},{2,6},{3,7},{4,0},{5,1},{6,2},{7,3},{8,12},{9,13},{10,... | collective-permute-start | bytes 3342344 | tf_op jit(solution)/shard_map/ppermute | solution.py:70
  228.3 2.6 %slice.165 = f32[512,512]{1,0:T(8,128)} reshape(f32[128,2048]{1,0:T(8,128)} %get-tuple-element.47) | data formatting | bytes 2097152 | tf_op jit(solution)/shard_map/slice | solution.py:174
  232.3 2.2 add_convert_fusion
  (125 shorter events, 53.5 us)
Async XLA Ops:
  7.2 92.7 %copy-start = (bf16[512,512]{1,0:T(8,128)(2,1)S(1)}, bf16[512,512]{1,0:T(8,128)(2,1)}, u32[]{:S(2)}) copy-start(bf16[512,512]{1,0:T(8,128)(2,1)} %param.19) | copy-start | bytes 1572868
  10.5 16.0 %copy-start.15 = (s32[4,12]{1,0:T(4,128)S(1)}, s32[4,12]{1,0:T(4,128)}, u32[]{:S(2)}) copy-start(s32[4,12]{1,0:T(4,128)} %param.17) | copy-start | bytes 580
  13.3 31.2 %all-to-all-start = ((bf16[64,2,2112]{2,1,0:T(2,128)(2,1)}), bf16[64,2,2112]{2,1,0:T(2,128)(2,1)S(1)}, u32[]{:S(2)}, u32[]{:S(2)}) async-start(bf16[64,2,2112]{2,1,0:T(2,128)(2,1)} %reshape.193), calls=%async_computation | async-start | bytes 1114112 | tf_op jit(solution)/shard_map/all_to_all | solution.py:116
  26.5 205.8 %reduce-scatter.2.cloned.1.call-start = ((), (), s32[]{:S(2)}) async-start(), calls=%async_computation.2 | async-start | bytes 5242880 | tf_op jit(solution)/shard_map/reduce_scatter | solution.py:176
  45.2 4.7 %copy-start.16 = (s32[4,12]{1,0:T(4,128)S(1)}, s32[4,12]{1,0:T(4,128)}, u32[]{:S(2)}) copy-start(s32[4,12]{1,0:T(4,128)} %param.16) | copy-start | bytes 580
  45.2 4.6 %copy-start.14 = (bf16[4,12,128,128]{3,2,1,0:T(8,128)(2,1)S(1)}, bf16[4,12,128,128]{3,2,1,0:T(8,128)(2,1)}, u32[]{:S(2)}) copy-start(bf16[4,12,128,128]{3,2,1,0:T(8,128)(2,1)} %param.15) | copy-start | bytes 4718596
  46.2 43.8 %copy-start.9 = (bf16[512,512]{1,0:T(8,128)(2,1)}, bf16[512,512]{1,0:T(8,128)(2,1)S(1)}, u32[]{:S(2)}) copy-start(bf16[512,512]{1,0:T(8,128)(2,1)S(1)} %convolution_convert_fusion) | copy-start | bytes 1572868
  46.2 24.5 %collective-permute-start.2 = (bf16[512,512]{1,0:T(8,128)(2,1)S(1)}, bf16[512,512]{1,0:T(8,128)(2,1)S(1)}, u32[]{:S(2)}, u32[]{:S(2)}) collective-permute-start(bf16[512,512]{1,0:T(8,128)(2,1)S(1)} %convolution_convert_fusion), channel_id=1, source_target_pairs={{0,3},{1,0},{2,1},{3,2},{4,7},{5,4},{6,5},{7,6},{8,11},{9,8},{10,9... | collective-permute-start | bytes 1572872 | tf_op jit(solution)/shard_map/ppermute | solution.py:79
  48.8 22.0 %collective-permute-start.1 = (bf16[512,512]{1,0:T(8,128)(2,1)S(1)}, bf16[512,512]{1,0:T(8,128)(2,1)S(1)}, u32[]{:S(2)}, u32[]{:S(2)}) collective-permute-start(bf16[512,512]{1,0:T(8,128)(2,1)S(1)} %convolution_convert_fusion), channel_id=1, source_target_pairs={{0,2},{1,3},{2,0},{3,1},{4,6},{5,7},{6,4},{7,5},{8,10},{9,11},{10,... | collective-permute-start | bytes 1572872 | tf_op jit(solution)/shard_map/ppermute | solution.py:79
  49.3 26.1 %collective-permute-start = (bf16[512,512]{1,0:T(8,128)(2,1)S(1)}, bf16[512,512]{1,0:T(8,128)(2,1)S(1)}, u32[]{:S(2)}, u32[]{:S(2)}) collective-permute-start(bf16[512,512]{1,0:T(8,128)(2,1)S(1)} %convolution_convert_fusion), channel_id=1, source_target_pairs={{0,1},{1,2},{2,3},{3,0},{4,5},{5,6},{6,7},{7,4},{8,9},{9,10},{10,1... | collective-permute-start | bytes 1572872 | tf_op jit(solution)/shard_map/ppermute | solution.py:79
  79.2 6.3 %copy-start.8 = (bf16[4,12,128,128]{3,2,1,0:T(8,128)(2,1)S(1)}, bf16[4,12,128,128]{3,2,1,0:T(8,128)(2,1)}, u32[]{:S(2)}) copy-start(bf16[4,12,128,128]{3,2,1,0:T(8,128)(2,1)} %get-tuple-element.42) | copy-start | bytes 4718596
  80.3 11.2 %collective-permute-start.3 = (bf16[512,512]{1,0:T(8,128)(2,1)}, bf16[512,512]{1,0:T(8,128)(2,1)}, u32[]{:S(2)}, u32[]{:S(2)}) collective-permute-start(bf16[512,512]{1,0:T(8,128)(2,1)} %get-tuple-element.49), channel_id=1, source_target_pairs={{0,4},{4,8},{8,12},{12,16},{16,20},{20,24},{24,28},{28,32},{32,36}... | collective-permute-start | bytes 1572872 | tf_op jit(solution)/shard_map/ppermute | solution.py:20
  83.1 10.8 %collective-permute-start.4 = (bf16[512,512]{1,0:T(8,128)(2,1)}, bf16[512,512]{1,0:T(8,128)(2,1)}, u32[]{:S(2)}, u32[]{:S(2)}) collective-permute-start(bf16[512,512]{1,0:T(8,128)(2,1)} %get-tuple-element.50), channel_id=1, source_target_pairs={{4,0},{8,4},{12,8},{16,12},{20,16},{24,20},{28,24},{32,28},{36,32}... | collective-permute-start | bytes 1572872 | tf_op jit(solution)/shard_map/ppermute | solution.py:23
  111.3 3.1 %collective-permute-start.5 = (f32[128,2176]{1,0:T(8,128)}, f32[128,2176]{1,0:T(8,128)}, u32[]{:S(2)}, u32[]{:S(2)}) collective-permute-start(f32[128,2176]{1,0:T(8,128)} %slice_select_fusion), channel_id=1, source_target_pairs={{0,4},{1,5},{2,6},{3,7},{4,0},{5,1},{6,2},{7,3},{8,12},{9,13},{10,... | collective-permute-start | bytes 3342344 | tf_op jit(solution)/shard_map/ppermute | solution.py:63
  125.5 12.8 %collective-permute-start.7 = (bf16[512,512]{1,0:T(8,128)(2,1)}, bf16[512,512]{1,0:T(8,128)(2,1)S(1)}, u32[]{:S(2)}, u32[]{:S(2)}) collective-permute-start(bf16[512,512]{1,0:T(8,128)(2,1)} %bitcast.29), channel_id=1, source_target_pairs={{0,4},{4,8},{8,12},{12,16},{16,20},{20,24},{24,28},{28,32},{32,36}... | collective-permute-start | bytes 1572872 | tf_op jit(solution)/shard_map/ppermute | solution.py:12
  127.9 11.6 %collective-permute-start.8 = (bf16[512,512]{1,0:T(8,128)(2,1)S(1)}, bf16[512,512]{1,0:T(8,128)(2,1)S(1)}, u32[]{:S(2)}, u32[]{:S(2)}) collective-permute-start(bf16[512,512]{1,0:T(8,128)(2,1)S(1)} %bitcast.81), channel_id=1, source_target_pairs={{4,0},{8,4},{12,8},{16,12},{20,16},{24,20},{28,24},{32,28},{36,32}... | collective-permute-start | bytes 1572872 | tf_op jit(solution)/shard_map/ppermute | solution.py:12
  136.3 15.0 %collective-permute-start.6 = (f32[64,2176]{1,0:T(8,128)S(1)}, f32[64,2176]{1,0:T(8,128)S(1)}, u32[]{:S(2)}, u32[]{:S(2)}) collective-permute-start(f32[64,2176]{1,0:T(8,128)S(1)} %slice_select_fusion.1), channel_id=1, source_target_pairs={{0,8},{1,9},{2,10},{3,11},{4,12},{5,13},{6,14},{7,15},{8,0},{9,1},... | collective-permute-start | bytes 1671176 | tf_op jit(solution)/shard_map/ppermute | solution.py:58
  141.8 9.5 %copy-start.7 = (f32[128,2176]{1,0:T(8,128)S(1)}, f32[128,2176]{1,0:T(8,128)}, u32[]{:S(2)}) copy-start(f32[128,2176]{1,0:T(8,128)} %copy-done.6) | copy-start | bytes 3342340
  151.5 7.7 %collective-permute-start.9 = (f32[32,2176]{1,0:T(8,128)S(1)}, f32[32,2176]{1,0:T(8,128)S(1)}, u32[]{:S(2)}, u32[]{:S(2)}) collective-permute-start(f32[32,2176]{1,0:T(8,128)S(1)} %slice_select_fusion.2), channel_id=1, source_target_pairs={{0,64},{1,65},{2,66},{3,67},{4,68},{5,69},{6,70},{7,71},{8,72},{9,... | collective-permute-start | bytes 835592 | tf_op jit(solution)/shard_map/ppermute | solution.py:63
  159.2 4.0 %collective-permute-start.10 = (f32[16,2176]{1,0:T(8,128)S(1)}, f32[16,2176]{1,0:T(8,128)S(1)}, u32[]{:S(2)}, u32[]{:S(2)}) collective-permute-start(f32[16,2176]{1,0:T(8,128)S(1)} %slice_select_fusion.3), channel_id=1, source_target_pairs={{0,1},{1,0},{2,3},{3,2},{4,5},{5,4},{6,7},{7,6},{8,9},{9,8},{10,11... | collective-permute-start | bytes 417800 | tf_op jit(solution)/shard_map/ppermute | solution.py:63
  163.2 5.3 %collective-permute-start.11 = (f32[16,2176]{1,0:T(8,128)S(1)}, f32[16,2176]{1,0:T(8,128)S(1)}, u32[]{:S(2)}, u32[]{:S(2)}) collective-permute-start(f32[16,2176]{1,0:T(8,128)S(1)} %select_add_fusion.3), channel_id=1, source_target_pairs={{0,16},{1,17},{2,18},{3,19},{4,20},{5,21},{6,22},{7,23},{8,24},{9,... | collective-permute-start | bytes 417800 | tf_op jit(solution)/shard_map/ppermute | solution.py:66
  168.6 5.5 %collective-permute-start.12 = (f32[16,2176]{1,0:T(8,128)S(1)}, f32[16,2176]{1,0:T(8,128)S(1)}, u32[]{:S(2)}, u32[]{:S(2)}) collective-permute-start(f32[16,2176]{1,0:T(8,128)S(1)} %add.148), channel_id=1, source_target_pairs={{0,128},{1,129},{2,130},{3,131},{4,132},{5,133},{6,134},{7,135},{8... | collective-permute-start | bytes 417800 | tf_op jit(solution)/shard_map/ppermute | solution.py:66
  174.1 8.7 %collective-permute-start.13 = (f32[16,2176]{1,0:T(8,128)S(1)}, f32[16,2176]{1,0:T(8,128)S(1)}, u32[]{:S(2)}, u32[]{:S(2)}) collective-permute-start(f32[16,2176]{1,0:T(8,128)S(1)} %add.149), channel_id=1, source_target_pairs={{0,2},{1,3},{2,0},{3,1},{4,6},{5,7},{6,4},{7,5},{8,10},{9,11},{10,... | collective-permute-start | bytes 417800 | tf_op jit(solution)/shard_map/ppermute | solution.py:66
  182.8 40.7 %copy-start.13 = (bf16[512,512]{1,0:T(8,128)(2,1)S(1)}, bf16[512,512]{1,0:T(8,128)(2,1)}, u32[]{:S(2)}) copy-start(bf16[512,512]{1,0:T(8,128)(2,1)} %param.18) | copy-start | bytes 1572868
  182.8 9.3 %collective-permute-start.14 = (f32[16,2176]{1,0:T(8,128)S(1)}, f32[16,2176]{1,0:T(8,128)S(1)}, u32[]{:S(2)}, u32[]{:S(2)}) collective-permute-start(f32[16,2176]{1,0:T(8,128)S(1)} %add.150), channel_id=1, source_target_pairs={{0,32},{1,33},{2,34},{3,35},{4,36},{5,37},{6,38},{7,39},{8,40},{9,... | collective-permute-start | bytes 417800 | tf_op jit(solution)/shard_map/ppermute | solution.py:66
  192.1 7.5 %collective-permute-start.15 = (f32[16,2176]{1,0:T(8,128)S(1)}, f32[16,2176]{1,0:T(8,128)S(1)}, u32[]{:S(2)}, u32[]{:S(2)}) collective-permute-start(f32[16,2176]{1,0:T(8,128)S(1)} %add.151), channel_id=1, source_target_pairs={{0,1},{1,0},{2,3},{3,2},{4,5},{5,4},{6,7},{7,6},{8,9},{9,8},{10,11... | collective-permute-start | bytes 417800 | tf_op jit(solution)/shard_map/ppermute | solution.py:70
  199.7 6.2 %collective-permute-start.16 = (f32[32,2176]{1,0:T(8,128)S(1)}, f32[32,2176]{1,0:T(8,128)S(1)}, u32[]{:S(2)}, u32[]{:S(2)}) collective-permute-start(f32[32,2176]{1,0:T(8,128)S(1)} %maximum_select_fusion.3), channel_id=1, source_target_pairs={{0,64},{1,65},{2,66},{3,67},{4,68},{5,69},{6,70},{7,71},{8,72},{9,... | collective-permute-start | bytes 835592 | tf_op jit(solution)/shard_map/ppermute | solution.py:70
  205.9 9.1 %collective-permute-start.17 = (f32[64,2176]{1,0:T(8,128)S(1)}, f32[64,2176]{1,0:T(8,128)S(1)}, u32[]{:S(2)}, u32[]{:S(2)}) collective-permute-start(f32[64,2176]{1,0:T(8,128)S(1)} %maximum_select_fusion.2), channel_id=1, source_target_pairs={{0,8},{1,9},{2,10},{3,11},{4,12},{5,13},{6,14},{7,15},{8,0},{9,1},... | collective-permute-start | bytes 1671176 | tf_op jit(solution)/shard_map/ppermute | solution.py:70
  215.0 10.8 %collective-permute-start.18 = (f32[128,2176]{1,0:T(8,128)S(1)}, f32[128,2176]{1,0:T(8,128)S(1)}, u32[]{:S(2)}, u32[]{:S(2)}) collective-permute-start(f32[128,2176]{1,0:T(8,128)S(1)} %maximum_select_fusion.1), channel_id=1, source_target_pairs={{0,4},{1,5},{2,6},{3,7},{4,0},{5,1},{6,2},{7,3},{8,12},{9,13},{10,... | collective-permute-start | bytes 3342344 | tf_op jit(solution)/shard_map/ppermute | solution.py:70
  228.3 2.6 %copy-start.12 = (f32[128,2048]{1,0:T(8,128)S(1)}, f32[128,2048]{1,0:T(8,128)}, u32[]{:S(2)}) copy-start(f32[128,2048]{1,0:T(8,128)} %get-tuple-element.48) | copy-start | bytes 3145732
  228.3 3.9 %copy-start.11 = (f32[512,512]{1,0:T(8,128)S(1)}, f32[512,512]{1,0:T(8,128)}, u32[]{:S(2)}) copy-start(f32[512,512]{1,0:T(8,128)} %fusion.62) | copy-start | bytes 3145732
  231.0 3.4 %copy-start.1 = (bf16[512,512]{1,0:T(8,128)(2,1)S(1)}, bf16[512,512]{1,0:T(8,128)(2,1)}, u32[]{:S(2)}) copy-start(bf16[512,512]{1,0:T(8,128)(2,1)} %param.19) | copy-start | bytes 1572868
  (8 other events, 14.3 us)
Sparse Core Ops, SparseCore 0:
  151.4 52.8 reduce-scatter.1

commit v6 on v4

--- a/solution.py
+++ b/solution.py
@@ -38,7 +38,7 @@
 
 
 HALVING_BITS = (2, 3, 6, 0)
-DOUBLING_BITS = (4, 7, 1, 5)
+DOUBLING_BITS = (4, 7, 5, 1)
 
 
 def halving_sum(block, axes):

time: 232 us -> 231 us (level)
  no operation moved by 1% of the time
where the time goes in v6:
time: 231 us; the launch traced here: 230 us
  waiting for transfers between devices  102 us (44%)
  starting transfers between devices  54.9 us (24%)
  matrix products  23.1 us (10%)
  local copies, waits for them, and re-layouts  20.5 us (9%)
  other arithmetic  15.3 us (7%)
  between operations  14.6 us (6%)
    ppermute x3, waiting for transfers between devices, gather_rep(): lax.ppermute(block, 'rep', [(i, (i + shift) % count) for i in range(count)])  23.8 us
    ppermute x4, waiting for transfers between devices, halving_sum(): got = lax.ppermute(block, axes, pairs)  20 us
    ppermute x4, waiting for transfers between devices, halving_sum(): lax.ppermute(block, axes, [(i, i ^ 1 << bit) for i in range(count)])  19 us
    all_to_all x1, waiting for transfers between devices, shards(): got = lax.all_to_all(sent, 'dom', split_axis=0, concat_axis=0, tiled=True)  17.9 us
    ppermute x4, starting transfers between devices, halving_sum(): got = lax.ppermute(block, axes, pairs)  15 us
    all_to_all x1, starting transfers between devices, shards(): got = lax.all_to_all(sent, 'dom', split_axis=0, concat_axis=0, tiled=True)  13.2 us
    ppermute x2, waiting for transfers between devices, shifted(): lax.ppermute(value, axis, [(source, source + steps) for source in range(f...  10.8 us
    ppermute x4, starting transfers between devices, halving_sum(): lax.ppermute(block, axes, [(i, i ^ 1 << bit) for i in range(count)])  10.2 us
  transfers between devices with their start and end apart: 21, of which 16 were waited for; matrix products, arithmetic and copies ran while one was open for 11% of the time, Pallas kernels for 0%

profile of v6, /device:TPU:1, one launch (start us, length us, event | category | flops | bytes accessed | tf_op | source)
XLA Modules:
  0.0 230.4 jit_solution(1731330485474103716)
XLA Ops:
  13.3 13.2 %all-to-all-start = ((bf16[64,2,2112]{2,1,0:T(2,128)(2,1)}), bf16[64,2,2112]{2,1,0:T(2,128)(2,1)S(1)}, u32[]{:S(2)}, u32[]{:S(2)}) async-start(bf16[64,2,2112]{2,1,0:T(2,128)(2,1)} %reshape.193), calls=%async_computation | async-start | bytes 1114112 | tf_op jit(solution)/shard_map/all_to_all | solution.py:109
  26.6 17.9 %all-to-all-done = bf16[64,2,2112]{2,1,0:T(2,128)(2,1)S(1)} async-done(((bf16[64,2,2112]{2,1,0:T(2,128)(2,1)}), bf16[64,2,2112]{2,1,0:T(2,128)(2,1)S(1)}, u32[]{:S(2)}, u32[]{:S(2)}) %all-to-all-start) | async-done | bytes 540704 | tf_op jit(solution)/shard_map/all_to_all | solution.py:109
  46.2 2.6 %collective-permute-start.2 = (bf16[512,512]{1,0:T(8,128)(2,1)S(1)}, bf16[512,512]{1,0:T(8,128)(2,1)S(1)}, u32[]{:S(2)}, u32[]{:S(2)}) collective-permute-start(bf16[512,512]{1,0:T(8,128)(2,1)S(1)} %convolution_convert_fusion), channel_id=1, source_target_pairs={{0,3},{1,0},{2,1},{3,2},{4,7},{5,4},{6,5},{7,6},{8,11},{9,8},{10,9... | collective-permute-start | bytes 1572872 | tf_op jit(solution)/shard_map/ppermute | solution.py:72
  51.6 19.2 %collective-permute-done.2 = bf16[512,512]{1,0:T(8,128)(2,1)S(1)} collective-permute-done((bf16[512,512]{1,0:T(8,128)(2,1)S(1)}, bf16[512,512]{1,0:T(8,128)(2,1)S(1)}, u32[]{:S(2)}, u32[]{:S(2)}) %collective-permute-start.2) | collective-permute-done | bytes 524320 | tf_op jit(solution)/shard_map/ppermute | solution.py:72
  70.8 4.6 %collective-permute-done = bf16[512,512]{1,0:T(8,128)(2,1)S(1)} collective-permute-done((bf16[512,512]{1,0:T(8,128)(2,1)S(1)}, bf16[512,512]{1,0:T(8,128)(2,1)S(1)}, u32[]{:S(2)}, u32[]{:S(2)}) %collective-permute-start) | collective-permute-done | bytes 524320 | tf_op jit(solution)/shard_map/ppermute | solution.py:72
  77.0 2.3 gather_fusion
  80.3 2.8 %collective-permute-start.3 = (bf16[512,512]{1,0:T(8,128)(2,1)}, bf16[512,512]{1,0:T(8,128)(2,1)}, u32[]{:S(2)}, u32[]{:S(2)}) collective-permute-start(bf16[512,512]{1,0:T(8,128)(2,1)} %get-tuple-element.41), channel_id=1, source_target_pairs={{0,4},{4,8},{8,12},{12,16},{16,20},{20,24},{24,28},{28,32},{32,36}... | collective-permute-start | bytes 1572872 | tf_op jit(solution)/shard_map/ppermute | solution.py:20
  83.1 2.4 %collective-permute-start.4 = (bf16[512,512]{1,0:T(8,128)(2,1)}, bf16[512,512]{1,0:T(8,128)(2,1)}, u32[]{:S(2)}, u32[]{:S(2)}) collective-permute-start(bf16[512,512]{1,0:T(8,128)(2,1)} %get-tuple-element.42), channel_id=1, source_target_pairs={{4,0},{8,4},{12,8},{16,12},{20,16},{24,20},{28,24},{32,28},{36,32}... | collective-permute-start | bytes 1572872 | tf_op jit(solution)/shard_map/ppermute | solution.py:23
  85.6 4.4 %subtract_convert_fusion = (bf16[4,24,128,128]{3,1,2,0:T(8,128)(2,1)}, bf16[4,24,128,128]{3,1,2,0:T(8,128)(2,1)}) fusion(bf16[4,12,128,128]{3,2,1,0:T(8,128)(2,1)S(1)} %copy-done.6, s32[4,12]{1,0:T(4,128)S(1)} %broadcast_subtract_fusion), kind=kOutput, calls=%fused_computation.2 | convolution fusion | flops 44041344 | bytes 7864512 | tf_op jit(solution)/shard_map/tke,tkab->teab/dot_general | solution.py:123
  91.4 2.5 %collective-permute-done.4 = bf16[512,512]{1,0:T(8,128)(2,1)} collective-permute-done((bf16[512,512]{1,0:T(8,128)(2,1)}, bf16[512,512]{1,0:T(8,128)(2,1)}, u32[]{:S(2)}, u32[]{:S(2)}) %collective-permute-start.4) | collective-permute-done | bytes 524320 | tf_op jit(solution)/shard_map/ppermute | solution.py:23
  106.5 2.1 reshape.173
  116.3 2.4 %slice.177 = f32[16,128,512]{2,1,0:T(8,128)} slice(f32[24,128,512]{2,1,0:T(8,128)S(1)} %get-tuple-element.50), slice={[4:20], [0:128], [0:512]} | slice | bytes 8388608 | tf_op jit(solution)/shard_map/slice | solution.py:161
  120.7 2.7 %collective-permute-start.6 = (bf16[512,512]{1,0:T(8,128)(2,1)S(1)}, bf16[512,512]{1,0:T(8,128)(2,1)S(1)}, u32[]{:S(2)}, u32[]{:S(2)}) collective-permute-start(bf16[512,512]{1,0:T(8,128)(2,1)S(1)} %bitcast.81), channel_id=1, source_target_pairs={{4,0},{8,4},{12,8},{16,12},{20,16},{24,20},{28,24},{32,28},{36,32}... | collective-permute-start | bytes 1572872 | tf_op jit(solution)/shard_map/ppermute | solution.py:12
  124.4 3.1 %collective-permute-done.5 = bf16[512,512]{1,0:T(8,128)(2,1)S(1)} collective-permute-done((bf16[512,512]{1,0:T(8,128)(2,1)S(1)}, bf16[512,512]{1,0:T(8,128)(2,1)S(1)}, u32[]{:S(2)}, u32[]{:S(2)}) %collective-permute-start.5) | collective-permute-done | bytes 524320 | tf_op jit(solution)/shard_map/ppermute | solution.py:12
  128.7 7.7 %collective-permute-done.6 = bf16[512,512]{1,0:T(8,128)(2,1)S(1)} collective-permute-done((bf16[512,512]{1,0:T(8,128)(2,1)S(1)}, bf16[512,512]{1,0:T(8,128)(2,1)S(1)}, u32[]{:S(2)}, u32[]{:S(2)}) %collective-permute-start.6) | collective-permute-done | bytes 524320 | tf_op jit(solution)/shard_map/ppermute | solution.py:12
  136.3 2.4 %fusion.33 = f32[2048,512]{1,0:T(8,128)} fusion(f32[2048,512]{1,0:T(8,128)} %constant_dynamic-update-slice_fusion, bf16[512,512]{1,0:T(8,128)(2,1)S(1)} %collective-permute-done.6), kind=kLoop, calls=%fused_computation.42 | loop fusion | flops 524288 | bytes 2621440 | tf_op jit(solution)/shard_map/scatter-add | solution.py:163
  140.8 3.9 %collective-permute-done.9 = f32[32,2176]{1,0:T(8,128)S(1)} collective-permute-done((f32[32,2176]{1,0:T(8,128)S(1)}, f32[32,2176]{1,0:T(8,128)S(1)}, u32[]{:S(2)}, u32[]{:S(2)}) %collective-permute-start.9) | collective-permute-done | bytes 278560 | tf_op jit(solution)/shard_map/ppermute | solution.py:56
  144.9 4.2 %collective-permute-done.10 = f32[16,2176]{1,0:T(8,128)S(1)} collective-permute-done((f32[16,2176]{1,0:T(8,128)S(1)}, f32[16,2176]{1,0:T(8,128)S(1)}, u32[]{:S(2)}, u32[]{:S(2)}) %collective-permute-start.10) | collective-permute-done | bytes 139296 | tf_op jit(solution)/shard_map/ppermute | solution.py:56
  149.1 2.5 %collective-permute-start.11 = (f32[16,2176]{1,0:T(8,128)S(1)}, f32[16,2176]{1,0:T(8,128)S(1)}, u32[]{:S(2)}, u32[]{:S(2)}) collective-permute-start(f32[16,2176]{1,0:T(8,128)S(1)} %select_add_fusion.3), channel_id=1, source_target_pairs={{0,16},{1,17},{2,18},{3,19},{4,20},{5,21},{6,22},{7,23},{8,24},{9,... | collective-permute-start | bytes 417800 | tf_op jit(solution)/shard_map/ppermute | solution.py:59
  151.6 2.9 %collective-permute-done.11 = f32[16,2176]{1,0:T(8,128)S(1)} collective-permute-done((f32[16,2176]{1,0:T(8,128)S(1)}, f32[16,2176]{1,0:T(8,128)S(1)}, u32[]{:S(2)}, u32[]{:S(2)}) %collective-permute-start.11) | collective-permute-done | bytes 139296 | tf_op jit(solution)/shard_map/ppermute | solution.py:59
  154.5 3.6 %collective-permute-start.12 = (f32[16,2176]{1,0:T(8,128)S(1)}, f32[16,2176]{1,0:T(8,128)S(1)}, u32[]{:S(2)}, u32[]{:S(2)}) collective-permute-start(f32[16,2176]{1,0:T(8,128)S(1)} %add.148), channel_id=1, source_target_pairs={{0,128},{1,129},{2,130},{3,131},{4,132},{5,133},{6,134},{7,135},{8... | collective-permute-start | bytes 417800 | tf_op jit(solution)/shard_map/ppermute | solution.py:59
  158.1 2.5 %collective-permute-done.12 = f32[16,2176]{1,0:T(8,128)S(1)} collective-permute-done((f32[16,2176]{1,0:T(8,128)S(1)}, f32[16,2176]{1,0:T(8,128)S(1)}, u32[]{:S(2)}, u32[]{:S(2)}) %collective-permute-start.12) | collective-permute-done | bytes 139296 | tf_op jit(solution)/shard_map/ppermute | solution.py:59
  160.6 4.0 %collective-permute-start.13 = (f32[16,2176]{1,0:T(8,128)S(1)}, f32[16,2176]{1,0:T(8,128)S(1)}, u32[]{:S(2)}, u32[]{:S(2)}) collective-permute-start(f32[16,2176]{1,0:T(8,128)S(1)} %add.149), channel_id=1, source_target_pairs={{0,32},{1,33},{2,34},{3,35},{4,36},{5,37},{6,38},{7,39},{8,40},{9,... | collective-permute-start | bytes 417800 | tf_op jit(solution)/shard_map/ppermute | solution.py:59
  164.6 5.1 %collective-permute-done.13 = f32[16,2176]{1,0:T(8,128)S(1)} collective-permute-done((f32[16,2176]{1,0:T(8,128)S(1)}, f32[16,2176]{1,0:T(8,128)S(1)}, u32[]{:S(2)}, u32[]{:S(2)}) %collective-permute-start.13) | collective-permute-done | bytes 139296 | tf_op jit(solution)/shard_map/ppermute | solution.py:59
  169.9 8.6 %collective-permute-done.14 = f32[16,2176]{1,0:T(8,128)S(1)} collective-permute-done((f32[16,2176]{1,0:T(8,128)S(1)}, f32[16,2176]{1,0:T(8,128)S(1)}, u32[]{:S(2)}, u32[]{:S(2)}) %collective-permute-start.14) | collective-permute-done | bytes 139296 | tf_op jit(solution)/shard_map/ppermute | solution.py:59
  178.5 8.1 %collective-permute-done.15 = f32[16,2176]{1,0:T(8,128)S(1)} collective-permute-done((f32[16,2176]{1,0:T(8,128)S(1)}, f32[16,2176]{1,0:T(8,128)S(1)}, u32[]{:S(2)}, u32[]{:S(2)}) %collective-permute-start.15) | collective-permute-done | bytes 139296 | tf_op jit(solution)/shard_map/ppermute | solution.py:63
  186.6 2.9 %collective-permute-start.16 = (f32[32,2176]{1,0:T(8,128)S(1)}, f32[32,2176]{1,0:T(8,128)S(1)}, u32[]{:S(2)}, u32[]{:S(2)}) collective-permute-start(f32[32,2176]{1,0:T(8,128)S(1)} %maximum_select_fusion.3), channel_id=1, source_target_pairs={{0,64},{1,65},{2,66},{3,67},{4,68},{5,69},{6,70},{7,71},{8,72},{9,... | collective-permute-start | bytes 835592 | tf_op jit(solution)/shard_map/ppermute | solution.py:63
  189.5 3.9 %collective-permute-done.16 = f32[32,2176]{1,0:T(8,128)S(1)} collective-permute-done((f32[32,2176]{1,0:T(8,128)S(1)}, f32[32,2176]{1,0:T(8,128)S(1)}, u32[]{:S(2)}, u32[]{:S(2)}) %collective-permute-start.16) | collective-permute-done | bytes 278560 | tf_op jit(solution)/shard_map/ppermute | solution.py:63
  195.4 7.1 %collective-permute-done.17 = f32[64,2176]{1,0:T(8,128)S(1)} collective-permute-done((f32[64,2176]{1,0:T(8,128)S(1)}, f32[64,2176]{1,0:T(8,128)S(1)}, u32[]{:S(2)}, u32[]{:S(2)}) %collective-permute-start.17) | collective-permute-done | bytes 557088 | tf_op jit(solution)/shard_map/ppermute | solution.py:63
  202.5 10.1 %collective-permute-start.18 = (f32[128,2176]{1,0:T(8,128)S(1)}, f32[128,2176]{1,0:T(8,128)S(1)}, u32[]{:S(2)}, u32[]{:S(2)}) collective-permute-start(f32[128,2176]{1,0:T(8,128)S(1)} %maximum_select_fusion.1), channel_id=1, source_target_pairs={{0,4},{1,5},{2,6},{3,7},{4,0},{5,1},{6,2},{7,3},{8,12},{9,13},{10,... | collective-permute-start | bytes 3342344 | tf_op jit(solution)/shard_map/ppermute | solution.py:63
  217.5 2.6 %slice.165 = f32[512,512]{1,0:T(8,128)} reshape(f32[128,2048]{1,0:T(8,128)} %get-tuple-element.39) | data formatting | bytes 2097152 | tf_op jit(solution)/shard_map/slice | solution.py:151
  221.4 2.2 add_convert_fusion
  (127 shorter events, 49.7 us)
Async XLA Ops:
  7.2 92.7 %copy-start = (bf16[512,512]{1,0:T(8,128)(2,1)S(1)}, bf16[512,512]{1,0:T(8,128)(2,1)}, u32[]{:S(2)}) copy-start(bf16[512,512]{1,0:T(8,128)(2,1)} %param.19) | copy-start | bytes 1572868
  10.5 16.0 %copy-start.16 = (s32[4,12]{1,0:T(4,128)S(1)}, s32[4,12]{1,0:T(4,128)}, u32[]{:S(2)}) copy-start(s32[4,12]{1,0:T(4,128)} %param.17) | copy-start | bytes 580
  13.3 31.2 %all-to-all-start = ((bf16[64,2,2112]{2,1,0:T(2,128)(2,1)}), bf16[64,2,2112]{2,1,0:T(2,128)(2,1)S(1)}, u32[]{:S(2)}, u32[]{:S(2)}) async-start(bf16[64,2,2112]{2,1,0:T(2,128)(2,1)} %reshape.193), calls=%async_computation | async-start | bytes 1114112 | tf_op jit(solution)/shard_map/all_to_all | solution.py:109
  26.5 194.9 %reduce-scatter.2.cloned.1.call-start = ((), (), s32[]{:S(2)}) async-start(), calls=%async_computation.2 | async-start | bytes 5242880 | tf_op jit(solution)/shard_map/reduce_scatter | solution.py:164
  45.2 4.7 %copy-start.17 = (s32[4,12]{1,0:T(4,128)S(1)}, s32[4,12]{1,0:T(4,128)}, u32[]{:S(2)}) copy-start(s32[4,12]{1,0:T(4,128)} %param.16) | copy-start | bytes 580
  45.2 4.6 %copy-start.15 = (bf16[4,12,128,128]{3,2,1,0:T(8,128)(2,1)S(1)}, bf16[4,12,128,128]{3,2,1,0:T(8,128)(2,1)}, u32[]{:S(2)}) copy-start(bf16[4,12,128,128]{3,2,1,0:T(8,128)(2,1)} %param.15) | copy-start | bytes 4718596
  46.2 43.8 %copy-start.7 = (bf16[512,512]{1,0:T(8,128)(2,1)}, bf16[512,512]{1,0:T(8,128)(2,1)S(1)}, u32[]{:S(2)}) copy-start(bf16[512,512]{1,0:T(8,128)(2,1)S(1)} %convolution_convert_fusion) | copy-start | bytes 1572868
  46.2 24.5 %collective-permute-start.2 = (bf16[512,512]{1,0:T(8,128)(2,1)S(1)}, bf16[512,512]{1,0:T(8,128)(2,1)S(1)}, u32[]{:S(2)}, u32[]{:S(2)}) collective-permute-start(bf16[512,512]{1,0:T(8,128)(2,1)S(1)} %convolution_convert_fusion), channel_id=1, source_target_pairs={{0,3},{1,0},{2,1},{3,2},{4,7},{5,4},{6,5},{7,6},{8,11},{9,8},{10,9... | collective-permute-start | bytes 1572872 | tf_op jit(solution)/shard_map/ppermute | solution.py:72
  48.8 22.0 %collective-permute-start.1 = (bf16[512,512]{1,0:T(8,128)(2,1)S(1)}, bf16[512,512]{1,0:T(8,128)(2,1)S(1)}, u32[]{:S(2)}, u32[]{:S(2)}) collective-permute-start(bf16[512,512]{1,0:T(8,128)(2,1)S(1)} %convolution_convert_fusion), channel_id=1, source_target_pairs={{0,2},{1,3},{2,0},{3,1},{4,6},{5,7},{6,4},{7,5},{8,10},{9,11},{10,... | collective-permute-start | bytes 1572872 | tf_op jit(solution)/shard_map/ppermute | solution.py:72
  49.3 26.1 %collective-permute-start = (bf16[512,512]{1,0:T(8,128)(2,1)S(1)}, bf16[512,512]{1,0:T(8,128)(2,1)S(1)}, u32[]{:S(2)}, u32[]{:S(2)}) collective-permute-start(bf16[512,512]{1,0:T(8,128)(2,1)S(1)} %convolution_convert_fusion), channel_id=1, source_target_pairs={{0,1},{1,2},{2,3},{3,0},{4,5},{5,6},{6,7},{7,4},{8,9},{9,10},{10,1... | collective-permute-start | bytes 1572872 | tf_op jit(solution)/shard_map/ppermute | solution.py:72
  79.2 6.3 %copy-start.6 = (bf16[4,12,128,128]{3,2,1,0:T(8,128)(2,1)S(1)}, bf16[4,12,128,128]{3,2,1,0:T(8,128)(2,1)}, u32[]{:S(2)}) copy-start(bf16[4,12,128,128]{3,2,1,0:T(8,128)(2,1)} %get-tuple-element.34) | copy-start | bytes 4718596
  80.3 11.2 %collective-permute-start.3 = (bf16[512,512]{1,0:T(8,128)(2,1)}, bf16[512,512]{1,0:T(8,128)(2,1)}, u32[]{:S(2)}, u32[]{:S(2)}) collective-permute-start(bf16[512,512]{1,0:T(8,128)(2,1)} %get-tuple-element.41), channel_id=1, source_target_pairs={{0,4},{4,8},{8,12},{12,16},{16,20},{20,24},{24,28},{28,32},{32,36}... | collective-permute-start | bytes 1572872 | tf_op jit(solution)/shard_map/ppermute | solution.py:20
  83.1 10.8 %collective-permute-start.4 = (bf16[512,512]{1,0:T(8,128)(2,1)}, bf16[512,512]{1,0:T(8,128)(2,1)}, u32[]{:S(2)}, u32[]{:S(2)}) collective-permute-start(bf16[512,512]{1,0:T(8,128)(2,1)} %get-tuple-element.42), channel_id=1, source_target_pairs={{4,0},{8,4},{12,8},{16,12},{20,16},{24,20},{28,24},{32,28},{36,32}... | collective-permute-start | bytes 1572872 | tf_op jit(solution)/shard_map/ppermute | solution.py:23
  93.9 2.2 copy-start.2
  110.5 12.8 %collective-permute-start.7 = (f32[128,2176]{1,0:T(8,128)S(1)}, f32[128,2176]{1,0:T(8,128)S(1)}, u32[]{:S(2)}, u32[]{:S(2)}) collective-permute-start(f32[128,2176]{1,0:T(8,128)S(1)} %slice_select_fusion), channel_id=1, source_target_pairs={{0,4},{1,5},{2,6},{3,7},{4,0},{5,1},{6,2},{7,3},{8,12},{9,13},{10,... | collective-permute-start | bytes 3342344 | tf_op jit(solution)/shard_map/ppermute | solution.py:56
  118.8 8.8 %collective-permute-start.5 = (bf16[512,512]{1,0:T(8,128)(2,1)S(1)}, bf16[512,512]{1,0:T(8,128)(2,1)S(1)}, u32[]{:S(2)}, u32[]{:S(2)}) collective-permute-start(bf16[512,512]{1,0:T(8,128)(2,1)S(1)} %bitcast.82), channel_id=1, source_target_pairs={{0,4},{4,8},{8,12},{12,16},{16,20},{20,24},{24,28},{28,32},{32,36}... | collective-permute-start | bytes 1572872 | tf_op jit(solution)/shard_map/ppermute | solution.py:12
  120.7 15.7 %collective-permute-start.6 = (bf16[512,512]{1,0:T(8,128)(2,1)S(1)}, bf16[512,512]{1,0:T(8,128)(2,1)S(1)}, u32[]{:S(2)}, u32[]{:S(2)}) collective-permute-start(bf16[512,512]{1,0:T(8,128)(2,1)S(1)} %bitcast.81), channel_id=1, source_target_pairs={{4,0},{8,4},{12,8},{16,12},{20,16},{24,20},{28,24},{32,28},{36,32}... | collective-permute-start | bytes 1572872 | tf_op jit(solution)/shard_map/ppermute | solution.py:12
  123.6 15.1 %collective-permute-start.8 = (f32[64,2176]{1,0:T(8,128)S(1)}, f32[64,2176]{1,0:T(8,128)S(1)}, u32[]{:S(2)}, u32[]{:S(2)}) collective-permute-start(f32[64,2176]{1,0:T(8,128)S(1)} %slice_select_fusion.1), channel_id=1, source_target_pairs={{0,8},{1,9},{2,10},{3,11},{4,12},{5,13},{6,14},{7,15},{8,0},{9,1},... | collective-permute-start | bytes 1671176 | tf_op jit(solution)/shard_map/ppermute | solution.py:56
  138.9 5.9 %collective-permute-start.9 = (f32[32,2176]{1,0:T(8,128)S(1)}, f32[32,2176]{1,0:T(8,128)S(1)}, u32[]{:S(2)}, u32[]{:S(2)}) collective-permute-start(f32[32,2176]{1,0:T(8,128)S(1)} %slice_select_fusion.2), channel_id=1, source_target_pairs={{0,64},{1,65},{2,66},{3,67},{4,68},{5,69},{6,70},{7,71},{8,72},{9,... | collective-permute-start | bytes 835592 | tf_op jit(solution)/shard_map/ppermute | solution.py:56
  144.8 4.3 %collective-permute-start.10 = (f32[16,2176]{1,0:T(8,128)S(1)}, f32[16,2176]{1,0:T(8,128)S(1)}, u32[]{:S(2)}, u32[]{:S(2)}) collective-permute-start(f32[16,2176]{1,0:T(8,128)S(1)} %slice_select_fusion.3), channel_id=1, source_target_pairs={{0,1},{1,0},{2,3},{3,2},{4,5},{5,4},{6,7},{7,6},{8,9},{9,8},{10,11... | collective-permute-start | bytes 417800 | tf_op jit(solution)/shard_map/ppermute | solution.py:56
  149.1 5.3 %collective-permute-start.11 = (f32[16,2176]{1,0:T(8,128)S(1)}, f32[16,2176]{1,0:T(8,128)S(1)}, u32[]{:S(2)}, u32[]{:S(2)}) collective-permute-start(f32[16,2176]{1,0:T(8,128)S(1)} %select_add_fusion.3), channel_id=1, source_target_pairs={{0,16},{1,17},{2,18},{3,19},{4,20},{5,21},{6,22},{7,23},{8,24},{9,... | collective-permute-start | bytes 417800 | tf_op jit(solution)/shard_map/ppermute | solution.py:59
  154.5 6.1 %collective-permute-start.12 = (f32[16,2176]{1,0:T(8,128)S(1)}, f32[16,2176]{1,0:T(8,128)S(1)}, u32[]{:S(2)}, u32[]{:S(2)}) collective-permute-start(f32[16,2176]{1,0:T(8,128)S(1)} %add.148), channel_id=1, source_target_pairs={{0,128},{1,129},{2,130},{3,131},{4,132},{5,133},{6,134},{7,135},{8... | collective-permute-start | bytes 417800 | tf_op jit(solution)/shard_map/ppermute | solution.py:59
  160.6 9.2 %collective-permute-start.13 = (f32[16,2176]{1,0:T(8,128)S(1)}, f32[16,2176]{1,0:T(8,128)S(1)}, u32[]{:S(2)}, u32[]{:S(2)}) collective-permute-start(f32[16,2176]{1,0:T(8,128)S(1)} %add.149), channel_id=1, source_target_pairs={{0,32},{1,33},{2,34},{3,35},{4,36},{5,37},{6,38},{7,39},{8,40},{9,... | collective-permute-start | bytes 417800 | tf_op jit(solution)/shard_map/ppermute | solution.py:59
  169.8 42.9 %copy-start.13 = (bf16[512,512]{1,0:T(8,128)(2,1)S(1)}, bf16[512,512]{1,0:T(8,128)(2,1)}, u32[]{:S(2)}) copy-start(bf16[512,512]{1,0:T(8,128)(2,1)} %param.18) | copy-start | bytes 1572868
  169.8 8.7 %collective-permute-start.14 = (f32[16,2176]{1,0:T(8,128)S(1)}, f32[16,2176]{1,0:T(8,128)S(1)}, u32[]{:S(2)}, u32[]{:S(2)}) collective-permute-start(f32[16,2176]{1,0:T(8,128)S(1)} %add.150), channel_id=1, source_target_pairs={{0,2},{1,3},{2,0},{3,1},{4,6},{5,7},{6,4},{7,5},{8,10},{9,11},{10,... | collective-permute-start | bytes 417800 | tf_op jit(solution)/shard_map/ppermute | solution.py:59
  178.4 8.2 %collective-permute-start.15 = (f32[16,2176]{1,0:T(8,128)S(1)}, f32[16,2176]{1,0:T(8,128)S(1)}, u32[]{:S(2)}, u32[]{:S(2)}) collective-permute-start(f32[16,2176]{1,0:T(8,128)S(1)} %add.151), channel_id=1, source_target_pairs={{0,1},{1,0},{2,3},{3,2},{4,5},{5,4},{6,7},{7,6},{8,9},{9,8},{10,11... | collective-permute-start | bytes 417800 | tf_op jit(solution)/shard_map/ppermute | solution.py:63
  186.6 6.8 %collective-permute-start.16 = (f32[32,2176]{1,0:T(8,128)S(1)}, f32[32,2176]{1,0:T(8,128)S(1)}, u32[]{:S(2)}, u32[]{:S(2)}) collective-permute-start(f32[32,2176]{1,0:T(8,128)S(1)} %maximum_select_fusion.3), channel_id=1, source_target_pairs={{0,64},{1,65},{2,66},{3,67},{4,68},{5,69},{6,70},{7,71},{8,72},{9,... | collective-permute-start | bytes 835592 | tf_op jit(solution)/shard_map/ppermute | solution.py:63
  193.5 9.0 %collective-permute-start.17 = (f32[64,2176]{1,0:T(8,128)S(1)}, f32[64,2176]{1,0:T(8,128)S(1)}, u32[]{:S(2)}, u32[]{:S(2)}) collective-permute-start(f32[64,2176]{1,0:T(8,128)S(1)} %maximum_select_fusion.2), channel_id=1, source_target_pairs={{0,8},{1,9},{2,10},{3,11},{4,12},{5,13},{6,14},{7,15},{8,0},{9,1},... | collective-permute-start | bytes 1671176 | tf_op jit(solution)/shard_map/ppermute | solution.py:63
  202.5 12.5 %collective-permute-start.18 = (f32[128,2176]{1,0:T(8,128)S(1)}, f32[128,2176]{1,0:T(8,128)S(1)}, u32[]{:S(2)}, u32[]{:S(2)}) collective-permute-start(f32[128,2176]{1,0:T(8,128)S(1)} %maximum_select_fusion.1), channel_id=1, source_target_pairs={{0,4},{1,5},{2,6},{3,7},{4,0},{5,1},{6,2},{7,3},{8,12},{9,13},{10,... | collective-permute-start | bytes 3342344 | tf_op jit(solution)/shard_map/ppermute | solution.py:63
  217.5 2.6 %copy-start.12 = (f32[128,2048]{1,0:T(8,128)S(1)}, f32[128,2048]{1,0:T(8,128)}, u32[]{:S(2)}) copy-start(f32[128,2048]{1,0:T(8,128)} %get-tuple-element.40) | copy-start | bytes 3145732
  217.5 3.9 %copy-start.9 = (f32[512,512]{1,0:T(8,128)S(1)}, f32[512,512]{1,0:T(8,128)}, u32[]{:S(2)}) copy-start(f32[512,512]{1,0:T(8,128)} %fusion.62) | copy-start | bytes 3145732
  220.1 3.4 %copy-start.1 = (bf16[512,512]{1,0:T(8,128)(2,1)S(1)}, bf16[512,512]{1,0:T(8,128)(2,1)}, u32[]{:S(2)}) copy-start(bf16[512,512]{1,0:T(8,128)(2,1)} %param.19) | copy-start | bytes 1572868
  (9 other events, 15.8 us)
Sparse Core Ops, SparseCore 0:
  138.8 52.3 reduce-scatter.1

commit v7 on v6

--- a/solution.py
+++ b/solution.py
@@ -37,7 +37,7 @@
     )
 
 
-HALVING_BITS = (2, 3, 6, 0)
+HALVING_BITS = (2, 6, 3, 0)
 DOUBLING_BITS = (4, 7, 5, 1)
 
 

time: 231 us -> 235 us (1.017)
  waiting for transfers between devices: 102 us -> 112 us
  starting transfers between devices: 54.9 us -> 48.5 us
    ppermute x4, waiting for transfers between devices: 8.14 us -> 25.6 us  [halving_sum(): block = kept + lax.ppermute(sent, axes, pairs)]
    ppermute x2, waiting for transfers between devices: 10.8 us -> 4.48 us  [shifted(): lax.ppermute(value, axis, [(source, source + steps) for source in range(f...]
    ppermute x4, waiting for transfers between devices: 20 us -> 15.9 us  [halving_sum(): got = lax.ppermute(block, axes, pairs)]
    ppermute x4, starting transfers between devices: 15 us -> 11.8 us  [halving_sum(): got = lax.ppermute(block, axes, pairs)]
    ppermute x4, waiting for transfers between devices: 19 us -> 22.1 us  [halving_sum(): lax.ppermute(block, axes, [(i, i ^ 1 << bit) for i in range(count)])]
    ppermute x4, starting transfers between devices: 10.2 us -> 7.47 us  [halving_sum(): lax.ppermute(block, axes, [(i, i ^ 1 << bit) for i in range(count)])]
  transfers between devices with their start and end apart: 21 -> 21, of which waited for: 16 -> 17; matrix products, arithmetic and copies ran while one was open for 11% -> 11% of each run, Pallas kernels for 0% -> 0%
where the time goes in v7:
time: 235 us; the launch traced here: 234 us
  waiting for transfers between devices  112 us (48%)
  starting transfers between devices  48.5 us (21%)
  matrix products  23.1 us (10%)
  local copies, waits for them, and re-layouts  20.5 us (9%)
  other arithmetic  15.3 us (7%)
  between operations  14.6 us (6%)
    ppermute x4, waiting for transfers between devices, halving_sum(): block = kept + lax.ppermute(sent, axes, pairs)  25.6 us
    ppermute x3, waiting for transfers between devices, gather_rep(): lax.ppermute(block, 'rep', [(i, (i + shift) % count) for i in range(count)])  23.8 us
    ppermute x4, waiting for transfers between devices, halving_sum(): lax.ppermute(block, axes, [(i, i ^ 1 << bit) for i in range(count)])  22.1 us
    all_to_all x1, waiting for transfers between devices, shards(): got = lax.all_to_all(sent, 'dom', split_axis=0, concat_axis=0, tiled=True)  17.9 us
    ppermute x4, waiting for transfers between devices, halving_sum(): got = lax.ppermute(block, axes, pairs)  15.9 us
    all_to_all x1, starting transfers between devices, shards(): got = lax.all_to_all(sent, 'dom', split_axis=0, concat_axis=0, tiled=True)  13.2 us
    ppermute x4, starting transfers between devices, halving_sum(): got = lax.ppermute(block, axes, pairs)  11.8 us
    ppermute x4, starting transfers between devices, halving_sum(): lax.ppermute(block, axes, [(i, i ^ 1 << bit) for i in range(count)])  7.47 us
  transfers between devices with their start and end apart: 21, of which 17 were waited for; matrix products, arithmetic and copies ran while one was open for 11% of the time, Pallas kernels for 0%

profile of v7, /device:TPU:1, one launch (start us, length us, event | category | flops | bytes accessed | tf_op | source)
XLA Modules:
  0.0 234.3 jit_solution(15268461058646113574)
XLA Ops:
  13.3 13.2 %all-to-all-start = ((bf16[64,2,2112]{2,1,0:T(2,128)(2,1)}), bf16[64,2,2112]{2,1,0:T(2,128)(2,1)S(1)}, u32[]{:S(2)}, u32[]{:S(2)}) async-start(bf16[64,2,2112]{2,1,0:T(2,128)(2,1)} %reshape.193), calls=%async_computation | async-start | bytes 1114112 | tf_op jit(solution)/shard_map/all_to_all | solution.py:109
  26.6 17.9 %all-to-all-done = bf16[64,2,2112]{2,1,0:T(2,128)(2,1)S(1)} async-done(((bf16[64,2,2112]{2,1,0:T(2,128)(2,1)}), bf16[64,2,2112]{2,1,0:T(2,128)(2,1)S(1)}, u32[]{:S(2)}, u32[]{:S(2)}) %all-to-all-start) | async-done | bytes 540704 | tf_op jit(solution)/shard_map/all_to_all | solution.py:109
  46.2 2.6 %collective-permute-start.2 = (bf16[512,512]{1,0:T(8,128)(2,1)S(1)}, bf16[512,512]{1,0:T(8,128)(2,1)S(1)}, u32[]{:S(2)}, u32[]{:S(2)}) collective-permute-start(bf16[512,512]{1,0:T(8,128)(2,1)S(1)} %convolution_convert_fusion), channel_id=1, source_target_pairs={{0,3},{1,0},{2,1},{3,2},{4,7},{5,4},{6,5},{7,6},{8,11},{9,8},{10,9... | collective-permute-start | bytes 1572872 | tf_op jit(solution)/shard_map/ppermute | solution.py:72
  51.6 19.2 %collective-permute-done.2 = bf16[512,512]{1,0:T(8,128)(2,1)S(1)} collective-permute-done((bf16[512,512]{1,0:T(8,128)(2,1)S(1)}, bf16[512,512]{1,0:T(8,128)(2,1)S(1)}, u32[]{:S(2)}, u32[]{:S(2)}) %collective-permute-start.2) | collective-permute-done | bytes 524320 | tf_op jit(solution)/shard_map/ppermute | solution.py:72
  70.8 4.6 %collective-permute-done = bf16[512,512]{1,0:T(8,128)(2,1)S(1)} collective-permute-done((bf16[512,512]{1,0:T(8,128)(2,1)S(1)}, bf16[512,512]{1,0:T(8,128)(2,1)S(1)}, u32[]{:S(2)}, u32[]{:S(2)}) %collective-permute-start) | collective-permute-done | bytes 524320 | tf_op jit(solution)/shard_map/ppermute | solution.py:72
  77.0 2.3 gather_fusion
  80.3 2.8 %collective-permute-start.3 = (bf16[512,512]{1,0:T(8,128)(2,1)}, bf16[512,512]{1,0:T(8,128)(2,1)}, u32[]{:S(2)}, u32[]{:S(2)}) collective-permute-start(bf16[512,512]{1,0:T(8,128)(2,1)} %get-tuple-element.41), channel_id=1, source_target_pairs={{0,4},{4,8},{8,12},{12,16},{16,20},{20,24},{24,28},{28,32},{32,36}... | collective-permute-start | bytes 1572872 | tf_op jit(solution)/shard_map/ppermute | solution.py:20
  83.1 2.4 %collective-permute-start.4 = (bf16[512,512]{1,0:T(8,128)(2,1)}, bf16[512,512]{1,0:T(8,128)(2,1)}, u32[]{:S(2)}, u32[]{:S(2)}) collective-permute-start(bf16[512,512]{1,0:T(8,128)(2,1)} %get-tuple-element.42), channel_id=1, source_target_pairs={{4,0},{8,4},{12,8},{16,12},{20,16},{24,20},{28,24},{32,28},{36,32}... | collective-permute-start | bytes 1572872 | tf_op jit(solution)/shard_map/ppermute | solution.py:23
  85.6 4.4 %subtract_convert_fusion = (bf16[4,24,128,128]{3,1,2,0:T(8,128)(2,1)}, bf16[4,24,128,128]{3,1,2,0:T(8,128)(2,1)}) fusion(bf16[4,12,128,128]{3,2,1,0:T(8,128)(2,1)S(1)} %copy-done.6, s32[4,12]{1,0:T(4,128)S(1)} %broadcast_subtract_fusion), kind=kOutput, calls=%fused_computation.2 | convolution fusion | flops 44041344 | bytes 7864512 | tf_op jit(solution)/shard_map/tke,tkab->teab/dot_general | solution.py:123
  91.4 2.5 %collective-permute-done.4 = bf16[512,512]{1,0:T(8,128)(2,1)} collective-permute-done((bf16[512,512]{1,0:T(8,128)(2,1)}, bf16[512,512]{1,0:T(8,128)(2,1)}, u32[]{:S(2)}, u32[]{:S(2)}) %collective-permute-start.4) | collective-permute-done | bytes 524320 | tf_op jit(solution)/shard_map/ppermute | solution.py:23
  106.5 2.1 reshape.173
  114.2 2.0 fusion.60
  116.3 2.4 %slice.177 = f32[16,128,512]{2,1,0:T(8,128)} slice(f32[24,128,512]{2,1,0:T(8,128)S(1)} %get-tuple-element.50), slice={[4:20], [0:128], [0:512]} | slice | bytes 8388608 | tf_op jit(solution)/shard_map/slice | solution.py:161
  120.7 2.7 %collective-permute-start.6 = (bf16[512,512]{1,0:T(8,128)(2,1)S(1)}, bf16[512,512]{1,0:T(8,128)(2,1)S(1)}, u32[]{:S(2)}, u32[]{:S(2)}) collective-permute-start(bf16[512,512]{1,0:T(8,128)(2,1)S(1)} %bitcast.81), channel_id=1, source_target_pairs={{4,0},{8,4},{12,8},{16,12},{20,16},{24,20},{28,24},{32,28},{36,32}... | collective-permute-start | bytes 1572872 | tf_op jit(solution)/shard_map/ppermute | solution.py:12
  123.6 2.3 collective-permute-start.8
  127.9 3.5 %collective-permute-done.6 = bf16[512,512]{1,0:T(8,128)(2,1)S(1)} collective-permute-done((bf16[512,512]{1,0:T(8,128)(2,1)S(1)}, bf16[512,512]{1,0:T(8,128)(2,1)S(1)}, u32[]{:S(2)}, u32[]{:S(2)}) %collective-permute-start.6) | collective-permute-done | bytes 524320 | tf_op jit(solution)/shard_map/ppermute | solution.py:12
  131.5 2.4 %fusion.33 = f32[2048,512]{1,0:T(8,128)} fusion(f32[2048,512]{1,0:T(8,128)} %constant_dynamic-update-slice_fusion, bf16[512,512]{1,0:T(8,128)(2,1)S(1)} %collective-permute-done.6), kind=kLoop, calls=%fused_computation.42 | loop fusion | flops 524288 | bytes 2621440 | tf_op jit(solution)/shard_map/scatter-add | solution.py:163
  133.9 9.6 %collective-permute-done.8 = f32[64,2176]{1,0:T(8,128)S(1)} collective-permute-done((f32[64,2176]{1,0:T(8,128)S(1)}, f32[64,2176]{1,0:T(8,128)S(1)}, u32[]{:S(2)}, u32[]{:S(2)}) %collective-permute-start.8) | collective-permute-done | bytes 557088 | tf_op jit(solution)/shard_map/ppermute | solution.py:56
  143.7 7.8 %collective-permute-done.9 = f32[32,2176]{1,0:T(8,128)S(1)} collective-permute-done((f32[32,2176]{1,0:T(8,128)S(1)}, f32[32,2176]{1,0:T(8,128)S(1)}, u32[]{:S(2)}, u32[]{:S(2)}) %collective-permute-start.9) | collective-permute-done | bytes 278560 | tf_op jit(solution)/shard_map/ppermute | solution.py:56
  151.7 8.2 %collective-permute-done.10 = f32[16,2176]{1,0:T(8,128)S(1)} collective-permute-done((f32[16,2176]{1,0:T(8,128)S(1)}, f32[16,2176]{1,0:T(8,128)S(1)}, u32[]{:S(2)}, u32[]{:S(2)}) %collective-permute-start.10) | collective-permute-done | bytes 139296 | tf_op jit(solution)/shard_map/ppermute | solution.py:56
  160.0 8.7 %collective-permute-done.11 = f32[16,2176]{1,0:T(8,128)S(1)} collective-permute-done((f32[16,2176]{1,0:T(8,128)S(1)}, f32[16,2176]{1,0:T(8,128)S(1)}, u32[]{:S(2)}, u32[]{:S(2)}) %collective-permute-start.11) | collective-permute-done | bytes 139296 | tf_op jit(solution)/shard_map/ppermute | solution.py:59
  168.8 2.7 %collective-permute-start.12 = (f32[16,2176]{1,0:T(8,128)S(1)}, f32[16,2176]{1,0:T(8,128)S(1)}, u32[]{:S(2)}, u32[]{:S(2)}) collective-permute-start(f32[16,2176]{1,0:T(8,128)S(1)} %add.148), channel_id=1, source_target_pairs={{0,128},{1,129},{2,130},{3,131},{4,132},{5,133},{6,134},{7,135},{8... | collective-permute-start | bytes 417800 | tf_op jit(solution)/shard_map/ppermute | solution.py:59
  171.5 2.8 %collective-permute-done.12 = f32[16,2176]{1,0:T(8,128)S(1)} collective-permute-done((f32[16,2176]{1,0:T(8,128)S(1)}, f32[16,2176]{1,0:T(8,128)S(1)}, u32[]{:S(2)}, u32[]{:S(2)}) %collective-permute-start.12) | collective-permute-done | bytes 139296 | tf_op jit(solution)/shard_map/ppermute | solution.py:59
  174.3 4.5 %collective-permute-start.13 = (f32[16,2176]{1,0:T(8,128)S(1)}, f32[16,2176]{1,0:T(8,128)S(1)}, u32[]{:S(2)}, u32[]{:S(2)}) collective-permute-start(f32[16,2176]{1,0:T(8,128)S(1)} %add.149), channel_id=1, source_target_pairs={{0,32},{1,33},{2,34},{3,35},{4,36},{5,37},{6,38},{7,39},{8,40},{9,... | collective-permute-start | bytes 417800 | tf_op jit(solution)/shard_map/ppermute | solution.py:59
  178.8 5.2 %collective-permute-done.13 = f32[16,2176]{1,0:T(8,128)S(1)} collective-permute-done((f32[16,2176]{1,0:T(8,128)S(1)}, f32[16,2176]{1,0:T(8,128)S(1)}, u32[]{:S(2)}, u32[]{:S(2)}) %collective-permute-start.13) | collective-permute-done | bytes 139296 | tf_op jit(solution)/shard_map/ppermute | solution.py:59
  184.2 5.4 %collective-permute-done.14 = f32[16,2176]{1,0:T(8,128)S(1)} collective-permute-done((f32[16,2176]{1,0:T(8,128)S(1)}, f32[16,2176]{1,0:T(8,128)S(1)}, u32[]{:S(2)}, u32[]{:S(2)}) %collective-permute-start.14) | collective-permute-done | bytes 139296 | tf_op jit(solution)/shard_map/ppermute | solution.py:59
  190.9 2.7 %collective-permute-done.15 = f32[16,2176]{1,0:T(8,128)S(1)} collective-permute-done((f32[16,2176]{1,0:T(8,128)S(1)}, f32[16,2176]{1,0:T(8,128)S(1)}, u32[]{:S(2)}, u32[]{:S(2)}) %collective-permute-start.15) | collective-permute-done | bytes 139296 | tf_op jit(solution)/shard_map/ppermute | solution.py:63
  193.7 5.4 %collective-permute-done.16 = f32[32,2176]{1,0:T(8,128)S(1)} collective-permute-done((f32[32,2176]{1,0:T(8,128)S(1)}, f32[32,2176]{1,0:T(8,128)S(1)}, u32[]{:S(2)}, u32[]{:S(2)}) %collective-permute-start.16) | collective-permute-done | bytes 278560 | tf_op jit(solution)/shard_map/ppermute | solution.py:63
  200.7 6.9 %collective-permute-done.17 = f32[64,2176]{1,0:T(8,128)S(1)} collective-permute-done((f32[64,2176]{1,0:T(8,128)S(1)}, f32[64,2176]{1,0:T(8,128)S(1)}, u32[]{:S(2)}, u32[]{:S(2)}) %collective-permute-start.17) | collective-permute-done | bytes 557088 | tf_op jit(solution)/shard_map/ppermute | solution.py:63
  207.7 8.9 %collective-permute-start.18 = (f32[128,2176]{1,0:T(8,128)S(1)}, f32[128,2176]{1,0:T(8,128)S(1)}, u32[]{:S(2)}, u32[]{:S(2)}) collective-permute-start(f32[128,2176]{1,0:T(8,128)S(1)} %maximum_select_fusion.1), channel_id=1, source_target_pairs={{0,4},{1,5},{2,6},{3,7},{4,0},{5,1},{6,2},{7,3},{8,12},{9,13},{10,... | collective-permute-start | bytes 3342344 | tf_op jit(solution)/shard_map/ppermute | solution.py:63
  221.4 2.6 %slice.165 = f32[512,512]{1,0:T(8,128)} reshape(f32[128,2048]{1,0:T(8,128)} %get-tuple-element.39) | data formatting | bytes 2097152 | tf_op jit(solution)/shard_map/slice | solution.py:151
  225.3 2.2 add_convert_fusion
  (127 shorter events, 47.0 us)
Async XLA Ops:
  7.2 92.7 %copy-start = (bf16[512,512]{1,0:T(8,128)(2,1)S(1)}, bf16[512,512]{1,0:T(8,128)(2,1)}, u32[]{:S(2)}) copy-start(bf16[512,512]{1,0:T(8,128)(2,1)} %param.19) | copy-start | bytes 1572868
  10.5 16.0 %copy-start.16 = (s32[4,12]{1,0:T(4,128)S(1)}, s32[4,12]{1,0:T(4,128)}, u32[]{:S(2)}) copy-start(s32[4,12]{1,0:T(4,128)} %param.17) | copy-start | bytes 580
  13.3 31.2 %all-to-all-start = ((bf16[64,2,2112]{2,1,0:T(2,128)(2,1)}), bf16[64,2,2112]{2,1,0:T(2,128)(2,1)S(1)}, u32[]{:S(2)}, u32[]{:S(2)}) async-start(bf16[64,2,2112]{2,1,0:T(2,128)(2,1)} %reshape.193), calls=%async_computation | async-start | bytes 1114112 | tf_op jit(solution)/shard_map/all_to_all | solution.py:109
  26.5 198.8 %reduce-scatter.2.cloned.1.call-start = ((), (), s32[]{:S(2)}) async-start(), calls=%async_computation.2 | async-start | bytes 5242880 | tf_op jit(solution)/shard_map/reduce_scatter | solution.py:164
  45.2 4.7 %copy-start.17 = (s32[4,12]{1,0:T(4,128)S(1)}, s32[4,12]{1,0:T(4,128)}, u32[]{:S(2)}) copy-start(s32[4,12]{1,0:T(4,128)} %param.16) | copy-start | bytes 580
  45.2 4.6 %copy-start.15 = (bf16[4,12,128,128]{3,2,1,0:T(8,128)(2,1)S(1)}, bf16[4,12,128,128]{3,2,1,0:T(8,128)(2,1)}, u32[]{:S(2)}) copy-start(bf16[4,12,128,128]{3,2,1,0:T(8,128)(2,1)} %param.15) | copy-start | bytes 4718596
  46.2 43.8 %copy-start.7 = (bf16[512,512]{1,0:T(8,128)(2,1)}, bf16[512,512]{1,0:T(8,128)(2,1)S(1)}, u32[]{:S(2)}) copy-start(bf16[512,512]{1,0:T(8,128)(2,1)S(1)} %convolution_convert_fusion) | copy-start | bytes 1572868
  46.2 24.5 %collective-permute-start.2 = (bf16[512,512]{1,0:T(8,128)(2,1)S(1)}, bf16[512,512]{1,0:T(8,128)(2,1)S(1)}, u32[]{:S(2)}, u32[]{:S(2)}) collective-permute-start(bf16[512,512]{1,0:T(8,128)(2,1)S(1)} %convolution_convert_fusion), channel_id=1, source_target_pairs={{0,3},{1,0},{2,1},{3,2},{4,7},{5,4},{6,5},{7,6},{8,11},{9,8},{10,9... | collective-permute-start | bytes 1572872 | tf_op jit(solution)/shard_map/ppermute | solution.py:72
  48.8 22.0 %collective-permute-start.1 = (bf16[512,512]{1,0:T(8,128)(2,1)S(1)}, bf16[512,512]{1,0:T(8,128)(2,1)S(1)}, u32[]{:S(2)}, u32[]{:S(2)}) collective-permute-start(bf16[512,512]{1,0:T(8,128)(2,1)S(1)} %convolution_convert_fusion), channel_id=1, source_target_pairs={{0,2},{1,3},{2,0},{3,1},{4,6},{5,7},{6,4},{7,5},{8,10},{9,11},{10,... | collective-permute-start | bytes 1572872 | tf_op jit(solution)/shard_map/ppermute | solution.py:72
  49.3 26.1 %collective-permute-start = (bf16[512,512]{1,0:T(8,128)(2,1)S(1)}, bf16[512,512]{1,0:T(8,128)(2,1)S(1)}, u32[]{:S(2)}, u32[]{:S(2)}) collective-permute-start(bf16[512,512]{1,0:T(8,128)(2,1)S(1)} %convolution_convert_fusion), channel_id=1, source_target_pairs={{0,1},{1,2},{2,3},{3,0},{4,5},{5,6},{6,7},{7,4},{8,9},{9,10},{10,1... | collective-permute-start | bytes 1572872 | tf_op jit(solution)/shard_map/ppermute | solution.py:72
  79.2 6.3 %copy-start.6 = (bf16[4,12,128,128]{3,2,1,0:T(8,128)(2,1)S(1)}, bf16[4,12,128,128]{3,2,1,0:T(8,128)(2,1)}, u32[]{:S(2)}) copy-start(bf16[4,12,128,128]{3,2,1,0:T(8,128)(2,1)} %get-tuple-element.34) | copy-start | bytes 4718596
  80.3 11.2 %collective-permute-start.3 = (bf16[512,512]{1,0:T(8,128)(2,1)}, bf16[512,512]{1,0:T(8,128)(2,1)}, u32[]{:S(2)}, u32[]{:S(2)}) collective-permute-start(bf16[512,512]{1,0:T(8,128)(2,1)} %get-tuple-element.41), channel_id=1, source_target_pairs={{0,4},{4,8},{8,12},{12,16},{16,20},{20,24},{24,28},{28,32},{32,36}... | collective-permute-start | bytes 1572872 | tf_op jit(solution)/shard_map/ppermute | solution.py:20
  83.1 10.8 %collective-permute-start.4 = (bf16[512,512]{1,0:T(8,128)(2,1)}, bf16[512,512]{1,0:T(8,128)(2,1)}, u32[]{:S(2)}, u32[]{:S(2)}) collective-permute-start(bf16[512,512]{1,0:T(8,128)(2,1)} %get-tuple-element.42), channel_id=1, source_target_pairs={{4,0},{8,4},{12,8},{16,12},{20,16},{24,20},{28,24},{32,28},{36,32}... | collective-permute-start | bytes 1572872 | tf_op jit(solution)/shard_map/ppermute | solution.py:23
  93.9 2.2 copy-start.2
  110.5 12.8 %collective-permute-start.7 = (f32[128,2176]{1,0:T(8,128)S(1)}, f32[128,2176]{1,0:T(8,128)S(1)}, u32[]{:S(2)}, u32[]{:S(2)}) collective-permute-start(f32[128,2176]{1,0:T(8,128)S(1)} %slice_select_fusion), channel_id=1, source_target_pairs={{0,4},{1,5},{2,6},{3,7},{4,0},{5,1},{6,2},{7,3},{8,12},{9,13},{10,... | collective-permute-start | bytes 3342344 | tf_op jit(solution)/shard_map/ppermute | solution.py:56
  118.8 8.0 %collective-permute-start.5 = (bf16[512,512]{1,0:T(8,128)(2,1)S(1)}, bf16[512,512]{1,0:T(8,128)(2,1)S(1)}, u32[]{:S(2)}, u32[]{:S(2)}) collective-permute-start(bf16[512,512]{1,0:T(8,128)(2,1)S(1)} %bitcast.82), channel_id=1, source_target_pairs={{0,4},{4,8},{8,12},{12,16},{16,20},{20,24},{24,28},{28,32},{32,36}... | collective-permute-start | bytes 1572872 | tf_op jit(solution)/shard_map/ppermute | solution.py:12
  120.7 10.8 %collective-permute-start.6 = (bf16[512,512]{1,0:T(8,128)(2,1)S(1)}, bf16[512,512]{1,0:T(8,128)(2,1)S(1)}, u32[]{:S(2)}, u32[]{:S(2)}) collective-permute-start(bf16[512,512]{1,0:T(8,128)(2,1)S(1)} %bitcast.81), channel_id=1, source_target_pairs={{4,0},{8,4},{12,8},{16,12},{20,16},{24,20},{28,24},{32,28},{36,32}... | collective-permute-start | bytes 1572872 | tf_op jit(solution)/shard_map/ppermute | solution.py:12
  123.6 19.9 %collective-permute-start.8 = (f32[64,2176]{1,0:T(8,128)S(1)}, f32[64,2176]{1,0:T(8,128)S(1)}, u32[]{:S(2)}, u32[]{:S(2)}) collective-permute-start(f32[64,2176]{1,0:T(8,128)S(1)} %slice_select_fusion.1), channel_id=1, source_target_pairs={{0,64},{1,65},{2,66},{3,67},{4,68},{5,69},{6,70},{7,71},{8,72},{9,... | collective-permute-start | bytes 1671176 | tf_op jit(solution)/shard_map/ppermute | solution.py:56
  143.6 7.9 %collective-permute-start.9 = (f32[32,2176]{1,0:T(8,128)S(1)}, f32[32,2176]{1,0:T(8,128)S(1)}, u32[]{:S(2)}, u32[]{:S(2)}) collective-permute-start(f32[32,2176]{1,0:T(8,128)S(1)} %slice_select_fusion.2), channel_id=1, source_target_pairs={{0,8},{1,9},{2,10},{3,11},{4,12},{5,13},{6,14},{7,15},{8,0},{9,1},... | collective-permute-start | bytes 835592 | tf_op jit(solution)/shard_map/ppermute | solution.py:56
  151.6 8.3 %collective-permute-start.10 = (f32[16,2176]{1,0:T(8,128)S(1)}, f32[16,2176]{1,0:T(8,128)S(1)}, u32[]{:S(2)}, u32[]{:S(2)}) collective-permute-start(f32[16,2176]{1,0:T(8,128)S(1)} %slice_select_fusion.3), channel_id=1, source_target_pairs={{0,1},{1,0},{2,3},{3,2},{4,5},{5,4},{6,7},{7,6},{8,9},{9,8},{10,11... | collective-permute-start | bytes 417800 | tf_op jit(solution)/shard_map/ppermute | solution.py:56
  159.9 8.8 %collective-permute-start.11 = (f32[16,2176]{1,0:T(8,128)S(1)}, f32[16,2176]{1,0:T(8,128)S(1)}, u32[]{:S(2)}, u32[]{:S(2)}) collective-permute-start(f32[16,2176]{1,0:T(8,128)S(1)} %select_add_fusion.3), channel_id=1, source_target_pairs={{0,16},{1,17},{2,18},{3,19},{4,20},{5,21},{6,22},{7,23},{8,24},{9,... | collective-permute-start | bytes 417800 | tf_op jit(solution)/shard_map/ppermute | solution.py:59
  168.8 5.5 %collective-permute-start.12 = (f32[16,2176]{1,0:T(8,128)S(1)}, f32[16,2176]{1,0:T(8,128)S(1)}, u32[]{:S(2)}, u32[]{:S(2)}) collective-permute-start(f32[16,2176]{1,0:T(8,128)S(1)} %add.148), channel_id=1, source_target_pairs={{0,128},{1,129},{2,130},{3,131},{4,132},{5,133},{6,134},{7,135},{8... | collective-permute-start | bytes 417800 | tf_op jit(solution)/shard_map/ppermute | solution.py:59
  174.3 9.8 %collective-permute-start.13 = (f32[16,2176]{1,0:T(8,128)S(1)}, f32[16,2176]{1,0:T(8,128)S(1)}, u32[]{:S(2)}, u32[]{:S(2)}) collective-permute-start(f32[16,2176]{1,0:T(8,128)S(1)} %add.149), channel_id=1, source_target_pairs={{0,32},{1,33},{2,34},{3,35},{4,36},{5,37},{6,38},{7,39},{8,40},{9,... | collective-permute-start | bytes 417800 | tf_op jit(solution)/shard_map/ppermute | solution.py:59
  184.1 32.5 %copy-start.13 = (bf16[512,512]{1,0:T(8,128)(2,1)S(1)}, bf16[512,512]{1,0:T(8,128)(2,1)}, u32[]{:S(2)}) copy-start(bf16[512,512]{1,0:T(8,128)(2,1)} %param.18) | copy-start | bytes 1572868
  184.1 5.5 %collective-permute-start.14 = (f32[16,2176]{1,0:T(8,128)S(1)}, f32[16,2176]{1,0:T(8,128)S(1)}, u32[]{:S(2)}, u32[]{:S(2)}) collective-permute-start(f32[16,2176]{1,0:T(8,128)S(1)} %add.150), channel_id=1, source_target_pairs={{0,2},{1,3},{2,0},{3,1},{4,6},{5,7},{6,4},{7,5},{8,10},{9,11},{10,... | collective-permute-start | bytes 417800 | tf_op jit(solution)/shard_map/ppermute | solution.py:59
  189.6 4.0 %collective-permute-start.15 = (f32[16,2176]{1,0:T(8,128)S(1)}, f32[16,2176]{1,0:T(8,128)S(1)}, u32[]{:S(2)}, u32[]{:S(2)}) collective-permute-start(f32[16,2176]{1,0:T(8,128)S(1)} %add.151), channel_id=1, source_target_pairs={{0,1},{1,0},{2,3},{3,2},{4,5},{5,4},{6,7},{7,6},{8,9},{9,8},{10,11... | collective-permute-start | bytes 417800 | tf_op jit(solution)/shard_map/ppermute | solution.py:63
  193.6 5.5 %collective-permute-start.16 = (f32[32,2176]{1,0:T(8,128)S(1)}, f32[32,2176]{1,0:T(8,128)S(1)}, u32[]{:S(2)}, u32[]{:S(2)}) collective-permute-start(f32[32,2176]{1,0:T(8,128)S(1)} %maximum_select_fusion.3), channel_id=1, source_target_pairs={{0,8},{1,9},{2,10},{3,11},{4,12},{5,13},{6,14},{7,15},{8,0},{9,1},... | collective-permute-start | bytes 835592 | tf_op jit(solution)/shard_map/ppermute | solution.py:63
  199.2 8.5 %collective-permute-start.17 = (f32[64,2176]{1,0:T(8,128)S(1)}, f32[64,2176]{1,0:T(8,128)S(1)}, u32[]{:S(2)}, u32[]{:S(2)}) collective-permute-start(f32[64,2176]{1,0:T(8,128)S(1)} %maximum_select_fusion.2), channel_id=1, source_target_pairs={{0,64},{1,65},{2,66},{3,67},{4,68},{5,69},{6,70},{7,71},{8,72},{9,... | collective-permute-start | bytes 1671176 | tf_op jit(solution)/shard_map/ppermute | solution.py:63
  207.7 11.2 %collective-permute-start.18 = (f32[128,2176]{1,0:T(8,128)S(1)}, f32[128,2176]{1,0:T(8,128)S(1)}, u32[]{:S(2)}, u32[]{:S(2)}) collective-permute-start(f32[128,2176]{1,0:T(8,128)S(1)} %maximum_select_fusion.1), channel_id=1, source_target_pairs={{0,4},{1,5},{2,6},{3,7},{4,0},{5,1},{6,2},{7,3},{8,12},{9,13},{10,... | collective-permute-start | bytes 3342344 | tf_op jit(solution)/shard_map/ppermute | solution.py:63
  221.4 2.6 %copy-start.12 = (f32[128,2048]{1,0:T(8,128)S(1)}, f32[128,2048]{1,0:T(8,128)}, u32[]{:S(2)}) copy-start(f32[128,2048]{1,0:T(8,128)} %get-tuple-element.40) | copy-start | bytes 3145732
  221.4 3.9 %copy-start.9 = (f32[512,512]{1,0:T(8,128)S(1)}, f32[512,512]{1,0:T(8,128)}, u32[]{:S(2)}) copy-start(f32[512,512]{1,0:T(8,128)} %fusion.62) | copy-start | bytes 3145732
  224.0 3.4 %copy-start.1 = (bf16[512,512]{1,0:T(8,128)(2,1)S(1)}, bf16[512,512]{1,0:T(8,128)(2,1)}, u32[]{:S(2)}) copy-start(bf16[512,512]{1,0:T(8,128)(2,1)} %param.19) | copy-start | bytes 1572868
  (9 other events, 15.8 us)
Sparse Core Ops, SparseCore 0:
  134.0 51.2 reduce-scatter.1

commit v8 on v6

--- a/solution.py
+++ b/solution.py
@@ -68,10 +68,21 @@
 def gather_rep(block):
     count = lax.axis_size("rep")
     place = lax.axis_index("rep")
-    parts = [block] + [
-        lax.ppermute(block, "rep", [(i, (i + shift) % count) for i in range(count)])
-        for shift in range(1, count)
-    ]
+    if count == 4:
+        ahead = [(i, (i + 1) % count) for i in range(count)]
+        behind = [(i, (i - 1) % count) for i in range(count)]
+        from_prev = lax.ppermute(block, "rep", ahead)
+        from_next = lax.ppermute(block, "rep", behind)
+        half = block.shape[0] // 2
+        far = jnp.concatenate(
+            [lax.ppermute(from_prev[:half], "rep", ahead), lax.ppermute(from_next[half:], "rep", behind)]
+        )
+        parts = [block, from_prev, far, from_next]
+    else:
+        parts = [block] + [
+            lax.ppermute(block, "rep", [(i, (i + shift) % count) for i in range(count)])
+            for shift in range(1, count)
+        ]
     source = (place - jnp.arange(count)) % count
     return jnp.stack(parts)[source].reshape(count * block.shape[0], *block.shape[1:])
 

time: 231 us -> 230 us (level)
  blocking collectives: 0 us -> 31 us
  waiting for transfers between devices: 102 us -> 81 us
  starting transfers between devices: 54.9 us -> 42.4 us
    all_to_all x0 -> x1, blocking collectives: none -> 31 us  [shards(): got = lax.all_to_all(sent, 'dom', split_axis=0, concat_axis=0, tiled=True)]
    all_to_all x1 -> x0, waiting for transfers between devices: 17.9 us -> none  [shards(): got = lax.all_to_all(sent, 'dom', split_axis=0, concat_axis=0, tiled=True)]
    all_to_all x1 -> x0, starting transfers between devices: 13.2 us -> none  [shards(): got = lax.all_to_all(sent, 'dom', split_axis=0, concat_axis=0, tiled=True)]
    ppermute x3 -> x4, waiting for transfers between devices: 23.8 us -> 16.6 us  [the longest x1 9.19 us: gather_rep(): from_next = lax.ppermute(block, 'rep', behind)]
    ppermute x4, waiting for transfers between devices: 19 us -> 22.6 us  [halving_sum(): lax.ppermute(block, axes, [(i, i ^ 1 << bit) for i in range(count)])]
    ppermute x4, starting transfers between devices: 15 us -> 12.3 us  [halving_sum(): got = lax.ppermute(block, axes, pairs)]
    ppermute x4, starting transfers between devices: 10.2 us -> 7.53 us  [halving_sum(): lax.ppermute(block, axes, [(i, i ^ 1 << bit) for i in range(count)])]
    ppermute x3 -> x4, starting transfers between devices: 3.68 us -> 6.13 us  [the longest x1 3.49 us: gather_rep(): lax.ppermute(from_next[half:], 'rep', behind)]
  transfers between devices with their start and end apart: 21 -> 21, of which waited for: 16 -> 17; matrix products, arithmetic and copies ran while one was open for 11% -> 12% of each run, Pallas kernels for 0% -> 0%
where the time goes in v8:
time: 230 us; the launch traced here: 229 us
  waiting for transfers between devices  81 us (35%)
  starting transfers between devices  42.4 us (18%)
  blocking collectives  31 us (13%)
  matrix products  23.1 us (10%)
  local copies, waits for them, and re-layouts  20.7 us (9%)
  other arithmetic  16.4 us (7%)
  between operations  14.6 us (6%)
    all_to_all x1, blocking collectives, shards(): got = lax.all_to_all(sent, 'dom', split_axis=0, concat_axis=0, tiled=True)  31 us
    ppermute x4, waiting for transfers between devices, halving_sum(): lax.ppermute(block, axes, [(i, i ^ 1 << bit) for i in range(count)])  22.6 us
    ppermute x4, waiting for transfers between devices, halving_sum(): got = lax.ppermute(block, axes, pairs)  21.5 us
    ppermute x4, starting transfers between devices, halving_sum(): got = lax.ppermute(block, axes, pairs)  12.3 us
    ppermute x1, waiting for transfers between devices, gather_rep(): from_next = lax.ppermute(block, 'rep', behind)  9.19 us
    ppermute x4, waiting for transfers between devices, halving_sum(): block = kept + lax.ppermute(sent, axes, pairs)  8.97 us
    ppermute x2, waiting for transfers between devices, shifted(): lax.ppermute(value, axis, [(source, source + steps) for source in range(f...  8.82 us
    ppermute x4, starting transfers between devices, halving_sum(): lax.ppermute(block, axes, [(i, i ^ 1 << bit) for i in range(count)])  7.53 us
  transfers between devices with their start and end apart: 21, of which 17 were waited for; matrix products, arithmetic and copies ran while one was open for 12% of the time, Pallas kernels for 0%

profile of v8, /device:TPU:1, one launch (start us, length us, event | category | flops | bytes accessed | tf_op | source)
XLA Modules:
  0.0 229.1 jit_solution(16219250848016641434)
XLA Ops:
  12.6 31.0 %all_to_all.12 = bf16[64,2,2112]{2,1,0:T(2,128)(2,1)S(1)} all-to-all(bf16[64,2,2112]{2,1,0:T(2,128)(2,1)S(1)} %reshape.193), channel_id=1, replica_groups=mesh['dom'=64,'rep'=4] {'dom'}, dimensions={0} | all-to-all | bytes 1081344 | tf_op jit(solution)/shard_map/all_to_all | solution.py:120
  45.2 2.6 %collective-permute-start.2 = (bf16[512,512]{1,0:T(8,128)(2,1)S(1)}, bf16[512,512]{1,0:T(8,128)(2,1)S(1)}, u32[]{:S(2)}, u32[]{:S(2)}) collective-permute-start(bf16[512,512]{1,0:T(8,128)(2,1)S(1)} %convolution_convert_fusion), channel_id=1, source_target_pairs={{0,3},{1,0},{2,1},{3,2},{4,7},{5,4},{6,5},{7,6},{8,11},{9,8},{10,9... | collective-permute-start | bytes 1572872 | tf_op jit(solution)/shard_map/ppermute | solution.py:75
  49.5 9.2 %collective-permute-done.2 = bf16[512,512]{1,0:T(8,128)(2,1)S(1)} collective-permute-done((bf16[512,512]{1,0:T(8,128)(2,1)S(1)}, bf16[512,512]{1,0:T(8,128)(2,1)S(1)}, u32[]{:S(2)}, u32[]{:S(2)}) %collective-permute-start.2) | collective-permute-done | bytes 524320 | tf_op jit(solution)/shard_map/ppermute | solution.py:75
  58.7 3.5 %collective-permute-start.3 = (bf16[256,512]{1,0:T(8,128)(2,1)S(1)}, bf16[256,512]{1,0:T(8,128)(2,1)S(1)}, u32[]{:S(2)}, u32[]{:S(2)}) collective-permute-start(bf16[256,512]{1,0:T(8,128)(2,1)S(1)} %slice.184), channel_id=1, source_target_pairs={{0,3},{1,0},{2,1},{3,2},{4,7},{5,4},{6,5},{7,6},{8,11},{9,8},{10,9... | collective-permute-start | bytes 786440 | tf_op jit(solution)/shard_map/ppermute | solution.py:78
  63.3 3.3 %collective-permute-done.3 = bf16[256,512]{1,0:T(8,128)(2,1)S(1)} collective-permute-done((bf16[256,512]{1,0:T(8,128)(2,1)S(1)}, bf16[256,512]{1,0:T(8,128)(2,1)S(1)}, u32[]{:S(2)}, u32[]{:S(2)}) %collective-permute-start.3) | collective-permute-done | bytes 262176 | tf_op jit(solution)/shard_map/ppermute | solution.py:78
  66.6 4.2 %collective-permute-done.1 = bf16[256,512]{1,0:T(8,128)(2,1)S(1)} collective-permute-done((bf16[256,512]{1,0:T(8,128)(2,1)S(1)}, bf16[256,512]{1,0:T(8,128)(2,1)S(1)}, u32[]{:S(2)}, u32[]{:S(2)}) %collective-permute-start.1) | collective-permute-done | bytes 262176 | tf_op jit(solution)/shard_map/ppermute | solution.py:78
  70.8 2.7 %pad_maximum_fusion.1 = bf16[4,512,512]{2,1,0:T(8,128)(2,1)} fusion(bf16[1,512,512]{2,1,0:T(8,128)(2,1)S(1)} %bitcast.82, bf16[1,512,512]{2,1,0:T(8,128)(2,1)S(1)} %maximum_bitcast_fusion.1, bf16[1,512,512]{2,1,0:T(8,128)(2,1)} %bitcast.4, bf16[1,512,512]{2,1,0:T(8,128)(2,1)S(1)} %bitcast.75), kind=kLoop, calls=%fused_computation.16 | loop fusion | flops 3145728 | bytes 4194304 | tf_op jit(solution)/shard_map/stack | solution.py:87
  73.5 2.3 gather_fusion
  76.8 4.2 %collective-permute-start.4 = (bf16[512,512]{1,0:T(8,128)(2,1)}, bf16[512,512]{1,0:T(8,128)(2,1)}, u32[]{:S(2)}, u32[]{:S(2)}) collective-permute-start(bf16[512,512]{1,0:T(8,128)(2,1)} %get-tuple-element.41), channel_id=1, source_target_pairs={{0,4},{4,8},{8,12},{12,16},{16,20},{20,24},{24,28},{28,32},{32,36}... | collective-permute-start | bytes 1572872 | tf_op jit(solution)/shard_map/ppermute | solution.py:20
  80.9 2.4 %collective-permute-start.5 = (bf16[512,512]{1,0:T(8,128)(2,1)}, bf16[512,512]{1,0:T(8,128)(2,1)}, u32[]{:S(2)}, u32[]{:S(2)}) collective-permute-start(bf16[512,512]{1,0:T(8,128)(2,1)} %get-tuple-element.42), channel_id=1, source_target_pairs={{4,0},{8,4},{12,8},{16,12},{20,16},{24,20},{28,24},{32,28},{36,32}... | collective-permute-start | bytes 1572872 | tf_op jit(solution)/shard_map/ppermute | solution.py:23
  83.4 4.4 %subtract_convert_fusion = (bf16[4,24,128,128]{3,1,2,0:T(8,128)(2,1)}, bf16[4,24,128,128]{3,1,2,0:T(8,128)(2,1)}) fusion(bf16[4,12,128,128]{3,2,1,0:T(8,128)(2,1)S(1)} %copy-done.6, s32[4,12]{1,0:T(4,128)S(1)} %broadcast_subtract_fusion), kind=kOutput, calls=%fused_computation.2 | convolution fusion | flops 44041344 | bytes 7864512 | tf_op jit(solution)/shard_map/tke,tkab->teab/dot_general | solution.py:134
  89.3 2.5 %collective-permute-done.5 = bf16[512,512]{1,0:T(8,128)(2,1)} collective-permute-done((bf16[512,512]{1,0:T(8,128)(2,1)}, bf16[512,512]{1,0:T(8,128)(2,1)}, u32[]{:S(2)}, u32[]{:S(2)}) %collective-permute-start.5) | collective-permute-done | bytes 524320 | tf_op jit(solution)/shard_map/ppermute | solution.py:23
  114.1 2.4 %slice.187 = f32[16,128,512]{2,1,0:T(8,128)} slice(f32[24,128,512]{2,1,0:T(8,128)S(1)} %get-tuple-element.50), slice={[4:20], [0:128], [0:512]} | slice | bytes 8388608 | tf_op jit(solution)/shard_map/slice | solution.py:172
  118.5 2.7 %collective-permute-start.7 = (bf16[512,512]{1,0:T(8,128)(2,1)S(1)}, bf16[512,512]{1,0:T(8,128)(2,1)S(1)}, u32[]{:S(2)}, u32[]{:S(2)}) collective-permute-start(bf16[512,512]{1,0:T(8,128)(2,1)S(1)} %bitcast.83), channel_id=1, source_target_pairs={{4,0},{8,4},{12,8},{16,12},{20,16},{24,20},{28,24},{32,28},{36,32}... | collective-permute-start | bytes 1572872 | tf_op jit(solution)/shard_map/ppermute | solution.py:12
  126.5 7.0 %collective-permute-done.7 = bf16[512,512]{1,0:T(8,128)(2,1)S(1)} collective-permute-done((bf16[512,512]{1,0:T(8,128)(2,1)S(1)}, bf16[512,512]{1,0:T(8,128)(2,1)S(1)}, u32[]{:S(2)}, u32[]{:S(2)}) %collective-permute-start.7) | collective-permute-done | bytes 524320 | tf_op jit(solution)/shard_map/ppermute | solution.py:12
  133.5 2.4 %fusion.33 = f32[2048,512]{1,0:T(8,128)} fusion(f32[2048,512]{1,0:T(8,128)} %constant_dynamic-update-slice_fusion, bf16[512,512]{1,0:T(8,128)(2,1)S(1)} %collective-permute-done.7), kind=kLoop, calls=%fused_computation.42 | loop fusion | flops 524288 | bytes 2621440 | tf_op jit(solution)/shard_map/scatter-add | solution.py:174
  136.9 2.9 %collective-permute-start.10 = (f32[32,2176]{1,0:T(8,128)S(1)}, f32[32,2176]{1,0:T(8,128)S(1)}, u32[]{:S(2)}, u32[]{:S(2)}) collective-permute-start(f32[32,2176]{1,0:T(8,128)S(1)} %slice_select_fusion.2), channel_id=1, source_target_pairs={{0,64},{1,65},{2,66},{3,67},{4,68},{5,69},{6,70},{7,71},{8,72},{9,... | collective-permute-start | bytes 835592 | tf_op jit(solution)/shard_map/ppermute | solution.py:56
  139.7 3.9 %collective-permute-done.10 = f32[32,2176]{1,0:T(8,128)S(1)} collective-permute-done((f32[32,2176]{1,0:T(8,128)S(1)}, f32[32,2176]{1,0:T(8,128)S(1)}, u32[]{:S(2)}, u32[]{:S(2)}) %collective-permute-start.10) | collective-permute-done | bytes 278560 | tf_op jit(solution)/shard_map/ppermute | solution.py:56
  143.8 4.2 %collective-permute-done.11 = f32[16,2176]{1,0:T(8,128)S(1)} collective-permute-done((f32[16,2176]{1,0:T(8,128)S(1)}, f32[16,2176]{1,0:T(8,128)S(1)}, u32[]{:S(2)}, u32[]{:S(2)}) %collective-permute-start.11) | collective-permute-done | bytes 139296 | tf_op jit(solution)/shard_map/ppermute | solution.py:56
  148.1 2.2 collective-permute-start.12
  150.2 4.6 %collective-permute-done.12 = f32[16,2176]{1,0:T(8,128)S(1)} collective-permute-done((f32[16,2176]{1,0:T(8,128)S(1)}, f32[16,2176]{1,0:T(8,128)S(1)}, u32[]{:S(2)}, u32[]{:S(2)}) %collective-permute-start.12) | collective-permute-done | bytes 139296 | tf_op jit(solution)/shard_map/ppermute | solution.py:59
  154.9 2.1 collective-permute-start.13
  157.0 3.4 %collective-permute-done.13 = f32[16,2176]{1,0:T(8,128)S(1)} collective-permute-done((f32[16,2176]{1,0:T(8,128)S(1)}, f32[16,2176]{1,0:T(8,128)S(1)}, u32[]{:S(2)}, u32[]{:S(2)}) %collective-permute-start.13) | collective-permute-done | bytes 139296 | tf_op jit(solution)/shard_map/ppermute | solution.py:59
  160.4 3.1 %collective-permute-start.14 = (f32[16,2176]{1,0:T(8,128)S(1)}, f32[16,2176]{1,0:T(8,128)S(1)}, u32[]{:S(2)}, u32[]{:S(2)}) collective-permute-start(f32[16,2176]{1,0:T(8,128)S(1)} %add.149), channel_id=1, source_target_pairs={{0,32},{1,33},{2,34},{3,35},{4,36},{5,37},{6,38},{7,39},{8,40},{9,... | collective-permute-start | bytes 417800 | tf_op jit(solution)/shard_map/ppermute | solution.py:59
  163.6 5.8 %collective-permute-done.14 = f32[16,2176]{1,0:T(8,128)S(1)} collective-permute-done((f32[16,2176]{1,0:T(8,128)S(1)}, f32[16,2176]{1,0:T(8,128)S(1)}, u32[]{:S(2)}, u32[]{:S(2)}) %collective-permute-start.14) | collective-permute-done | bytes 139296 | tf_op jit(solution)/shard_map/ppermute | solution.py:59
  169.5 8.8 %collective-permute-done.15 = f32[16,2176]{1,0:T(8,128)S(1)} collective-permute-done((f32[16,2176]{1,0:T(8,128)S(1)}, f32[16,2176]{1,0:T(8,128)S(1)}, u32[]{:S(2)}, u32[]{:S(2)}) %collective-permute-start.15) | collective-permute-done | bytes 139296 | tf_op jit(solution)/shard_map/ppermute | solution.py:59
  178.4 8.8 %collective-permute-done.16 = f32[16,2176]{1,0:T(8,128)S(1)} collective-permute-done((f32[16,2176]{1,0:T(8,128)S(1)}, f32[16,2176]{1,0:T(8,128)S(1)}, u32[]{:S(2)}, u32[]{:S(2)}) %collective-permute-start.16) | collective-permute-done | bytes 139296 | tf_op jit(solution)/shard_map/ppermute | solution.py:63
  188.7 4.4 %collective-permute-done.17 = f32[32,2176]{1,0:T(8,128)S(1)} collective-permute-done((f32[32,2176]{1,0:T(8,128)S(1)}, f32[32,2176]{1,0:T(8,128)S(1)}, u32[]{:S(2)}, u32[]{:S(2)}) %collective-permute-start.17) | collective-permute-done | bytes 278560 | tf_op jit(solution)/shard_map/ppermute | solution.py:63
  194.2 7.4 %collective-permute-done.18 = f32[64,2176]{1,0:T(8,128)S(1)} collective-permute-done((f32[64,2176]{1,0:T(8,128)S(1)}, f32[64,2176]{1,0:T(8,128)S(1)}, u32[]{:S(2)}, u32[]{:S(2)}) %collective-permute-start.18) | collective-permute-done | bytes 557088 | tf_op jit(solution)/shard_map/ppermute | solution.py:63
  201.6 9.7 %collective-permute-start.19 = (f32[128,2176]{1,0:T(8,128)S(1)}, f32[128,2176]{1,0:T(8,128)S(1)}, u32[]{:S(2)}, u32[]{:S(2)}) collective-permute-start(f32[128,2176]{1,0:T(8,128)S(1)} %maximum_select_fusion.1), channel_id=1, source_target_pairs={{0,4},{1,5},{2,6},{3,7},{4,0},{5,1},{6,2},{7,3},{8,12},{9,13},{10,... | collective-permute-start | bytes 3342344 | tf_op jit(solution)/shard_map/ppermute | solution.py:63
  216.2 2.6 %slice.173 = f32[512,512]{1,0:T(8,128)} reshape(f32[128,2048]{1,0:T(8,128)} %get-tuple-element.39) | data formatting | bytes 2097152 | tf_op jit(solution)/shard_map/slice | solution.py:162
  220.1 2.2 add_convert_fusion
  (131 shorter events, 51.9 us)
Async XLA Ops:
  7.2 90.5 %copy-start = (bf16[512,512]{1,0:T(8,128)(2,1)S(1)}, bf16[512,512]{1,0:T(8,128)(2,1)}, u32[]{:S(2)}) copy-start(bf16[512,512]{1,0:T(8,128)(2,1)} %param.19) | copy-start | bytes 1572868
  7.2 212.9 %reduce-scatter.2.cloned.1.call-start = ((), (), s32[]{:S(2)}) async-start(), calls=%async_computation.2 | async-start | bytes 5242880 | tf_op jit(solution)/shard_map/reduce_scatter | solution.py:175
  44.2 3.5 %copy-start.16 = (s32[4,12]{1,0:T(4,128)S(1)}, s32[4,12]{1,0:T(4,128)}, u32[]{:S(2)}) copy-start(s32[4,12]{1,0:T(4,128)} %param.17) | copy-start | bytes 580
  44.3 3.6 %copy-start.15 = (bf16[4,12,128,128]{3,2,1,0:T(8,128)(2,1)S(1)}, bf16[4,12,128,128]{3,2,1,0:T(8,128)(2,1)}, u32[]{:S(2)}) copy-start(bf16[4,12,128,128]{3,2,1,0:T(8,128)(2,1)} %param.15) | copy-start | bytes 4718596
  45.2 42.6 %copy-start.7 = (bf16[512,512]{1,0:T(8,128)(2,1)}, bf16[512,512]{1,0:T(8,128)(2,1)S(1)}, u32[]{:S(2)}) copy-start(bf16[512,512]{1,0:T(8,128)(2,1)S(1)} %convolution_convert_fusion) | copy-start | bytes 1572868
  45.2 18.1 %copy-start.17 = (s32[4,12]{1,0:T(4,128)S(1)}, s32[4,12]{1,0:T(4,128)}, u32[]{:S(2)}) copy-start(s32[4,12]{1,0:T(4,128)} %param.16) | copy-start | bytes 580
  45.2 13.5 %collective-permute-start.2 = (bf16[512,512]{1,0:T(8,128)(2,1)S(1)}, bf16[512,512]{1,0:T(8,128)(2,1)S(1)}, u32[]{:S(2)}, u32[]{:S(2)}) collective-permute-start(bf16[512,512]{1,0:T(8,128)(2,1)S(1)} %convolution_convert_fusion), channel_id=1, source_target_pairs={{0,3},{1,0},{2,1},{3,2},{4,7},{5,4},{6,5},{7,6},{8,11},{9,8},{10,9... | collective-permute-start | bytes 1572872 | tf_op jit(solution)/shard_map/ppermute | solution.py:75
  47.8 14.4 %collective-permute-start = (bf16[512,512]{1,0:T(8,128)(2,1)S(1)}, bf16[512,512]{1,0:T(8,128)(2,1)}, u32[]{:S(2)}, u32[]{:S(2)}) collective-permute-start(bf16[512,512]{1,0:T(8,128)(2,1)S(1)} %convolution_convert_fusion), channel_id=1, source_target_pairs={{0,1},{1,2},{2,3},{3,0},{4,5},{5,6},{6,7},{7,4},{8,9},{9,10},{10,1... | collective-permute-start | bytes 1572872 | tf_op jit(solution)/shard_map/ppermute | solution.py:74
  58.7 7.9 %collective-permute-start.3 = (bf16[256,512]{1,0:T(8,128)(2,1)S(1)}, bf16[256,512]{1,0:T(8,128)(2,1)S(1)}, u32[]{:S(2)}, u32[]{:S(2)}) collective-permute-start(bf16[256,512]{1,0:T(8,128)(2,1)S(1)} %slice.184), channel_id=1, source_target_pairs={{0,3},{1,0},{2,1},{3,2},{4,7},{5,4},{6,5},{7,6},{8,11},{9,8},{10,9... | collective-permute-start | bytes 786440 | tf_op jit(solution)/shard_map/ppermute | solution.py:78
  63.2 7.6 %collective-permute-start.1 = (bf16[256,512]{1,0:T(8,128)(2,1)S(1)}, bf16[256,512]{1,0:T(8,128)(2,1)S(1)}, u32[]{:S(2)}, u32[]{:S(2)}) collective-permute-start(bf16[256,512]{1,0:T(8,128)(2,1)S(1)} %slice.183), channel_id=1, source_target_pairs={{0,1},{1,2},{2,3},{3,0},{4,5},{5,6},{6,7},{7,4},{8,9},{9,10},{10,1... | collective-permute-start | bytes 786440 | tf_op jit(solution)/shard_map/ppermute | solution.py:78
  75.7 7.6 %copy-start.6 = (bf16[4,12,128,128]{3,2,1,0:T(8,128)(2,1)S(1)}, bf16[4,12,128,128]{3,2,1,0:T(8,128)(2,1)}, u32[]{:S(2)}) copy-start(bf16[4,12,128,128]{3,2,1,0:T(8,128)(2,1)} %get-tuple-element.34) | copy-start | bytes 4718596
  76.8 12.5 %collective-permute-start.4 = (bf16[512,512]{1,0:T(8,128)(2,1)}, bf16[512,512]{1,0:T(8,128)(2,1)}, u32[]{:S(2)}, u32[]{:S(2)}) collective-permute-start(bf16[512,512]{1,0:T(8,128)(2,1)} %get-tuple-element.41), channel_id=1, source_target_pairs={{0,4},{4,8},{8,12},{12,16},{16,20},{20,24},{24,28},{28,32},{32,36}... | collective-permute-start | bytes 1572872 | tf_op jit(solution)/shard_map/ppermute | solution.py:20
  80.9 10.8 %collective-permute-start.5 = (bf16[512,512]{1,0:T(8,128)(2,1)}, bf16[512,512]{1,0:T(8,128)(2,1)}, u32[]{:S(2)}, u32[]{:S(2)}) collective-permute-start(bf16[512,512]{1,0:T(8,128)(2,1)} %get-tuple-element.42), channel_id=1, source_target_pairs={{4,0},{8,4},{12,8},{16,12},{20,16},{24,20},{28,24},{32,28},{36,32}... | collective-permute-start | bytes 1572872 | tf_op jit(solution)/shard_map/ppermute | solution.py:23
  91.8 2.2 copy-start.2
  108.4 12.8 %collective-permute-start.8 = (f32[128,2176]{1,0:T(8,128)S(1)}, f32[128,2176]{1,0:T(8,128)S(1)}, u32[]{:S(2)}, u32[]{:S(2)}) collective-permute-start(f32[128,2176]{1,0:T(8,128)S(1)} %slice_select_fusion), channel_id=1, source_target_pairs={{0,4},{1,5},{2,6},{3,7},{4,0},{5,1},{6,2},{7,3},{8,12},{9,13},{10,... | collective-permute-start | bytes 3342344 | tf_op jit(solution)/shard_map/ppermute | solution.py:56
  116.6 8.8 %collective-permute-start.6 = (bf16[512,512]{1,0:T(8,128)(2,1)S(1)}, bf16[512,512]{1,0:T(8,128)(2,1)S(1)}, u32[]{:S(2)}, u32[]{:S(2)}) collective-permute-start(bf16[512,512]{1,0:T(8,128)(2,1)S(1)} %bitcast.84), channel_id=1, source_target_pairs={{0,4},{4,8},{8,12},{12,16},{16,20},{20,24},{24,28},{28,32},{32,36}... | collective-permute-start | bytes 1572872 | tf_op jit(solution)/shard_map/ppermute | solution.py:12
  118.5 15.0 %collective-permute-start.7 = (bf16[512,512]{1,0:T(8,128)(2,1)S(1)}, bf16[512,512]{1,0:T(8,128)(2,1)S(1)}, u32[]{:S(2)}, u32[]{:S(2)}) collective-permute-start(bf16[512,512]{1,0:T(8,128)(2,1)S(1)} %bitcast.83), channel_id=1, source_target_pairs={{4,0},{8,4},{12,8},{16,12},{20,16},{24,20},{28,24},{32,28},{36,32}... | collective-permute-start | bytes 1572872 | tf_op jit(solution)/shard_map/ppermute | solution.py:12
  121.4 15.3 %collective-permute-start.9 = (f32[64,2176]{1,0:T(8,128)S(1)}, f32[64,2176]{1,0:T(8,128)S(1)}, u32[]{:S(2)}, u32[]{:S(2)}) collective-permute-start(f32[64,2176]{1,0:T(8,128)S(1)} %slice_select_fusion.1), channel_id=1, source_target_pairs={{0,8},{1,9},{2,10},{3,11},{4,12},{5,13},{6,14},{7,15},{8,0},{9,1},... | collective-permute-start | bytes 1671176 | tf_op jit(solution)/shard_map/ppermute | solution.py:56
  136.9 6.8 %collective-permute-start.10 = (f32[32,2176]{1,0:T(8,128)S(1)}, f32[32,2176]{1,0:T(8,128)S(1)}, u32[]{:S(2)}, u32[]{:S(2)}) collective-permute-start(f32[32,2176]{1,0:T(8,128)S(1)} %slice_select_fusion.2), channel_id=1, source_target_pairs={{0,64},{1,65},{2,66},{3,67},{4,68},{5,69},{6,70},{7,71},{8,72},{9,... | collective-permute-start | bytes 835592 | tf_op jit(solution)/shard_map/ppermute | solution.py:56
  143.7 4.3 %collective-permute-start.11 = (f32[16,2176]{1,0:T(8,128)S(1)}, f32[16,2176]{1,0:T(8,128)S(1)}, u32[]{:S(2)}, u32[]{:S(2)}) collective-permute-start(f32[16,2176]{1,0:T(8,128)S(1)} %slice_select_fusion.3), channel_id=1, source_target_pairs={{0,1},{1,0},{2,3},{3,2},{4,5},{5,4},{6,7},{7,6},{8,9},{9,8},{10,11... | collective-permute-start | bytes 417800 | tf_op jit(solution)/shard_map/ppermute | solution.py:56
  148.1 6.8 %collective-permute-start.12 = (f32[16,2176]{1,0:T(8,128)S(1)}, f32[16,2176]{1,0:T(8,128)S(1)}, u32[]{:S(2)}, u32[]{:S(2)}) collective-permute-start(f32[16,2176]{1,0:T(8,128)S(1)} %select_add_fusion.3), channel_id=1, source_target_pairs={{0,16},{1,17},{2,18},{3,19},{4,20},{5,21},{6,22},{7,23},{8,24},{9,... | collective-permute-start | bytes 417800 | tf_op jit(solution)/shard_map/ppermute | solution.py:59
  154.9 5.5 %collective-permute-start.13 = (f32[16,2176]{1,0:T(8,128)S(1)}, f32[16,2176]{1,0:T(8,128)S(1)}, u32[]{:S(2)}, u32[]{:S(2)}) collective-permute-start(f32[16,2176]{1,0:T(8,128)S(1)} %add.148), channel_id=1, source_target_pairs={{0,128},{1,129},{2,130},{3,131},{4,132},{5,133},{6,134},{7,135},{8... | collective-permute-start | bytes 417800 | tf_op jit(solution)/shard_map/ppermute | solution.py:59
  160.4 8.9 %collective-permute-start.14 = (f32[16,2176]{1,0:T(8,128)S(1)}, f32[16,2176]{1,0:T(8,128)S(1)}, u32[]{:S(2)}, u32[]{:S(2)}) collective-permute-start(f32[16,2176]{1,0:T(8,128)S(1)} %add.149), channel_id=1, source_target_pairs={{0,32},{1,33},{2,34},{3,35},{4,36},{5,37},{6,38},{7,39},{8,40},{9,... | collective-permute-start | bytes 417800 | tf_op jit(solution)/shard_map/ppermute | solution.py:59
  169.4 42.0 %copy-start.13 = (bf16[512,512]{1,0:T(8,128)(2,1)S(1)}, bf16[512,512]{1,0:T(8,128)(2,1)}, u32[]{:S(2)}) copy-start(bf16[512,512]{1,0:T(8,128)(2,1)} %param.18) | copy-start | bytes 1572868
  169.4 8.9 %collective-permute-start.15 = (f32[16,2176]{1,0:T(8,128)S(1)}, f32[16,2176]{1,0:T(8,128)S(1)}, u32[]{:S(2)}, u32[]{:S(2)}) collective-permute-start(f32[16,2176]{1,0:T(8,128)S(1)} %add.150), channel_id=1, source_target_pairs={{0,2},{1,3},{2,0},{3,1},{4,6},{5,7},{6,4},{7,5},{8,10},{9,11},{10,... | collective-permute-start | bytes 417800 | tf_op jit(solution)/shard_map/ppermute | solution.py:59
  178.3 8.9 %collective-permute-start.16 = (f32[16,2176]{1,0:T(8,128)S(1)}, f32[16,2176]{1,0:T(8,128)S(1)}, u32[]{:S(2)}, u32[]{:S(2)}) collective-permute-start(f32[16,2176]{1,0:T(8,128)S(1)} %add.151), channel_id=1, source_target_pairs={{0,1},{1,0},{2,3},{3,2},{4,5},{5,4},{6,7},{7,6},{8,9},{9,8},{10,11... | collective-permute-start | bytes 417800 | tf_op jit(solution)/shard_map/ppermute | solution.py:63
  187.3 5.8 %collective-permute-start.17 = (f32[32,2176]{1,0:T(8,128)S(1)}, f32[32,2176]{1,0:T(8,128)S(1)}, u32[]{:S(2)}, u32[]{:S(2)}) collective-permute-start(f32[32,2176]{1,0:T(8,128)S(1)} %maximum_select_fusion.3), channel_id=1, source_target_pairs={{0,64},{1,65},{2,66},{3,67},{4,68},{5,69},{6,70},{7,71},{8,72},{9,... | collective-permute-start | bytes 835592 | tf_op jit(solution)/shard_map/ppermute | solution.py:63
  193.1 8.5 %collective-permute-start.18 = (f32[64,2176]{1,0:T(8,128)S(1)}, f32[64,2176]{1,0:T(8,128)S(1)}, u32[]{:S(2)}, u32[]{:S(2)}) collective-permute-start(f32[64,2176]{1,0:T(8,128)S(1)} %maximum_select_fusion.2), channel_id=1, source_target_pairs={{0,8},{1,9},{2,10},{3,11},{4,12},{5,13},{6,14},{7,15},{8,0},{9,1},... | collective-permute-start | bytes 1671176 | tf_op jit(solution)/shard_map/ppermute | solution.py:63
  201.6 12.1 %collective-permute-start.19 = (f32[128,2176]{1,0:T(8,128)S(1)}, f32[128,2176]{1,0:T(8,128)S(1)}, u32[]{:S(2)}, u32[]{:S(2)}) collective-permute-start(f32[128,2176]{1,0:T(8,128)S(1)} %maximum_select_fusion.1), channel_id=1, source_target_pairs={{0,4},{1,5},{2,6},{3,7},{4,0},{5,1},{6,2},{7,3},{8,12},{9,13},{10,... | collective-permute-start | bytes 3342344 | tf_op jit(solution)/shard_map/ppermute | solution.py:63
  216.2 2.6 %copy-start.12 = (f32[128,2048]{1,0:T(8,128)S(1)}, f32[128,2048]{1,0:T(8,128)}, u32[]{:S(2)}) copy-start(f32[128,2048]{1,0:T(8,128)} %get-tuple-element.40) | copy-start | bytes 3145732
  216.2 3.9 %copy-start.9 = (f32[512,512]{1,0:T(8,128)S(1)}, f32[512,512]{1,0:T(8,128)}, u32[]{:S(2)}) copy-start(f32[512,512]{1,0:T(8,128)} %fusion.62) | copy-start | bytes 3145732
  218.8 3.4 %copy-start.1 = (bf16[512,512]{1,0:T(8,128)(2,1)S(1)}, bf16[512,512]{1,0:T(8,128)(2,1)}, u32[]{:S(2)}) copy-start(bf16[512,512]{1,0:T(8,128)(2,1)} %param.19) | copy-start | bytes 1572868
  (9 other events, 15.8 us)
Sparse Core Ops, SparseCore 0:
  136.0 53.8 reduce-scatter.1

commit v9 on v8

--- a/solution.py
+++ b/solution.py
@@ -83,8 +83,11 @@
             lax.ppermute(block, "rep", [(i, (i + shift) % count) for i in range(count)])
             for shift in range(1, count)
         ]
-    source = (place - jnp.arange(count)) % count
-    return jnp.stack(parts)[source].reshape(count * block.shape[0], *block.shape[1:])
+    rows = block.shape[0]
+    whole = jnp.zeros((count * rows, *block.shape[1:]), block.dtype)
+    for shift, part in enumerate(parts):
+        whole = lax.dynamic_update_slice_in_dim(whole, part, ((place - shift) % count) * rows, axis=0)
+    return whole
 
 
 def pass_rim(values, offset):

time: 230 us -> 229 us (level)
  blocking collectives: 31 us -> 0 us
  waiting for transfers between devices: 81 us -> 97.8 us
  starting transfers between devices: 42.4 us -> 55.4 us
  other arithmetic: 16.4 us -> 13.9 us
    all_to_all x1 -> x0, blocking collectives: 31 us -> none  [shards(): got = lax.all_to_all(sent, 'dom', split_axis=0, concat_axis=0, tiled=True)]
    all_to_all x0 -> x1, waiting for transfers between devices: none -> 18 us  [shards(): got = lax.all_to_all(sent, 'dom', split_axis=0, concat_axis=0, tiled=True)]
    all_to_all x0 -> x1, starting transfers between devices: none -> 13.2 us  [shards(): got = lax.all_to_all(sent, 'dom', split_axis=0, concat_axis=0, tiled=True)]
    another operation x3 -> x1, other arithmetic: 3.45 us -> 0.76 us  [the longest x2 2.7 us: gather_rep(): jnp.stack(parts)[source].reshape(count * block.shape[0], *block.shape[1:])]
  transfers between devices with their start and end apart: 21 -> 22, of which waited for: 17 -> 18; matrix products, arithmetic and copies ran while one was open for 12% -> 13% of each run, Pallas kernels for 0% -> 0%
where the time goes in v9:
time: 229 us; the launch traced here: 228 us
  waiting for transfers between devices  97.8 us (43%)
  starting transfers between devices  55.4 us (24%)
  matrix products  24.2 us (11%)
  local copies, waits for them, and re-layouts  22.5 us (10%)
  between operations  14.6 us (6%)
  other arithmetic  13.9 us (6%)
    ppermute x4, waiting for transfers between devices, halving_sum(): lax.ppermute(block, axes, [(i, i ^ 1 << bit) for i in range(count)])  22.8 us
    ppermute x4, waiting for transfers between devices, halving_sum(): got = lax.ppermute(block, axes, pairs)  21.5 us
    all_to_all x1, waiting for transfers between devices, shards(): got = lax.all_to_all(sent, 'dom', split_axis=0, concat_axis=0, tiled=True)  18 us
    all_to_all x1, starting transfers between devices, shards(): got = lax.all_to_all(sent, 'dom', split_axis=0, concat_axis=0, tiled=True)  13.2 us
    ppermute x4, starting transfers between devices, halving_sum(): got = lax.ppermute(block, axes, pairs)  12.2 us
    ppermute x2, waiting for transfers between devices, shifted(): lax.ppermute(value, axis, [(source, source + steps) for source in range(f...  9 us
    ppermute x1, waiting for transfers between devices, gather_rep(): from_next = lax.ppermute(block, 'rep', behind)  8.85 us
    ppermute x4, waiting for transfers between devices, halving_sum(): block = kept + lax.ppermute(sent, axes, pairs)  8.77 us
  transfers between devices with their start and end apart: 22, of which 18 were waited for; matrix products, arithmetic and copies ran while one was open for 13% of the time, Pallas kernels for 0%

profile of v9, /device:TPU:1, one launch (start us, length us, event | category | flops | bytes accessed | tf_op | source)
XLA Modules:
  0.0 228.3 jit_solution(10802573480072448630)
XLA Ops:
  13.3 13.2 %all-to-all-start = ((bf16[64,2,2112]{2,1,0:T(2,128)(2,1)}), bf16[64,2,2112]{2,1,0:T(2,128)(2,1)S(1)}, u32[]{:S(2)}, u32[]{:S(2)}) async-start(bf16[64,2,2112]{2,1,0:T(2,128)(2,1)} %reshape.130), calls=%async_computation | async-start | bytes 1114112 | tf_op jit(solution)/shard_map/all_to_all | solution.py:123
  26.6 18.0 %all-to-all-done = bf16[64,2,2112]{2,1,0:T(2,128)(2,1)S(1)} async-done(((bf16[64,2,2112]{2,1,0:T(2,128)(2,1)}), bf16[64,2,2112]{2,1,0:T(2,128)(2,1)S(1)}, u32[]{:S(2)}, u32[]{:S(2)}) %all-to-all-start) | async-done | bytes 540704 | tf_op jit(solution)/shard_map/all_to_all | solution.py:123
  48.2 2.5 %collective-permute-start.2 = (bf16[512,512]{1,0:T(8,128)(2,1)S(1)}, bf16[512,512]{1,0:T(8,128)(2,1)}, u32[]{:S(2)}, u32[]{:S(2)}) collective-permute-start(bf16[512,512]{1,0:T(8,128)(2,1)S(1)} %get-tuple-element.50), channel_id=1, source_target_pairs={{0,3},{1,0},{2,1},{3,2},{4,7},{5,4},{6,5},{7,6},{8,11},{9,8},{10,9... | collective-permute-start | bytes 1572872 | tf_op jit(solution)/shard_map/ppermute | solution.py:75
  52.8 8.8 %collective-permute-done.2 = bf16[512,512]{1,0:T(8,128)(2,1)} collective-permute-done((bf16[512,512]{1,0:T(8,128)(2,1)S(1)}, bf16[512,512]{1,0:T(8,128)(2,1)}, u32[]{:S(2)}, u32[]{:S(2)}) %collective-permute-start.2) | collective-permute-done | bytes 524320 | tf_op jit(solution)/shard_map/ppermute | solution.py:75
  62.6 3.6 %collective-permute-start.3 = (bf16[256,512]{1,0:T(8,128)(2,1)S(1)}, bf16[256,512]{1,0:T(8,128)(2,1)S(1)}, u32[]{:S(2)}, u32[]{:S(2)}) collective-permute-start(bf16[256,512]{1,0:T(8,128)(2,1)S(1)} %slice.174), channel_id=1, source_target_pairs={{0,3},{1,0},{2,1},{3,2},{4,7},{5,4},{6,5},{7,6},{8,11},{9,8},{10,9... | collective-permute-start | bytes 786440 | tf_op jit(solution)/shard_map/ppermute | solution.py:78
  68.4 2.2 collective-permute-done.3
  70.5 4.2 %collective-permute-done.1 = bf16[256,512]{1,0:T(8,128)(2,1)S(1)} collective-permute-done((bf16[256,512]{1,0:T(8,128)(2,1)S(1)}, bf16[256,512]{1,0:T(8,128)(2,1)S(1)}, u32[]{:S(2)}, u32[]{:S(2)}) %collective-permute-start.1) | collective-permute-done | bytes 262176 | tf_op jit(solution)/shard_map/ppermute | solution.py:78
  76.9 4.2 %collective-permute-start.4 = (bf16[512,512]{1,0:T(8,128)(2,1)}, bf16[512,512]{1,0:T(8,128)(2,1)}, u32[]{:S(2)}, u32[]{:S(2)}) collective-permute-start(bf16[512,512]{1,0:T(8,128)(2,1)} %get-tuple-element.41), channel_id=1, source_target_pairs={{0,4},{4,8},{8,12},{12,16},{16,20},{20,24},{24,28},{28,32},{32,36}... | collective-permute-start | bytes 1572872 | tf_op jit(solution)/shard_map/ppermute | solution.py:20
  81.1 2.4 %collective-permute-start.5 = (bf16[512,512]{1,0:T(8,128)(2,1)}, bf16[512,512]{1,0:T(8,128)(2,1)}, u32[]{:S(2)}, u32[]{:S(2)}) collective-permute-start(bf16[512,512]{1,0:T(8,128)(2,1)} %get-tuple-element.42), channel_id=1, source_target_pairs={{4,0},{8,4},{12,8},{16,12},{20,16},{24,20},{28,24},{32,28},{36,32}... | collective-permute-start | bytes 1572872 | tf_op jit(solution)/shard_map/ppermute | solution.py:23
  83.5 4.4 %subtract_convert_fusion = (bf16[4,24,128,128]{3,1,2,0:T(8,128)(2,1)}, bf16[4,24,128,128]{3,1,2,0:T(8,128)(2,1)}) fusion(bf16[4,12,128,128]{3,2,1,0:T(8,128)(2,1)S(1)} %get-tuple-element.34, s32[4,12]{1,0:T(4,128)S(1)} %broadcast_subtract_fusion), kind=kOutput, calls=%fused_computation.1 | convolution fusion | flops 44041344 | bytes 7864512 | tf_op jit(solution)/shard_map/tke,tkab->teab/dot_general | solution.py:137
  89.4 2.5 %collective-permute-done.5 = bf16[512,512]{1,0:T(8,128)(2,1)} collective-permute-done((bf16[512,512]{1,0:T(8,128)(2,1)}, bf16[512,512]{1,0:T(8,128)(2,1)}, u32[]{:S(2)}, u32[]{:S(2)}) %collective-permute-start.5) | collective-permute-done | bytes 524320 | tf_op jit(solution)/shard_map/ppermute | solution.py:23
  103.6 2.1 reshape.118
  113.3 2.4 %slice.177 = f32[16,128,512]{2,1,0:T(8,128)} slice(f32[24,128,512]{2,1,0:T(8,128)S(1)} %get-tuple-element.52), slice={[4:20], [0:128], [0:512]} | slice | bytes 8388608 | tf_op jit(solution)/shard_map/slice | solution.py:175
  117.8 2.7 %collective-permute-start.7 = (bf16[512,512]{1,0:T(8,128)(2,1)S(1)}, bf16[512,512]{1,0:T(8,128)(2,1)S(1)}, u32[]{:S(2)}, u32[]{:S(2)}) collective-permute-start(bf16[512,512]{1,0:T(8,128)(2,1)S(1)} %bitcast.68), channel_id=1, source_target_pairs={{4,0},{8,4},{12,8},{16,12},{20,16},{24,20},{28,24},{32,28},{36,32}... | collective-permute-start | bytes 1572872 | tf_op jit(solution)/shard_map/ppermute | solution.py:12
  120.7 2.0 collective-permute-start.9
  125.8 7.1 %collective-permute-done.7 = bf16[512,512]{1,0:T(8,128)(2,1)S(1)} collective-permute-done((bf16[512,512]{1,0:T(8,128)(2,1)S(1)}, bf16[512,512]{1,0:T(8,128)(2,1)S(1)}, u32[]{:S(2)}, u32[]{:S(2)}) %collective-permute-start.7) | collective-permute-done | bytes 524320 | tf_op jit(solution)/shard_map/ppermute | solution.py:12
  132.9 2.4 %fusion.33 = f32[2048,512]{1,0:T(8,128)} fusion(f32[2048,512]{1,0:T(8,128)} %constant_dynamic-update-slice_fusion, bf16[512,512]{1,0:T(8,128)(2,1)S(1)} %collective-permute-done.7), kind=kLoop, calls=%fused_computation.40 | loop fusion | flops 524288 | bytes 2621440 | tf_op jit(solution)/shard_map/scatter-add | solution.py:177
  136.0 3.0 %collective-permute-start.10 = (f32[32,2176]{1,0:T(8,128)S(1)}, f32[32,2176]{1,0:T(8,128)S(1)}, u32[]{:S(2)}, u32[]{:S(2)}) collective-permute-start(f32[32,2176]{1,0:T(8,128)S(1)} %slice_select_fusion.2), channel_id=1, source_target_pairs={{0,64},{1,65},{2,66},{3,67},{4,68},{5,69},{6,70},{7,71},{8,72},{9,... | collective-permute-start | bytes 835592 | tf_op jit(solution)/shard_map/ppermute | solution.py:56
  139.0 3.9 %collective-permute-done.10 = f32[32,2176]{1,0:T(8,128)S(1)} collective-permute-done((f32[32,2176]{1,0:T(8,128)S(1)}, f32[32,2176]{1,0:T(8,128)S(1)}, u32[]{:S(2)}, u32[]{:S(2)}) %collective-permute-start.10) | collective-permute-done | bytes 278560 | tf_op jit(solution)/shard_map/ppermute | solution.py:56
  143.1 4.2 %collective-permute-done.11 = f32[16,2176]{1,0:T(8,128)S(1)} collective-permute-done((f32[16,2176]{1,0:T(8,128)S(1)}, f32[16,2176]{1,0:T(8,128)S(1)}, u32[]{:S(2)}, u32[]{:S(2)}) %collective-permute-start.11) | collective-permute-done | bytes 139296 | tf_op jit(solution)/shard_map/ppermute | solution.py:56
  149.4 4.8 %collective-permute-done.12 = f32[16,2176]{1,0:T(8,128)S(1)} collective-permute-done((f32[16,2176]{1,0:T(8,128)S(1)}, f32[16,2176]{1,0:T(8,128)S(1)}, u32[]{:S(2)}, u32[]{:S(2)}) %collective-permute-start.12) | collective-permute-done | bytes 139296 | tf_op jit(solution)/shard_map/ppermute | solution.py:59
  154.2 2.1 collective-permute-start.13
  156.3 3.4 %collective-permute-done.13 = f32[16,2176]{1,0:T(8,128)S(1)} collective-permute-done((f32[16,2176]{1,0:T(8,128)S(1)}, f32[16,2176]{1,0:T(8,128)S(1)}, u32[]{:S(2)}, u32[]{:S(2)}) %collective-permute-start.13) | collective-permute-done | bytes 139296 | tf_op jit(solution)/shard_map/ppermute | solution.py:59
  159.7 3.1 %collective-permute-start.14 = (f32[16,2176]{1,0:T(8,128)S(1)}, f32[16,2176]{1,0:T(8,128)S(1)}, u32[]{:S(2)}, u32[]{:S(2)}) collective-permute-start(f32[16,2176]{1,0:T(8,128)S(1)} %add.160), channel_id=1, source_target_pairs={{0,32},{1,33},{2,34},{3,35},{4,36},{5,37},{6,38},{7,39},{8,40},{9,... | collective-permute-start | bytes 417800 | tf_op jit(solution)/shard_map/ppermute | solution.py:59
  162.8 5.8 %collective-permute-done.14 = f32[16,2176]{1,0:T(8,128)S(1)} collective-permute-done((f32[16,2176]{1,0:T(8,128)S(1)}, f32[16,2176]{1,0:T(8,128)S(1)}, u32[]{:S(2)}, u32[]{:S(2)}) %collective-permute-start.14) | collective-permute-done | bytes 139296 | tf_op jit(solution)/shard_map/ppermute | solution.py:59
  168.7 8.8 %collective-permute-done.15 = f32[16,2176]{1,0:T(8,128)S(1)} collective-permute-done((f32[16,2176]{1,0:T(8,128)S(1)}, f32[16,2176]{1,0:T(8,128)S(1)}, u32[]{:S(2)}, u32[]{:S(2)}) %collective-permute-start.15) | collective-permute-done | bytes 139296 | tf_op jit(solution)/shard_map/ppermute | solution.py:59
  177.7 8.8 %collective-permute-done.16 = f32[16,2176]{1,0:T(8,128)S(1)} collective-permute-done((f32[16,2176]{1,0:T(8,128)S(1)}, f32[16,2176]{1,0:T(8,128)S(1)}, u32[]{:S(2)}, u32[]{:S(2)}) %collective-permute-start.16) | collective-permute-done | bytes 139296 | tf_op jit(solution)/shard_map/ppermute | solution.py:63
  187.9 4.4 %collective-permute-done.17 = f32[32,2176]{1,0:T(8,128)S(1)} collective-permute-done((f32[32,2176]{1,0:T(8,128)S(1)}, f32[32,2176]{1,0:T(8,128)S(1)}, u32[]{:S(2)}, u32[]{:S(2)}) %collective-permute-start.17) | collective-permute-done | bytes 278560 | tf_op jit(solution)/shard_map/ppermute | solution.py:63
  193.4 7.4 %collective-permute-done.18 = f32[64,2176]{1,0:T(8,128)S(1)} collective-permute-done((f32[64,2176]{1,0:T(8,128)S(1)}, f32[64,2176]{1,0:T(8,128)S(1)}, u32[]{:S(2)}, u32[]{:S(2)}) %collective-permute-start.18) | collective-permute-done | bytes 557088 | tf_op jit(solution)/shard_map/ppermute | solution.py:63
  200.9 9.6 %collective-permute-start.19 = (f32[128,2176]{1,0:T(8,128)S(1)}, f32[128,2176]{1,0:T(8,128)S(1)}, u32[]{:S(2)}, u32[]{:S(2)}) collective-permute-start(f32[128,2176]{1,0:T(8,128)S(1)} %maximum_select_fusion.1), channel_id=1, source_target_pairs={{0,4},{1,5},{2,6},{3,7},{4,0},{5,1},{6,2},{7,3},{8,12},{9,13},{10,... | collective-permute-start | bytes 3342344 | tf_op jit(solution)/shard_map/ppermute | solution.py:63
  215.4 2.6 %slice.165 = f32[512,512]{1,0:T(8,128)} reshape(f32[128,2048]{1,0:T(8,128)} %get-tuple-element.39) | data formatting | bytes 2097152 | tf_op jit(solution)/shard_map/slice | solution.py:165
  219.3 2.2 add_convert_fusion
  (129 shorter events, 54.9 us)
Async XLA Ops:
  7.2 89.7 %copy-start = (bf16[512,512]{1,0:T(8,128)(2,1)S(1)}, bf16[512,512]{1,0:T(8,128)(2,1)}, u32[]{:S(2)}) copy-start(bf16[512,512]{1,0:T(8,128)(2,1)} %param.19) | copy-start | bytes 1572868
  13.3 31.2 %all-to-all-start = ((bf16[64,2,2112]{2,1,0:T(2,128)(2,1)}), bf16[64,2,2112]{2,1,0:T(2,128)(2,1)S(1)}, u32[]{:S(2)}, u32[]{:S(2)}) async-start(bf16[64,2,2112]{2,1,0:T(2,128)(2,1)} %reshape.130), calls=%async_computation | async-start | bytes 1114112 | tf_op jit(solution)/shard_map/all_to_all | solution.py:123
  26.5 192.8 %reduce-scatter.2.cloned.1.call-start = ((), (), s32[]{:S(2)}) async-start(), calls=%async_computation.2 | async-start | bytes 5242880 | tf_op jit(solution)/shard_map/reduce_scatter | solution.py:178
  46.3 4.4 %copy-start.15 = (s32[4,12]{1,0:T(4,128)S(1)}, s32[4,12]{1,0:T(4,128)}, u32[]{:S(2)}) copy-start(s32[4,12]{1,0:T(4,128)} %param.17) | copy-start | bytes 580
  48.1 20.2 %copy-start.12 = (bf16[512,512]{1,0:T(8,128)(2,1)}, bf16[512,512]{1,0:T(8,128)(2,1)S(1)}, u32[]{:S(2)}) copy-start(bf16[512,512]{1,0:T(8,128)(2,1)S(1)} %get-tuple-element.50) | copy-start | bytes 1572868
  48.1 19.1 %copy-start.16 = (s32[4,12]{1,0:T(4,128)S(1)}, s32[4,12]{1,0:T(4,128)}, u32[]{:S(2)}) copy-start(s32[4,12]{1,0:T(4,128)} %param.16) | copy-start | bytes 580
  48.2 13.5 %collective-permute-start.2 = (bf16[512,512]{1,0:T(8,128)(2,1)S(1)}, bf16[512,512]{1,0:T(8,128)(2,1)}, u32[]{:S(2)}, u32[]{:S(2)}) collective-permute-start(bf16[512,512]{1,0:T(8,128)(2,1)S(1)} %get-tuple-element.50), channel_id=1, source_target_pairs={{0,3},{1,0},{2,1},{3,2},{4,7},{5,4},{6,5},{7,6},{8,11},{9,8},{10,9... | collective-permute-start | bytes 1572872 | tf_op jit(solution)/shard_map/ppermute | solution.py:75
  50.7 15.5 %collective-permute-start = (bf16[512,512]{1,0:T(8,128)(2,1)S(1)}, bf16[512,512]{1,0:T(8,128)(2,1)}, u32[]{:S(2)}, u32[]{:S(2)}) collective-permute-start(bf16[512,512]{1,0:T(8,128)(2,1)S(1)} %get-tuple-element.50), channel_id=1, source_target_pairs={{0,1},{1,2},{2,3},{3,0},{4,5},{5,6},{6,7},{7,4},{8,9},{9,10},{10,1... | collective-permute-start | bytes 1572872 | tf_op jit(solution)/shard_map/ppermute | solution.py:74
  62.6 8.0 %collective-permute-start.3 = (bf16[256,512]{1,0:T(8,128)(2,1)S(1)}, bf16[256,512]{1,0:T(8,128)(2,1)S(1)}, u32[]{:S(2)}, u32[]{:S(2)}) collective-permute-start(bf16[256,512]{1,0:T(8,128)(2,1)S(1)} %slice.174), channel_id=1, source_target_pairs={{0,3},{1,0},{2,1},{3,2},{4,7},{5,4},{6,5},{7,6},{8,11},{9,8},{10,9... | collective-permute-start | bytes 786440 | tf_op jit(solution)/shard_map/ppermute | solution.py:78
  67.1 7.6 %collective-permute-start.1 = (bf16[256,512]{1,0:T(8,128)(2,1)S(1)}, bf16[256,512]{1,0:T(8,128)(2,1)S(1)}, u32[]{:S(2)}, u32[]{:S(2)}) collective-permute-start(bf16[256,512]{1,0:T(8,128)(2,1)S(1)} %slice.173), channel_id=1, source_target_pairs={{0,1},{1,2},{2,3},{3,0},{4,5},{5,6},{6,7},{7,4},{8,9},{9,10},{10,1... | collective-permute-start | bytes 786440 | tf_op jit(solution)/shard_map/ppermute | solution.py:78
  76.9 12.5 %collective-permute-start.4 = (bf16[512,512]{1,0:T(8,128)(2,1)}, bf16[512,512]{1,0:T(8,128)(2,1)}, u32[]{:S(2)}, u32[]{:S(2)}) collective-permute-start(bf16[512,512]{1,0:T(8,128)(2,1)} %get-tuple-element.41), channel_id=1, source_target_pairs={{0,4},{4,8},{8,12},{12,16},{16,20},{20,24},{24,28},{28,32},{32,36}... | collective-permute-start | bytes 1572872 | tf_op jit(solution)/shard_map/ppermute | solution.py:20
  81.1 10.8 %collective-permute-start.5 = (bf16[512,512]{1,0:T(8,128)(2,1)}, bf16[512,512]{1,0:T(8,128)(2,1)}, u32[]{:S(2)}, u32[]{:S(2)}) collective-permute-start(bf16[512,512]{1,0:T(8,128)(2,1)} %get-tuple-element.42), channel_id=1, source_target_pairs={{4,0},{8,4},{12,8},{16,12},{20,16},{24,20},{28,24},{32,28},{36,32}... | collective-permute-start | bytes 1572872 | tf_op jit(solution)/shard_map/ppermute | solution.py:23
  83.5 4.4 %copy-start.10 = (bf16[512,512]{1,0:T(8,128)(2,1)S(1)}, bf16[512,512]{1,0:T(8,128)(2,1)}, u32[]{:S(2)}) copy-start(bf16[512,512]{1,0:T(8,128)(2,1)} %param.18) | copy-start | bytes 1572868
  89.4 3.8 %copy-start.2 = (bf16[4,24,128,128]{3,1,2,0:T(8,128)(2,1)S(1)}, bf16[4,24,128,128]{3,1,2,0:T(8,128)(2,1)}, u32[]{:S(2)}) copy-start(bf16[4,24,128,128]{3,1,2,0:T(8,128)(2,1)} %get-tuple-element.35) | copy-start | bytes 9437188
  107.6 12.8 %collective-permute-start.8 = (f32[128,2176]{1,0:T(8,128)S(1)}, f32[128,2176]{1,0:T(8,128)S(1)}, u32[]{:S(2)}, u32[]{:S(2)}) collective-permute-start(f32[128,2176]{1,0:T(8,128)S(1)} %slice_select_fusion), channel_id=1, source_target_pairs={{0,4},{1,5},{2,6},{3,7},{4,0},{5,1},{6,2},{7,3},{8,12},{9,13},{10,... | collective-permute-start | bytes 3342344 | tf_op jit(solution)/shard_map/ppermute | solution.py:56
  115.8 8.8 %collective-permute-start.6 = (bf16[512,512]{1,0:T(8,128)(2,1)S(1)}, bf16[512,512]{1,0:T(8,128)(2,1)S(1)}, u32[]{:S(2)}, u32[]{:S(2)}) collective-permute-start(bf16[512,512]{1,0:T(8,128)(2,1)S(1)} %bitcast.69), channel_id=1, source_target_pairs={{0,4},{4,8},{8,12},{12,16},{16,20},{20,24},{24,28},{28,32},{32,36}... | collective-permute-start | bytes 1572872 | tf_op jit(solution)/shard_map/ppermute | solution.py:12
  117.8 15.1 %collective-permute-start.7 = (bf16[512,512]{1,0:T(8,128)(2,1)S(1)}, bf16[512,512]{1,0:T(8,128)(2,1)S(1)}, u32[]{:S(2)}, u32[]{:S(2)}) collective-permute-start(bf16[512,512]{1,0:T(8,128)(2,1)S(1)} %bitcast.68), channel_id=1, source_target_pairs={{4,0},{8,4},{12,8},{16,12},{20,16},{24,20},{28,24},{32,28},{36,32}... | collective-permute-start | bytes 1572872 | tf_op jit(solution)/shard_map/ppermute | solution.py:12
  120.7 15.2 %collective-permute-start.9 = (f32[64,2176]{1,0:T(8,128)S(1)}, f32[64,2176]{1,0:T(8,128)S(1)}, u32[]{:S(2)}, u32[]{:S(2)}) collective-permute-start(f32[64,2176]{1,0:T(8,128)S(1)} %slice_select_fusion.1), channel_id=1, source_target_pairs={{0,8},{1,9},{2,10},{3,11},{4,12},{5,13},{6,14},{7,15},{8,0},{9,1},... | collective-permute-start | bytes 1671176 | tf_op jit(solution)/shard_map/ppermute | solution.py:56
  136.0 7.0 %collective-permute-start.10 = (f32[32,2176]{1,0:T(8,128)S(1)}, f32[32,2176]{1,0:T(8,128)S(1)}, u32[]{:S(2)}, u32[]{:S(2)}) collective-permute-start(f32[32,2176]{1,0:T(8,128)S(1)} %slice_select_fusion.2), channel_id=1, source_target_pairs={{0,64},{1,65},{2,66},{3,67},{4,68},{5,69},{6,70},{7,71},{8,72},{9,... | collective-permute-start | bytes 835592 | tf_op jit(solution)/shard_map/ppermute | solution.py:56
  143.0 4.3 %collective-permute-start.11 = (f32[16,2176]{1,0:T(8,128)S(1)}, f32[16,2176]{1,0:T(8,128)S(1)}, u32[]{:S(2)}, u32[]{:S(2)}) collective-permute-start(f32[16,2176]{1,0:T(8,128)S(1)} %slice_select_fusion.3), channel_id=1, source_target_pairs={{0,1},{1,0},{2,3},{3,2},{4,5},{5,4},{6,7},{7,6},{8,9},{9,8},{10,11... | collective-permute-start | bytes 417800 | tf_op jit(solution)/shard_map/ppermute | solution.py:56
  147.4 6.8 %collective-permute-start.12 = (f32[16,2176]{1,0:T(8,128)S(1)}, f32[16,2176]{1,0:T(8,128)S(1)}, u32[]{:S(2)}, u32[]{:S(2)}) collective-permute-start(f32[16,2176]{1,0:T(8,128)S(1)} %select_add_fusion.3), channel_id=1, source_target_pairs={{0,16},{1,17},{2,18},{3,19},{4,20},{5,21},{6,22},{7,23},{8,24},{9,... | collective-permute-start | bytes 417800 | tf_op jit(solution)/shard_map/ppermute | solution.py:59
  154.2 5.5 %collective-permute-start.13 = (f32[16,2176]{1,0:T(8,128)S(1)}, f32[16,2176]{1,0:T(8,128)S(1)}, u32[]{:S(2)}, u32[]{:S(2)}) collective-permute-start(f32[16,2176]{1,0:T(8,128)S(1)} %add.159), channel_id=1, source_target_pairs={{0,128},{1,129},{2,130},{3,131},{4,132},{5,133},{6,134},{7,135},{8... | collective-permute-start | bytes 417800 | tf_op jit(solution)/shard_map/ppermute | solution.py:59
  159.7 8.9 %collective-permute-start.14 = (f32[16,2176]{1,0:T(8,128)S(1)}, f32[16,2176]{1,0:T(8,128)S(1)}, u32[]{:S(2)}, u32[]{:S(2)}) collective-permute-start(f32[16,2176]{1,0:T(8,128)S(1)} %add.160), channel_id=1, source_target_pairs={{0,32},{1,33},{2,34},{3,35},{4,36},{5,37},{6,38},{7,39},{8,40},{9,... | collective-permute-start | bytes 417800 | tf_op jit(solution)/shard_map/ppermute | solution.py:59
  168.6 41.9 %copy-start.11 = (bf16[512,512]{1,0:T(8,128)(2,1)S(1)}, bf16[512,512]{1,0:T(8,128)(2,1)}, u32[]{:S(2)}) copy-start(bf16[512,512]{1,0:T(8,128)(2,1)} %param.18) | copy-start | bytes 1572868
  168.6 8.9 %collective-permute-start.15 = (f32[16,2176]{1,0:T(8,128)S(1)}, f32[16,2176]{1,0:T(8,128)S(1)}, u32[]{:S(2)}, u32[]{:S(2)}) collective-permute-start(f32[16,2176]{1,0:T(8,128)S(1)} %add.161), channel_id=1, source_target_pairs={{0,2},{1,3},{2,0},{3,1},{4,6},{5,7},{6,4},{7,5},{8,10},{9,11},{10,... | collective-permute-start | bytes 417800 | tf_op jit(solution)/shard_map/ppermute | solution.py:59
  177.6 8.9 %collective-permute-start.16 = (f32[16,2176]{1,0:T(8,128)S(1)}, f32[16,2176]{1,0:T(8,128)S(1)}, u32[]{:S(2)}, u32[]{:S(2)}) collective-permute-start(f32[16,2176]{1,0:T(8,128)S(1)} %add.162), channel_id=1, source_target_pairs={{0,1},{1,0},{2,3},{3,2},{4,5},{5,4},{6,7},{7,6},{8,9},{9,8},{10,11... | collective-permute-start | bytes 417800 | tf_op jit(solution)/shard_map/ppermute | solution.py:63
  186.5 5.8 %collective-permute-start.17 = (f32[32,2176]{1,0:T(8,128)S(1)}, f32[32,2176]{1,0:T(8,128)S(1)}, u32[]{:S(2)}, u32[]{:S(2)}) collective-permute-start(f32[32,2176]{1,0:T(8,128)S(1)} %maximum_select_fusion.3), channel_id=1, source_target_pairs={{0,64},{1,65},{2,66},{3,67},{4,68},{5,69},{6,70},{7,71},{8,72},{9,... | collective-permute-start | bytes 835592 | tf_op jit(solution)/shard_map/ppermute | solution.py:63
  192.4 8.5 %collective-permute-start.18 = (f32[64,2176]{1,0:T(8,128)S(1)}, f32[64,2176]{1,0:T(8,128)S(1)}, u32[]{:S(2)}, u32[]{:S(2)}) collective-permute-start(f32[64,2176]{1,0:T(8,128)S(1)} %maximum_select_fusion.2), channel_id=1, source_target_pairs={{0,8},{1,9},{2,10},{3,11},{4,12},{5,13},{6,14},{7,15},{8,0},{9,1},... | collective-permute-start | bytes 1671176 | tf_op jit(solution)/shard_map/ppermute | solution.py:63
  200.9 12.0 %collective-permute-start.19 = (f32[128,2176]{1,0:T(8,128)S(1)}, f32[128,2176]{1,0:T(8,128)S(1)}, u32[]{:S(2)}, u32[]{:S(2)}) collective-permute-start(f32[128,2176]{1,0:T(8,128)S(1)} %maximum_select_fusion.1), channel_id=1, source_target_pairs={{0,4},{1,5},{2,6},{3,7},{4,0},{5,1},{6,2},{7,3},{8,12},{9,13},{10,... | collective-permute-start | bytes 3342344 | tf_op jit(solution)/shard_map/ppermute | solution.py:63
  215.4 2.6 %copy-start.9 = (f32[128,2048]{1,0:T(8,128)S(1)}, f32[128,2048]{1,0:T(8,128)}, u32[]{:S(2)}) copy-start(f32[128,2048]{1,0:T(8,128)} %get-tuple-element.40) | copy-start | bytes 3145732
  215.4 3.9 %copy-start.6 = (f32[512,512]{1,0:T(8,128)S(1)}, f32[512,512]{1,0:T(8,128)}, u32[]{:S(2)}) copy-start(f32[512,512]{1,0:T(8,128)} %fusion.61) | copy-start | bytes 3145732
  218.0 3.4 %copy-start.1 = (bf16[512,512]{1,0:T(8,128)(2,1)S(1)}, bf16[512,512]{1,0:T(8,128)(2,1)}, u32[]{:S(2)}) copy-start(bf16[512,512]{1,0:T(8,128)(2,1)} %param.19) | copy-start | bytes 1572868
  (9 other events, 15.8 us)
Sparse Core Ops, SparseCore 0:
  135.4 53.7 reduce-scatter.1
